TPU v7x, 512 devices: a whole 4x8x8 slice. The times are simulated.
512 devices in a mesh: group: 64 (over z, y), mp: 8 (over x, core).
Axes of the slice: x: 4, y: 8, z: 8, core: 2. Of those that a mesh axis runs over, the one named last changes fastest.
Arguments:
- tokens: bfloat16 [8192, 4096], P('group', 'mp'), may hold values from -3000 to 3000
- attn_gain: float32 [4096], replicated, may hold values from 0.1 to 1.9
- q_weight: bfloat16 [4096, 4096], P('group', 'mp'), may hold values from -0.09375 to 0.09375
- k_weight: bfloat16 [4096, 512], P('group'), may hold values from -0.09375 to 0.09375
- v_weight: bfloat16 [4096, 512], P('group'), may hold values from -0.09375 to 0.09375
- kv_pool: bfloat16 [4096, 8, 2, 16, 128], P('group', 'mp'), may hold values from -1000 to 1000
- page_table: int32 [256, 16], replicated, may hold values from 0 to 4095, as said below
- lengths: int32 [256], P('group'), may hold values from 2 to 256
- token_request: int32 [8192], P('group'), may hold values from 0 to 3
Outputs:
- attention: bfloat16 [8192, 4096], P('group', 'mp')
- decode_cache: bfloat16 [256, 8, 2, 256, 128], P('group', 'mp')
Inputs may be any that keep to these rules, and one draw needn't show every extreme that they name: Every pool page stands in exactly one slot of page_table. The pages that one group index holds for the requests of one owner (requests o * 4 to (o + 1) * 4 - 1) number at most 2, and exactly 2 for some pairs of holder and owner.
All inputs are finite; a program needn't handle non-finite values.
Results may differ from a plain program's by a relative error of at most 0.038.
Values may be sent and summed in bfloat16 or wider, within the bound.
No kernel may reach another device: no remote copies, remote signals or barrier semaphores. Data moves between devices by JAX's collectives and lax.ppermute only.
A program may use at most 64 MiB of HBM per device.

v0:
```python
import jax
import jax.numpy as jnp
from jax import lax
from jax.sharding import PartitionSpec as P

HEADS = 32
KVH = 4


rope_theta = 5000000.0
norm_eps = 1e-05


def from_partner(x, axis, bit):
    return lax.ppermute(x, axis, [(i, i ^ 1 << bit) for i in range(lax.axis_size(axis))])


def rotate(vectors, position):
    half_dim = vectors.shape[-1] // 2
    frequency = rope_theta ** (-(jnp.arange(half_dim, dtype=jnp.float32) / half_dim))
    angles = position.astype(jnp.float32)[:, None, None] * frequency[None, None, :]
    cosine = jnp.cos(angles)
    sine_part = jnp.sin(angles)
    first_half = vectors[..., :half_dim]
    second = vectors[..., half_dim:]
    return jnp.concatenate(
        [first_half * cosine - second * sine_part, second * cosine + first_half * sine_part],
        axis=-1,
    )


def normalize(group_rows, attn_gain):
    features = group_rows.astype(jnp.float32)
    root_mean = jnp.sqrt(jnp.mean(features * features, axis=-1, keepdims=True) + norm_eps)
    return (features / root_mean * attn_gain).astype(jnp.bfloat16)


def token_positions(token_request, group_lengths, request_count):
    member = (token_request[:, None] == jnp.arange(request_count, dtype=jnp.int32)[None, :]).astype(
        jnp.int32
    )
    earlier = jnp.sum((jnp.cumsum(member, axis=0) - member) * member, axis=1)
    return jnp.sum(member * group_lengths[None, :], axis=1) + earlier


def build_mask(token_request, group_lengths, max_len):
    request_count = group_lengths.shape[0]
    key_index = jnp.arange(request_count * max_len, dtype=jnp.int32)
    key_request = key_index // max_len
    key_alive = key_index % max_len < group_lengths[key_request]
    cached = (token_request[:, None] == key_request[None, :]) & key_alive[None, :]
    token_order = jnp.arange(token_request.shape[0], dtype=jnp.int32)
    fresh = (token_request[:, None] == token_request[None, :]) & (
        token_order[None, :] <= token_order[:, None]
    )
    return jnp.concatenate([cached, fresh], axis=1)


def weigh(scores, allowed):
    masked = jnp.where(allowed, scores, -1e30)
    row_top = jnp.max(masked, axis=-1, keepdims=True)
    exponent = jnp.exp(masked - row_top)
    return (exponent / jnp.sum(exponent, axis=-1, keepdims=True)).astype(jnp.bfloat16)


def on_device(
    tokens, attn_gain, q_weight, k_weight, v_weight, kv_pool, page_table, lengths, token_request
):
    groups = lax.axis_size("group")
    group_idx = lax.axis_index("group")
    mp_idx = lax.axis_index("mp")
    pool_pages = kv_pool.shape[0]
    pair_count = kv_pool.shape[1]
    page_len = kv_pool.shape[3]
    head_dim = kv_pool.shape[4]
    requests_here = lengths.shape[0]
    slot_count = pool_pages // requests_here
    max_len = slot_count * page_len
    capacity = 2 * pool_pages // groups
    flat_table = page_table.reshape(-1)
    slot_ids = jnp.arange(flat_table.shape[0], dtype=jnp.int32)
    owner_slot = jnp.zeros((flat_table.shape[0],), jnp.int32).at[flat_table].set(slot_ids)
    held_slots = lax.dynamic_slice_in_dim(owner_slot, group_idx * pool_pages, pool_pages)
    target_owner = held_slots // pool_pages
    slot_local = held_slots % pool_pages
    owner_hits = (target_owner[:, None] == jnp.arange(groups, dtype=jnp.int32)[None, :]).astype(
        jnp.int32
    )
    order_within = jnp.sum((jnp.cumsum(owner_hits, axis=0) - owner_hits) * owner_hits, axis=1)
    buffer_row = target_owner * capacity + order_within
    page_rows = kv_pool.reshape(pool_pages, -1)
    row_width = page_rows.shape[1]
    outgoing = (
        jnp.zeros((groups * capacity, row_width), jnp.bfloat16)
        .at[buffer_row]
        .set(page_rows)
        .reshape(groups, capacity, row_width)
    )
    outgoing_slots = (
        jnp.full((groups * capacity,), -1, jnp.int32)
        .at[buffer_row]
        .set(slot_local)
        .reshape(groups, capacity)
    )
    arrived, arrived_slots = (
        lax.all_to_all(outgoing, "group", split_axis=0, concat_axis=0, tiled=True),
        lax.all_to_all(outgoing_slots, "group", split_axis=0, concat_axis=0, tiled=True),
    )
    landing = jnp.where(arrived_slots < 0, pool_pages, arrived_slots).reshape(-1)
    placed = (
        jnp.zeros((pool_pages + 1, row_width), jnp.bfloat16)
        .at[landing]
        .set(arrived.reshape(-1, row_width))[:pool_pages]
    )
    decoded = placed.reshape(requests_here, slot_count, pair_count, 2, page_len, head_dim)
    decoded = decoded.transpose(0, 2, 3, 1, 4, 5).reshape(
        requests_here, pair_count, 2, max_len, head_dim
    )
    alive_mask = jnp.arange(max_len, dtype=jnp.int32)[None, :] < lengths[:, None]
    decoded = jnp.where(alive_mask[:, None, None, :, None], decoded, jnp.zeros((), jnp.bfloat16))
    whole_rows = lax.all_gather(tokens, "mp", axis=1, tiled=True)
    normed = normalize(whole_rows, attn_gain)
    rows_here = tokens.shape[0]
    heads_here = q_weight.shape[1] // head_dim
    per_kv = HEADS // KVH
    first_kv = mp_idx * heads_here // per_kv
    key_cols = lax.dynamic_slice_in_dim(k_weight, first_kv * head_dim, head_dim, 1)
    value_cols = lax.dynamic_slice_in_dim(v_weight, first_kv * head_dim, head_dim, 1)
    query_sum = jnp.dot(
        normed,
        lax.all_gather(q_weight, "group", axis=0, tiled=True),
        preferred_element_type=jnp.float32,
    )
    key_sum = jnp.dot(
        normed,
        lax.all_gather(key_cols, "group", axis=0, tiled=True),
        preferred_element_type=jnp.float32,
    )
    value_sum = jnp.dot(
        normed,
        lax.all_gather(value_cols, "group", axis=0, tiled=True),
        preferred_element_type=jnp.float32,
    )
    position = token_positions(token_request, lengths, requests_here)
    queries = (
        rotate(query_sum.reshape(rows_here, heads_here, head_dim), position)
        .astype(jnp.bfloat16)
        .transpose(1, 0, 2)
    )
    new_keys = rotate(key_sum.reshape(rows_here, 1, head_dim), position).astype(jnp.bfloat16)[:, 0]
    new_values = value_sum.astype(jnp.bfloat16)
    allowed = build_mask(token_request, lengths, max_len)
    score_scale = head_dim ** (-0.5)
    partner_cache = from_partner(decoded, "mp", 0)
    is_even = mp_idx % 2 == 0
    layer_zero = jnp.where(is_even, decoded, partner_cache)[:, 0]
    all_keys = jnp.concatenate(
        [layer_zero[:, 0].reshape(requests_here * max_len, head_dim), new_keys], axis=0
    )
    all_values = jnp.concatenate(
        [layer_zero[:, 1].reshape(requests_here * max_len, head_dim), new_values], axis=0
    )

    def attend(query_one):
        scores = (
            jnp.einsum("td,nd->tn", query_one, all_keys, preferred_element_type=jnp.float32)
            * score_scale
        )
        attn_probs = weigh(scores, allowed)
        return jnp.dot(attn_probs, all_values, preferred_element_type=jnp.float32).astype(
            jnp.bfloat16
        )

    heads_out = lax.map(attend, queries)
    attention = heads_out.transpose(1, 0, 2).reshape(rows_here, heads_here * head_dim)
    return (attention, partner_cache)


def solution(mesh):
    return jax.shard_map(
        on_device,
        mesh=mesh,
        in_specs=(
            P("group", "mp"),
            P(),
            P("group", "mp"),
            P("group", None),
            P("group", None),
            P("group", "mp", None, None, None),
            P(),
            P("group"),
            P("group"),
        ),
        out_specs=(P("group", "mp"), P("group", "mp", None, None, None)),
        check_vma=False,
    )
```

profile of v0, /device:TPU:1, one launch (start us, length us, event | category | flops | bytes accessed | tf_op | source)
XLA Modules:
  0.0 322.5 jit_solution(18150802313634479583)
XLA Ops:
  7.2 0.7 all-gather.5.cloned.1.call-update
  8.7 1.3 constant_dynamic-slice_fusion
  10.6 0.8 copy.29
  11.6 15.5 %scatter_custom_fusion = s32[4096]{0:T(1024)S(1)} fusion(s32[4096]{0:T(1024)S(1)} %bitcast.75, s32[4096]{0:T(1024)S(1)} %iota.46, s32[]{:T(128)} %copy.64), kind=kCustom, calls=%fused_computation.79 | custom fusion | bytes 16388 | tf_op jit(solution)/shard_map/scatter | solution.py:82
  27.7 0.8 scatter_custom_fusion.1
  28.5 0.8 all_to_all.11
  29.2 17.1 %all-to-all-start = ((s32[64,1,2]{2,1,0:T(1,128)}), s32[64,1,2]{2,1,0:T(1,128)S(1)}, u32[]{:S(2)}, u32[]{:S(2)}) async-start(s32[64,1,2]{2,1,0:T(1,128)} %bitcast.4), calls=%async_computation | async-start | bytes 65536 | tf_op jit(solution)/shard_map/all_to_all | solution.py:107
  46.4 0.7 fusion.16
  47.3 1.5 fusion.45
  48.8 2.6 compare_select_fusion.2
  51.3 0.9 select_reduce_fusion
  52.2 0.8 fusion.17
  53.3 0.7 iota_compare_fusion.3
  54.1 2.3 scatter_custom_fusion.2
  56.4 1.5 reshape.342
  57.9 12.3 %all-to-all-start.1 = ((bf16[64,2,4096]{2,1,0:T(2,128)(2,1)}), bf16[64,2,4096]{2,1,0:T(2,128)(2,1)S(1)}, u32[]{:S(2)}, u32[]{:S(2)}) async-start(bf16[64,2,4096]{2,1,0:T(2,128)(2,1)} %reshape.342), calls=%async_computation.1 | async-start | bytes 2097152 | tf_op jit(solution)/shard_map/all_to_all | solution.py:106
  70.9 0.7 reduce.3
  71.8 1.5 fusion.7
  73.3 1.6 fusion.9
  74.9 22.4 %all-to-all-done.1 = bf16[64,2,4096]{2,1,0:T(2,128)(2,1)S(1)} async-done(((bf16[64,2,4096]{2,1,0:T(2,128)(2,1)}), bf16[64,2,4096]{2,1,0:T(2,128)(2,1)S(1)}, u32[]{:S(2)}, u32[]{:S(2)}) %all-to-all-start.1) | async-done | bytes 1048608 | tf_op jit(solution)/shard_map/all_to_all | solution.py:106
  97.3 1.2 reshape.387
  98.5 2.8 scatter_custom_fusion.3
  101.7 5.9 %collective-permute-start = (bf16[4,1,2,256,128]{4,3,2,0,1:T(8,128)(2,1)S(1)}, bf16[4,1,2,256,128]{4,3,2,0,1:T(8,128)(2,1)S(1)}, u32[]{:S(2)}, u32[]{:S(2)}) collective-permute-start(bf16[4,1,2,256,128]{4,3,2,0,1:T(8,128)(2,1)S(1)} %bitcast_select_fusion), channel_id=1, source_target_pairs={{0,1},{1,0},{2,3},{3,2},{4,5},{5,4},{6,7},{7,6},{8,9},{9,8},{10,11... | collective-permute-start | bytes 1572872 | tf_op jit(solution)/shard_map/ppermute | solution.py:15
  107.7 30.1 %all-gather.9.cloned.1.call-done = bf16[4096,128]{1,0:T(8,128)(2,1)} async-done(((bf16[64,128]{1,0:T(8,128)(2,1)}), bf16[4096,128]{1,0:T(8,128)(2,1)}) %all-gather.9.cloned.1.call-update) | async-done | bytes 1048592 | tf_op jit(solution)/shard_map/all_gather | solution.py:136
  137.8 1.7 convolution_bitcast_fusion
  139.9 80.1 %all-gather.11.cloned.1.call-done = bf16[4096,128]{1,0:T(8,128)(2,1)} async-done(((bf16[64,128]{1,0:T(8,128)(2,1)}), bf16[4096,128]{1,0:T(8,128)(2,1)}) %all-gather.11.cloned.1.call-update) | async-done | bytes 1048592 | tf_op jit(solution)/shard_map/all_gather | solution.py:141
  220.0 1.6 convolution_convert_fusion.1
  222.0 85.4 %all-gather.7.cloned.1.call-done = bf16[4096,512]{1,0:T(8,128)(2,1)} async-done(((bf16[64,512]{1,0:T(8,128)(2,1)}), bf16[4096,512]{1,0:T(8,128)(2,1)}) %all-gather.7.cloned.1.call-update) | async-done | bytes 4194320 | tf_op jit(solution)/shard_map/all_gather | solution.py:131
  307.4 2.9 fusion.46
  310.8 3.7 %while.10 = (s32[]{:T(128)}, bf16[4,128,128]{2,1,0:T(8,128)(2,1)S(1)}, bf16[4,128,128]{2,1,0:T(8,128)(2,1)S(1)}, bf16[1152,128]{1,0:T(8,128)(2,1)S(1)}, pred[128...) while((s32[]{:T(128)}, bf16[4,128,128]{2,1,0:T(8,128)(2,1)S(1)}, ...), condition=%wide.region_13.14_spmd, body=%wide.region_10.13_spmd.sunk | while | flops 76693248 | bytes 2574941 | solution.py:174
  314.5 0.7 copy_bitcast_fusion
  315.2 0.8 copy.65
  (66 shorter events, 8.5 us)
Async XLA Ops:
  7.2 0.8 copy-start
  7.2 64.6 %all-gather.5.cloned.1.call-start = ((), (), s32[]{:S(2)}) async-start(), calls=%async_computation.2 | async-start | bytes 1179648 | tf_op jit(solution)/shard_map/all_gather | solution.py:121
  7.9 129.9 %all-gather.9.cloned.1.call-start = ((), (), s32[]{:S(2)}) async-start(), calls=%async_computation.4 | async-start | bytes 1064960 | tf_op jit(solution)/shard_map/all_gather | solution.py:136
  8.7 211.3 %all-gather.11.cloned.1.call-start = ((), (), s32[]{:S(2)}) async-start(), calls=%async_computation.5 | async-start | bytes 1064960 | tf_op jit(solution)/shard_map/all_gather | solution.py:141
  10.1 297.3 %all-gather.7.cloned.1.call-start = ((), (), s32[]{:S(2)}) async-start(), calls=%async_computation.3 | async-start | bytes 4259840 | tf_op jit(solution)/shard_map/all_gather | solution.py:131
  29.2 28.6 %all-to-all-start = ((s32[64,1,2]{2,1,0:T(1,128)}), s32[64,1,2]{2,1,0:T(1,128)S(1)}, u32[]{:S(2)}, u32[]{:S(2)}) async-start(s32[64,1,2]{2,1,0:T(1,128)} %bitcast.4), calls=%async_computation | async-start | bytes 65536 | tf_op jit(solution)/shard_map/all_to_all | solution.py:107
  56.4 13.8 %copy-start.2 = (s32[128]{0:T(128)S(1)}, s32[128]{0:T(128)}, u32[]{:S(2)}) copy-start(s32[128]{0:T(128)} %param.19) | copy-start | bytes 1540
  57.9 15.5 %copy-start.1 = (f32[4096]{0:T(1024)S(1)}, f32[4096]{0:T(1024)}, u32[]{:S(2)}) copy-start(f32[4096]{0:T(1024)} %param.12) | copy-start | bytes 49156
  57.9 39.4 %all-to-all-start.1 = ((bf16[64,2,4096]{2,1,0:T(2,128)(2,1)}), bf16[64,2,4096]{2,1,0:T(2,128)(2,1)S(1)}, u32[]{:S(2)}, u32[]{:S(2)}) async-start(bf16[64,2,4096]{2,1,0:T(2,128)(2,1)} %reshape.342), calls=%async_computation.1 | async-start | bytes 2097152 | tf_op jit(solution)/shard_map/all_to_all | solution.py:106
  101.7 119.9 %collective-permute-start = (bf16[4,1,2,256,128]{4,3,2,0,1:T(8,128)(2,1)S(1)}, bf16[4,1,2,256,128]{4,3,2,0,1:T(8,128)(2,1)S(1)}, u32[]{:S(2)}, u32[]{:S(2)}) collective-permute-start(bf16[4,1,2,256,128]{4,3,2,0,1:T(8,128)(2,1)S(1)} %bitcast_select_fusion), channel_id=1, source_target_pairs={{0,1},{1,0},{2,3},{3,2},{4,5},{5,4},{6,7},{7,6},{8,9},{9,8},{10,11... | collective-permute-start | bytes 1572872 | tf_op jit(solution)/shard_map/ppermute | solution.py:15
Sparse Core Ops, SparseCore 0:
  10.1 34.5 all-gather.4
  48.4 89.3 all-gather.8
  140.9 79.0 all-gather.10
  222.9 84.3 all-gather.6
where the time goes:
time: 327 us; the launch traced here: 323 us
  waiting for transfers between devices  219 us (67%)
  starting transfers between devices  35.5 us (11%)
  local copies, waits for them, and re-layouts  32 us (10%)
  between operations  14.2 us (4%)
  other arithmetic  12.5 us (4%)
  matrix products  8.94 us (3%)
    all_gather x1, waiting for transfers between devices, on_device(): lax.all_gather(q_weight, 'group', axis=0, tiled=True)  85.4 us
    all_gather x1, waiting for transfers between devices, on_device(): lax.all_gather(value_cols, 'group', axis=0, tiled=True)  80.1 us
    all_gather x1, waiting for transfers between devices, on_device(): lax.all_gather(key_cols, 'group', axis=0, tiled=True)  30.1 us
    all_to_all x1, waiting for transfers between devices, on_device(): lax.all_to_all(outgoing, 'group', split_axis=0, concat_axis=0, tiled=True)  22.4 us
    all_to_all x1, starting transfers between devices, on_device(): lax.all_to_all(outgoing_slots, 'group', split_axis=0, concat_axis=0, tile...  17.1 us
    scatter x1, local copies, waits for them, and re-layouts, on_device(): jnp.zeros((flat_table.shape[0],), jnp.int32).at[flat_table].set(slot_ids)  15.5 us
    all_to_all x1, starting transfers between devices, on_device(): lax.all_to_all(outgoing, 'group', split_axis=0, concat_axis=0, tiled=True)  12.3 us
  transfers between devices with their start and end apart: 7, of which 4 were waited for; matrix products, arithmetic and copies ran while one was open for 14% of the time, Pallas kernels for 0%

commit v1 on v0

--- a/solution.py
+++ b/solution.py
@@ -126,21 +126,16 @@
     first_kv = mp_idx * heads_here // per_kv
     key_cols = lax.dynamic_slice_in_dim(k_weight, first_kv * head_dim, head_dim, 1)
     value_cols = lax.dynamic_slice_in_dim(v_weight, first_kv * head_dim, head_dim, 1)
-    query_sum = jnp.dot(
+    q_cols = q_weight.shape[1]
+    joined_cols = jnp.concatenate([q_weight, key_cols, value_cols], axis=1)
+    joined_sum = jnp.dot(
         normed,
-        lax.all_gather(q_weight, "group", axis=0, tiled=True),
+        lax.all_gather(joined_cols, "group", axis=0, tiled=True),
         preferred_element_type=jnp.float32,
     )
-    key_sum = jnp.dot(
-        normed,
-        lax.all_gather(key_cols, "group", axis=0, tiled=True),
-        preferred_element_type=jnp.float32,
-    )
-    value_sum = jnp.dot(
-        normed,
-        lax.all_gather(value_cols, "group", axis=0, tiled=True),
-        preferred_element_type=jnp.float32,
-    )
+    query_sum = joined_sum[:, :q_cols]
+    key_sum = joined_sum[:, q_cols : q_cols + head_dim]
+    value_sum = joined_sum[:, q_cols + head_dim :]
     position = token_positions(token_request, lengths, requests_here)
     queries = (
         rotate(query_sum.reshape(rows_here, heads_here, head_dim), position)

time: 327 us -> 168 us (0.51); the launches traced: 323 us -> 167 us
  waiting for transfers between devices: 219 us -> 78 us
  starting transfers between devices: 35.5 us -> 28.9 us
  local copies, waits for them, and re-layouts: 32 us -> 28.3 us
    all_gather x3 -> x1, waiting for transfers between devices: 196 us -> 47.5 us  [on_device(): lax.all_gather(joined_cols, 'group', axis=0, tiled=True)]
    all_to_all x1, starting transfers between devices: 12.3 us -> 5.91 us  [on_device(): lax.all_to_all(outgoing, 'group', split_axis=0, concat_axis=0, tiled=True)]
    all_to_all x1, waiting for transfers between devices: 0.01 us -> 6.23 us  [on_device(): lax.all_to_all(outgoing_slots, 'group', split_axis=0, concat_axis=0, tile...]
  transfers between devices with their start and end apart: 7 -> 5, of which waited for: 4 -> 3; matrix products, arithmetic and copies ran while one was open for 14% -> 21% of each run, Pallas kernels for 0% -> 0%
where the time goes in v1:
time: 168 us; the launch traced here: 167 us
  waiting for transfers between devices  78 us (46%)
  starting transfers between devices  28.9 us (17%)
  local copies, waits for them, and re-layouts  28.3 us (17%)
  between operations  14.4 us (9%)
  other arithmetic  10.6 us (6%)
  matrix products  6.52 us (4%)
    all_gather x1, waiting for transfers between devices, on_device(): lax.all_gather(joined_cols, 'group', axis=0, tiled=True)  47.5 us
    all_to_all x1, waiting for transfers between devices, on_device(): lax.all_to_all(outgoing, 'group', split_axis=0, concat_axis=0, tiled=True)  23.5 us
    all_to_all x1, starting transfers between devices, on_device(): lax.all_to_all(outgoing_slots, 'group', split_axis=0, concat_axis=0, tile...  17.1 us
    scatter x1, local copies, waits for them, and re-layouts, on_device(): jnp.zeros((flat_table.shape[0],), jnp.int32).at[flat_table].set(slot_ids)  15.5 us
    all_to_all x1, waiting for transfers between devices, on_device(): lax.all_to_all(outgoing_slots, 'group', split_axis=0, concat_axis=0, tile...  6.23 us
    all_to_all x1, starting transfers between devices, on_device(): lax.all_to_all(outgoing, 'group', split_axis=0, concat_axis=0, tiled=True)  5.91 us
    ppermute x1, starting transfers between devices, from_partner(): lax.ppermute(x, axis, [(i, i ^ 1 << bit) for i in range(lax.axis_size(axi...  5.74 us
    dot_general x1, matrix products, on_device(): jnp.dot(normed, lax.all_gather(joined_cols, 'group', axis=0, tiled=True),...  3.84 us
  transfers between devices with their start and end apart: 5, of which 3 were waited for; matrix products, arithmetic and copies ran while one was open for 21% of the time, Pallas kernels for 0%

profile of v1, /device:TPU:1, one launch (start us, length us, event | category | flops | bytes accessed | tf_op | source)
XLA Modules:
  0.0 166.8 jit_solution(10560465115088864470)
XLA Ops:
  7.2 0.7 all-gather.3.cloned.1.call-update
  8.0 0.8 constant_dynamic-slice_fusion
  8.7 1.5 pad_maximum_fusion.1
  10.2 0.8 copy.26
  11.2 15.5 %scatter_custom_fusion = s32[4096]{0:T(1024)S(1)} fusion(s32[4096]{0:T(1024)S(1)} %bitcast.74, s32[4096]{0:T(1024)S(1)} %iota.46, s32[]{:T(128)} %copy.60), kind=kCustom, calls=%fused_computation.82 | custom fusion | bytes 16388 | tf_op jit(solution)/shard_map/scatter | solution.py:82
  27.3 0.8 scatter_custom_fusion.1
  28.1 0.8 all_to_all.11
  28.8 17.1 %all-to-all-start = ((s32[64,1,2]{2,1,0:T(1,128)}), s32[64,1,2]{2,1,0:T(1,128)S(1)}, u32[]{:S(2)}, u32[]{:S(2)}) async-start(s32[64,1,2]{2,1,0:T(1,128)} %bitcast.4), calls=%async_computation | async-start | bytes 65536 | tf_op jit(solution)/shard_map/all_to_all | solution.py:107
  46.0 0.7 fusion.28
  46.7 2.3 %scatter_custom_fusion.2 = bf16[128,4096]{1,0:T(8,128)(2,1)S(1)} fusion(s32[64]{0:T(128)S(1)} %compare_select_fusion.7, bf16[8,8,32,128]{3,2,1,0:T(8,128)(2,1)} %bitcast.72, bf16[]{:T(256)} %constant.130.clone.1), kind=kCustom, calls=%fused_computation.24 | custom fusion | bytes 1572866 | tf_op jit(solution)/shard_map/scatter | solution.py:96
  49.0 1.5 reshape.342
  50.5 6.2 %all-to-all-done = s32[64,1,2]{2,1,0:T(1,128)S(1)} async-done(((s32[64,1,2]{2,1,0:T(1,128)}), s32[64,1,2]{2,1,0:T(1,128)S(1)}, u32[]{:S(2)}, u32[]{:S(2)}) %all-to-all-start) | async-done | bytes 544 | tf_op jit(solution)/shard_map/all_to_all | solution.py:107
  56.8 5.9 %all-to-all-start.1 = ((bf16[64,2,4096]{2,1,0:T(2,128)(2,1)}), bf16[64,2,4096]{2,1,0:T(2,128)(2,1)S(1)}, u32[]{:S(2)}, u32[]{:S(2)}) async-start(bf16[64,2,4096]{2,1,0:T(2,128)(2,1)} %reshape.342), calls=%async_computation.1 | async-start | bytes 2097152 | tf_op jit(solution)/shard_map/all_to_all | solution.py:106
  62.9 0.6 fusion.49
  63.5 2.5 %compare_select_fusion.2 = s32[1024,1]{0,1:T(1,128)S(1)} fusion(s32[]{:T(128)} %bitcast.13, s32[]{:T(128)} %bitcast.14, s32[]{:T(128)} %bitcast.16, s32[]{:T(128)} %bitcast.15), kind=kLoop, calls=%fused_computation.68 | loop fusion | flops 17408 | bytes 4112 | tf_op jit(solution)/shard_map/gather | solution.py:50
  66.5 0.5 broadcast.369
  67.0 0.7 reduce.3
  67.9 23.5 %all-to-all-done.1 = bf16[64,2,4096]{2,1,0:T(2,128)(2,1)S(1)} async-done(((bf16[64,2,4096]{2,1,0:T(2,128)(2,1)}), bf16[64,2,4096]{2,1,0:T(2,128)(2,1)S(1)}, u32[]{:S(2)}, u32[]{:S(2)}) %all-to-all-start.1) | async-done | bytes 1048608 | tf_op jit(solution)/shard_map/all_to_all | solution.py:106
  91.5 0.4 reshape.387
  91.9 2.1 %scatter_custom_fusion.3 = bf16[65,4096]{1,0:T(8,128)(2,1)S(1)} fusion(s32[128]{0:T(128)S(1)} %fusion.43, bf16[128,4096]{1,0:T(8,128)(2,1)S(1)} %reshape.387, bf16[]{:T(256)} %constant.130.clone.1), kind=kCustom, calls=%fused_computation.34 | custom fusion | bytes 532482 | tf_op jit(solution)/shard_map/scatter | solution.py:113
  94.4 5.7 %collective-permute-start = (bf16[4,1,2,256,128]{4,3,2,0,1:T(8,128)(2,1)S(1)}, bf16[4,1,2,256,128]{4,3,2,0,1:T(8,128)(2,1)S(1)}, u32[]{:S(2)}, u32[]{:S(2)}) collective-permute-start(bf16[4,1,2,256,128]{4,3,2,0,1:T(8,128)(2,1)S(1)} %bitcast_select_fusion), channel_id=1, source_target_pairs={{0,1},{1,0},{2,3},{3,2},{4,5},{5,4},{6,7},{7,6},{8,9},{9,8},{10,11... | collective-permute-start | bytes 1572872 | tf_op jit(solution)/shard_map/ppermute | solution.py:15
  100.5 1.6 fusion.7
  102.4 47.5 %all-gather.5.cloned.1.call-done = bf16[4096,768]{1,0:T(8,128)(2,1)} async-done(((bf16[64,768]{1,0:T(8,128)(2,1)}), bf16[4096,768]{1,0:T(8,128)(2,1)}) %all-gather.5.cloned.1.call-update) | async-done | bytes 6291472 | tf_op jit(solution)/shard_map/all_gather | solution.py:133
  149.9 3.8 %fusion.10 = f32[128,768]{1,0:T(8,128)S(1)} fusion(bf16[4096,768]{1,0:T(8,128)(2,1)} %all-gather.5.cloned.1.call-done, bf16[128,4096]{1,0:T(8,128)(2,1)S(1)} %copy-done, f32[4096]{0:T(1024)S(1)} %copy-done.3, f32[128]{0:T(128)S(1)} %add_sqrt_fusion), kind=kOutput, calls=%fused_computation.20 | convolution fusion | flops 807403520 | bytes 7750144 | tf_op jit(solution)/shard_map/dot_general | solution.py:131
  154.7 3.8 %while.10 = (s32[]{:T(128)}, bf16[4,128,128]{2,1,0:T(8,128)(2,1)S(1)}, bf16[4,128,128]{2,1,0:T(8,128)(2,1)S(1)}, bf16[1152,128]{1,0:T(8,128)(2,1)S(1)}, pred[128...) while((s32[]{:T(128)}, bf16[4,128,128]{2,1,0:T(8,128)(2,1)S(1)}, ...), condition=%wide.region_13.14_spmd, body=%wide.region_10.13_spmd.sunk | while | flops 76693248 | bytes 2574941 | solution.py:169
  154.8 0.3 fusion.61
  155.4 0.3 fusion.63
  155.7 0.3 fusion.61
  156.6 0.3 fusion.61
  157.6 0.3 fusion.61
  158.5 0.7 copy_bitcast_fusion
  159.2 0.8 copy.61
  (60 shorter events, 5.5 us)
Async XLA Ops:
  7.2 93.4 %all-gather.3.cloned.1.call-start = ((), (), s32[]{:S(2)}) async-start(), calls=%async_computation.2 | async-start | bytes 1179648 | tf_op jit(solution)/shard_map/all_gather | solution.py:121
  7.9 142.0 %all-gather.5.cloned.1.call-start = ((), (), s32[]{:S(2)}) async-start(), calls=%async_computation.3 | async-start | bytes 6389760 | tf_op jit(solution)/shard_map/all_gather | solution.py:133
  28.8 27.9 %all-to-all-start = ((s32[64,1,2]{2,1,0:T(1,128)}), s32[64,1,2]{2,1,0:T(1,128)S(1)}, u32[]{:S(2)}, u32[]{:S(2)}) async-start(s32[64,1,2]{2,1,0:T(1,128)} %bitcast.4), calls=%async_computation | async-start | bytes 65536 | tf_op jit(solution)/shard_map/all_to_all | solution.py:107
  49.0 13.9 %copy-start.2 = (s32[4]{0:T(128)S(1)}, s32[4]{0:T(128)}, u32[]{:S(2)}) copy-start(s32[4]{0:T(128)} %param.18) | copy-start | bytes 52
  49.0 17.0 %copy-start.1 = (s32[128]{0:T(128)S(1)}, s32[128]{0:T(128)}, u32[]{:S(2)}) copy-start(s32[128]{0:T(128)} %param.19) | copy-start | bytes 1540
  56.8 34.7 %all-to-all-start.1 = ((bf16[64,2,4096]{2,1,0:T(2,128)(2,1)}), bf16[64,2,4096]{2,1,0:T(2,128)(2,1)S(1)}, u32[]{:S(2)}, u32[]{:S(2)}) async-start(bf16[64,2,4096]{2,1,0:T(2,128)(2,1)} %reshape.342), calls=%async_computation.1 | async-start | bytes 2097152 | tf_op jit(solution)/shard_map/all_to_all | solution.py:106
  94.4 55.5 %copy-start.3 = (f32[4096]{0:T(1024)S(1)}, f32[4096]{0:T(1024)}, u32[]{:S(2)}) copy-start(f32[4096]{0:T(1024)} %param.12) | copy-start | bytes 49156
  94.4 7.7 %collective-permute-start = (bf16[4,1,2,256,128]{4,3,2,0,1:T(8,128)(2,1)S(1)}, bf16[4,1,2,256,128]{4,3,2,0,1:T(8,128)(2,1)S(1)}, u32[]{:S(2)}, u32[]{:S(2)}) collective-permute-start(bf16[4,1,2,256,128]{4,3,2,0,1:T(8,128)(2,1)S(1)} %bitcast_select_fusion), channel_id=1, source_target_pairs={{0,1},{1,0},{2,3},{3,2},{4,5},{5,4},{6,7},{7,6},{8,9},{9,8},{10,11... | collective-permute-start | bytes 1572872 | tf_op jit(solution)/shard_map/ppermute | solution.py:15
  100.5 49.4 %copy-start = (bf16[128,4096]{1,0:T(8,128)(2,1)S(1)}, bf16[128,4096]{1,0:T(8,128)(2,1)}, u32[]{:S(2)}) copy-start(bf16[128,4096]{1,0:T(8,128)(2,1)} %all-gather.3.cloned.1.call-done) | copy-start | bytes 3145732
Sparse Core Ops, SparseCore 0:
  10.1 34.5 all-gather.2
  48.3 101.5 all-gather.4

commit v2 on v1

--- a/solution.py
+++ b/solution.py
@@ -1,10 +1,11 @@
 import jax
 import jax.numpy as jnp
 from jax import lax
-from jax.sharding import PartitionSpec as P
+from jax.sharding import Mesh, PartitionSpec as P
 
 HEADS = 32
 KVH = 4
+GROUP = ("gz", "gy")
 
 
 rope_theta = 5000000.0
@@ -66,8 +67,8 @@
 def on_device(
     tokens, attn_gain, q_weight, k_weight, v_weight, kv_pool, page_table, lengths, token_request
 ):
-    groups = lax.axis_size("group")
-    group_idx = lax.axis_index("group")
+    groups = lax.axis_size(GROUP)
+    group_idx = lax.axis_index(GROUP)
     mp_idx = lax.axis_index("mp")
     pool_pages = kv_pool.shape[0]
     pair_count = kv_pool.shape[1]
@@ -103,8 +104,8 @@
         .reshape(groups, capacity)
     )
     arrived, arrived_slots = (
-        lax.all_to_all(outgoing, "group", split_axis=0, concat_axis=0, tiled=True),
-        lax.all_to_all(outgoing_slots, "group", split_axis=0, concat_axis=0, tiled=True),
+        lax.all_to_all(outgoing, GROUP, split_axis=0, concat_axis=0, tiled=True),
+        lax.all_to_all(outgoing_slots, GROUP, split_axis=0, concat_axis=0, tiled=True),
     )
     landing = jnp.where(arrived_slots < 0, pool_pages, arrived_slots).reshape(-1)
     placed = (
@@ -130,7 +131,9 @@
     joined_cols = jnp.concatenate([q_weight, key_cols, value_cols], axis=1)
     joined_sum = jnp.dot(
         normed,
-        lax.all_gather(joined_cols, "group", axis=0, tiled=True),
+        lax.all_gather(
+            lax.all_gather(joined_cols, "gy", axis=0, tiled=True), "gz", axis=0, tiled=True
+        ),
         preferred_element_type=jnp.float32,
     )
     query_sum = joined_sum[:, :q_cols]
@@ -171,21 +174,32 @@
     return (attention, partner_cache)
 
 
+def split_mesh(mesh):
+    devices = mesh.devices
+    groups, parts = devices.shape
+    try:
+        z_of = [d.coords[2] for d in devices[:, 0]]
+        inner = next((i for i in range(1, groups) if z_of[i] != z_of[0]), groups)
+    except (AttributeError, IndexError, TypeError):
+        inner = int(round(groups**0.5))
+    return Mesh(devices.reshape(groups // inner, inner, parts), ("gz", "gy", "mp"))
+
+
 def solution(mesh):
     return jax.shard_map(
         on_device,
-        mesh=mesh,
+        mesh=split_mesh(mesh),
         in_specs=(
-            P("group", "mp"),
+            P(GROUP, "mp"),
             P(),
-            P("group", "mp"),
-            P("group", None),
-            P("group", None),
-            P("group", "mp", None, None, None),
+            P(GROUP, "mp"),
+            P(GROUP, None),
+            P(GROUP, None),
+            P(GROUP, "mp", None, None, None),
             P(),
-            P("group"),
-            P("group"),
+            P(GROUP),
+            P(GROUP),
         ),
-        out_specs=(P("group", "mp"), P("group", "mp", None, None, None)),
+        out_specs=(P(GROUP, "mp"), P(GROUP, "mp", None, None, None)),
         check_vma=False,
     )

time: 168 us -> 165 us (0.982)
  waiting for transfers between devices: 78 us -> 49.2 us
  blocking collectives: 0 us -> 24.5 us
  starting transfers between devices: 28.9 us -> 32.6 us
    all_gather x0 -> x1, blocking collectives: none -> 24.5 us  [on_device(): lax.all_gather(joined_cols, 'gy', axis=0, tiled=True)]
    all_gather x1, waiting for transfers between devices: 47.5 us -> 24.5 us  [on_device(): lax.all_gather(lax.all_gather(joined_cols, 'gy', axis=0, tiled=True), 'gz...]
    ppermute x1, starting transfers between devices: 5.74 us -> 12.6 us  [from_partner(): lax.ppermute(x, axis, [(i, i ^ 1 << bit) for i in range(lax.axis_size(axi...]
    all_to_all x2, waiting for transfers between devices: 29.8 us -> 24 us  [the longest x1 16.6 us: on_device(): lax.all_to_all(outgoing, GROUP, split_axis=0, concat_axis=0, tiled=True)]
    all_to_all x2, starting transfers between devices: 23 us -> 19.9 us  [the longest x1 15.2 us: on_device(): lax.all_to_all(outgoing_slots, GROUP, split_axis=0, concat_axis=0, tiled=...]
  transfers between devices with their start and end apart: 5 -> 5, of which waited for: 3 -> 3; matrix products, arithmetic and copies ran while one was open for 21% -> 20% of each run, Pallas kernels for 0% -> 0%
where the time goes in v2:
time: 165 us; the launch traced here: 164 us
  waiting for transfers between devices  49.2 us (30%)
  starting transfers between devices  32.6 us (20%)
  local copies, waits for them, and re-layouts  27.2 us (16%)
  blocking collectives  24.5 us (15%)
  between operations  14.5 us (9%)
  other arithmetic  9.38 us (6%)
  matrix products  6.54 us (4%)
    all_gather x1, blocking collectives, on_device(): lax.all_gather(joined_cols, 'gy', axis=0, tiled=True)  24.5 us
    all_gather x1, waiting for transfers between devices, on_device(): lax.all_gather(lax.all_gather(joined_cols, 'gy', axis=0, tiled=True), 'gz...  24.5 us
    all_to_all x1, waiting for transfers between devices, on_device(): lax.all_to_all(outgoing, GROUP, split_axis=0, concat_axis=0, tiled=True)  16.6 us
    scatter x1, local copies, waits for them, and re-layouts, on_device(): jnp.zeros((flat_table.shape[0],), jnp.int32).at[flat_table].set(slot_ids)  15.5 us
    all_to_all x1, starting transfers between devices, on_device(): lax.all_to_all(outgoing_slots, GROUP, split_axis=0, concat_axis=0, tiled=...  15.2 us
    ppermute x1, starting transfers between devices, from_partner(): lax.ppermute(x, axis, [(i, i ^ 1 << bit) for i in range(lax.axis_size(axi...  12.6 us
    all_to_all x1, waiting for transfers between devices, on_device(): lax.all_to_all(outgoing_slots, GROUP, split_axis=0, concat_axis=0, tiled=...  7.41 us
    all_to_all x1, starting transfers between devices, on_device(): lax.all_to_all(outgoing, GROUP, split_axis=0, concat_axis=0, tiled=True)  4.74 us
  transfers between devices with their start and end apart: 5, of which 3 were waited for; matrix products, arithmetic and copies ran while one was open for 20% of the time, Pallas kernels for 0%

profile of v2, /device:TPU:1, one launch (start us, length us, event | category | flops | bytes accessed | tf_op | source)
XLA Modules:
  0.0 164.1 jit_solution(1183774778455679669)
XLA Ops:
  7.2 0.7 all-gather.3.cloned.1.call-update
  8.0 0.8 constant_dynamic-slice_fusion
  8.7 0.8 pad_maximum_fusion.1
  9.6 24.5 %all_gather.10 = bf16[512,768]{1,0:T(8,128)(2,1)} all-gather(bf16[64,768]{1,0:T(8,128)(2,1)S(1)} %pad_maximum_fusion.1), channel_id=1, replica_groups=mesh['gz'=8,'gy'=8,'mp'=8] {'gy'}, dimensions={0}, use_global_device_ids=true | all-gather | bytes 884736 | tf_op jit(solution)/shard_map/all_gather | solution.py:135
  34.4 15.5 %scatter_custom_fusion = s32[4096]{0:T(1024)S(1)} fusion(s32[4096]{0:T(1024)S(1)} %bitcast.70, s32[4096]{0:T(1024)S(1)} %iota.46, s32[]{:T(128)} %copy.60), kind=kCustom, calls=%fused_computation.82 | custom fusion | bytes 16388 | tf_op jit(solution)/shard_map/scatter | solution.py:83
  50.5 0.8 scatter_custom_fusion.1
  51.3 0.8 all_to_all.11
  52.1 15.2 %all-to-all-start = ((s32[64,1,2]{2,1,0:T(1,128)}), s32[64,1,2]{2,1,0:T(1,128)S(1)}, u32[]{:S(2)}, u32[]{:S(2)}) async-start(s32[64,1,2]{2,1,0:T(1,128)} %bitcast.4), calls=%async_computation | async-start | bytes 65536 | tf_op jit(solution)/shard_map/all_to_all | solution.py:108
  67.4 1.8 %scatter_custom_fusion.2 = bf16[128,4096]{1,0:T(8,128)(2,1)S(1)} fusion(s32[64]{0:T(128)S(1)} %compare_select_fusion.7, bf16[8,8,32,128]{3,2,1,0:T(8,128)(2,1)S(1)} %bitcast.68, bf16[]{:T(256)} %constant.132.clone.1), kind=kCustom, calls=%fused_computation.24 | custom fusion | bytes 1572866 | tf_op jit(solution)/shard_map/scatter | solution.py:97
  69.2 1.5 reshape.342
  70.7 7.4 %all-to-all-done = s32[64,1,2]{2,1,0:T(1,128)S(1)} async-done(((s32[64,1,2]{2,1,0:T(1,128)}), s32[64,1,2]{2,1,0:T(1,128)S(1)}, u32[]{:S(2)}, u32[]{:S(2)}) %all-to-all-start) | async-done | bytes 544 | tf_op jit(solution)/shard_map/all_to_all | solution.py:108
  78.1 4.7 %all-to-all-start.1 = ((bf16[64,2,4096]{2,1,0:T(2,128)(2,1)}), bf16[64,2,4096]{2,1,0:T(2,128)(2,1)S(1)}, u32[]{:S(2)}, u32[]{:S(2)}) async-start(bf16[64,2,4096]{2,1,0:T(2,128)(2,1)} %reshape.342), calls=%async_computation.1 | async-start | bytes 2097152 | tf_op jit(solution)/shard_map/all_to_all | solution.py:107
  83.1 0.7 fusion.49
  83.7 2.5 %compare_select_fusion.2 = s32[1024,1]{0,1:T(1,128)S(1)} fusion(s32[]{:T(128)} %bitcast.13, s32[]{:T(128)} %bitcast.14, s32[]{:T(128)} %bitcast.16, s32[]{:T(128)} %bitcast.15), kind=kLoop, calls=%fused_computation.68 | loop fusion | flops 17408 | bytes 4112 | tf_op jit(solution)/shard_map/gather | solution.py:51
  86.8 0.5 broadcast.369
  87.3 0.7 reduce.3
  88.2 16.6 %all-to-all-done.1 = bf16[64,2,4096]{2,1,0:T(2,128)(2,1)S(1)} async-done(((bf16[64,2,4096]{2,1,0:T(2,128)(2,1)}), bf16[64,2,4096]{2,1,0:T(2,128)(2,1)S(1)}, u32[]{:S(2)}, u32[]{:S(2)}) %all-to-all-start.1) | async-done | bytes 1048608 | tf_op jit(solution)/shard_map/all_to_all | solution.py:107
  104.8 0.4 reshape.387
  105.2 2.1 %scatter_custom_fusion.3 = bf16[65,4096]{1,0:T(8,128)(2,1)S(1)} fusion(s32[128]{0:T(128)S(1)} %fusion.43, bf16[128,4096]{1,0:T(8,128)(2,1)S(1)} %reshape.387, bf16[]{:T(256)} %constant.132.clone.1), kind=kCustom, calls=%fused_computation.34 | custom fusion | bytes 532482 | tf_op jit(solution)/shard_map/scatter | solution.py:114
  107.7 12.6 %collective-permute-start = (bf16[4,1,2,256,128]{4,3,2,0,1:T(8,128)(2,1)S(1)}, bf16[4,1,2,256,128]{4,3,2,0,1:T(8,128)(2,1)S(1)}, u32[]{:S(2)}, u32[]{:S(2)}) collective-permute-start(bf16[4,1,2,256,128]{4,3,2,0,1:T(8,128)(2,1)S(1)} %bitcast_select_fusion), channel_id=1, source_target_pairs={{0,1},{1,0},{2,3},{3,2},{4,5},{5,4},{6,7},{7,6},{8,9},{9,8},{10,11... | collective-permute-start | bytes 1572872 | tf_op jit(solution)/shard_map/ppermute | solution.py:16
  120.7 1.6 fusion.7
  122.6 24.5 %all-gather.5.cloned.1.call-done = bf16[4096,768]{1,0:T(8,128)(2,1)} async-done(((bf16[512,768]{1,0:T(8,128)(2,1)}), bf16[4096,768]{1,0:T(8,128)(2,1)}) %all-gather.5.cloned.1.call-update) | async-done | bytes 6291472 | tf_op jit(solution)/shard_map/all_gather | solution.py:134
  147.1 3.9 %fusion.10 = f32[128,768]{1,0:T(8,128)S(1)} fusion(bf16[4096,768]{1,0:T(8,128)(2,1)} %all-gather.5.cloned.1.call-done, bf16[128,4096]{1,0:T(8,128)(2,1)S(1)} %copy-done, f32[4096]{0:T(1024)S(1)} %copy-done.5, f32[128]{0:T(128)S(1)} %add_sqrt_fusion), kind=kOutput, calls=%fused_computation.20 | convolution fusion | flops 807403520 | bytes 7750144 | tf_op jit(solution)/shard_map/dot_general | solution.py:132
  152.0 3.8 %while.10 = (s32[]{:T(128)}, bf16[4,128,128]{2,1,0:T(8,128)(2,1)S(1)}, bf16[4,128,128]{2,1,0:T(8,128)(2,1)S(1)}, bf16[1152,128]{1,0:T(8,128)(2,1)S(1)}, pred[128...) while((s32[]{:T(128)}, bf16[4,128,128]{2,1,0:T(8,128)(2,1)S(1)}, ...), condition=%wide.region_13.14_spmd, body=%wide.region_10.13_spmd.sunk | while | flops 76693248 | bytes 2574941 | solution.py:172
  152.0 0.3 fusion.61
  152.6 0.3 fusion.63
  152.9 0.3 fusion.61
  153.9 0.3 fusion.61
  154.8 0.3 fusion.61
  155.4 0.3 fusion.63
  155.8 0.7 copy_bitcast_fusion
  156.4 0.8 copy.61
  (65 shorter events, 5.3 us)
Async XLA Ops:
  7.2 27.0 %copy-start.2 = (s32[256,16]{0,1:T(8,128)S(1)}, s32[256,16]{0,1:T(8,128)}, u32[]{:S(2)}) copy-start(s32[256,16]{0,1:T(8,128)} %param.17) | copy-start | bytes 49156
  7.2 60.1 %copy-start.3 = (s32[128]{0:T(128)S(1)}, s32[128]{0:T(128)}, u32[]{:S(2)}) copy-start(s32[128]{0:T(128)} %param.19) | copy-start | bytes 1540
  7.2 60.2 %copy-start.1 = (bf16[64,1,2,16,128]{4,3,2,1,0:T(8,128)(2,1)S(1)}, bf16[64,1,2,16,128]{4,3,2,1,0:T(8,128)(2,1)}, u32[]{:S(2)}) copy-start(bf16[64,1,2,16,128]{4,3,2,1,0:T(8,128)(2,1)} %param.16) | copy-start | bytes 1572868
  7.2 113.5 %all-gather.3.cloned.1.call-start = ((), (), s32[]{:S(2)}) async-start(), calls=%async_computation.2 | async-start | bytes 1179648 | tf_op jit(solution)/shard_map/all_gather | solution.py:122
  7.9 139.2 %all-gather.5.cloned.1.call-start = ((), (), s32[]{:S(2)}) async-start(), calls=%async_computation.3 | async-start | bytes 7077888 | tf_op jit(solution)/shard_map/all_gather | solution.py:134
  52.1 26.0 %all-to-all-start = ((s32[64,1,2]{2,1,0:T(1,128)}), s32[64,1,2]{2,1,0:T(1,128)S(1)}, u32[]{:S(2)}, u32[]{:S(2)}) async-start(s32[64,1,2]{2,1,0:T(1,128)} %bitcast.4), calls=%async_computation | async-start | bytes 65536 | tf_op jit(solution)/shard_map/all_to_all | solution.py:108
  69.1 13.9 %copy-start.4 = (s32[4]{0:T(128)S(1)}, s32[4]{0:T(128)}, u32[]{:S(2)}) copy-start(s32[4]{0:T(128)} %param.18) | copy-start | bytes 52
  78.1 26.7 %all-to-all-start.1 = ((bf16[64,2,4096]{2,1,0:T(2,128)(2,1)}), bf16[64,2,4096]{2,1,0:T(2,128)(2,1)S(1)}, u32[]{:S(2)}, u32[]{:S(2)}) async-start(bf16[64,2,4096]{2,1,0:T(2,128)(2,1)} %reshape.342), calls=%async_computation.1 | async-start | bytes 2097152 | tf_op jit(solution)/shard_map/all_to_all | solution.py:107
  107.7 39.4 %copy-start.5 = (f32[4096]{0:T(1024)S(1)}, f32[4096]{0:T(1024)}, u32[]{:S(2)}) copy-start(f32[4096]{0:T(1024)} %param.12) | copy-start | bytes 49156
  107.7 14.6 %collective-permute-start = (bf16[4,1,2,256,128]{4,3,2,0,1:T(8,128)(2,1)S(1)}, bf16[4,1,2,256,128]{4,3,2,0,1:T(8,128)(2,1)S(1)}, u32[]{:S(2)}, u32[]{:S(2)}) collective-permute-start(bf16[4,1,2,256,128]{4,3,2,0,1:T(8,128)(2,1)S(1)} %bitcast_select_fusion), channel_id=1, source_target_pairs={{0,1},{1,0},{2,3},{3,2},{4,5},{5,4},{6,7},{7,6},{8,9},{9,8},{10,11... | collective-permute-start | bytes 1572872 | tf_op jit(solution)/shard_map/ppermute | solution.py:16
  120.7 26.4 %copy-start = (bf16[128,4096]{1,0:T(8,128)(2,1)S(1)}, bf16[128,4096]{1,0:T(8,128)(2,1)}, u32[]{:S(2)}) copy-start(bf16[128,4096]{1,0:T(8,128)(2,1)} %all-gather.3.cloned.1.call-done) | copy-start | bytes 3145732
Sparse Core Ops, SparseCore 0:
  10.1 34.4 all-gather.2
  46.7 100.3 all-gather.4

commit v3 on v2

--- a/solution.py
+++ b/solution.py
@@ -14,6 +14,21 @@
 
 def from_partner(x, axis, bit):
     return lax.ppermute(x, axis, [(i, i ^ 1 << bit) for i in range(lax.axis_size(axis))])
+
+
+def gather_by_permutes(x, axis, dim):
+    count = lax.axis_size(axis)
+    me = lax.axis_index(axis)
+    pieces = [x] + [
+        lax.ppermute(x, axis, [(i, (i + shift) % count) for i in range(count)])
+        for shift in range(1, count)
+    ]
+    stacked = jnp.stack(pieces[::-1], axis=0)
+    ordered = jnp.roll(stacked, me + 1, axis=0)
+    ordered = jnp.moveaxis(ordered, 0, dim)
+    shape = list(x.shape)
+    shape[dim] *= count
+    return ordered.reshape(shape)
 
 
 def rotate(vectors, position):
@@ -119,38 +134,40 @@
     )
     alive_mask = jnp.arange(max_len, dtype=jnp.int32)[None, :] < lengths[:, None]
     decoded = jnp.where(alive_mask[:, None, None, :, None], decoded, jnp.zeros((), jnp.bfloat16))
-    whole_rows = lax.all_gather(tokens, "mp", axis=1, tiled=True)
+    whole_rows = gather_by_permutes(tokens, "mp", 1)
     normed = normalize(whole_rows, attn_gain)
     rows_here = tokens.shape[0]
     heads_here = q_weight.shape[1] // head_dim
     per_kv = HEADS // KVH
     first_kv = mp_idx * heads_here // per_kv
-    key_cols = lax.dynamic_slice_in_dim(k_weight, first_kv * head_dim, head_dim, 1)
-    value_cols = lax.dynamic_slice_in_dim(v_weight, first_kv * head_dim, head_dim, 1)
+    is_even = mp_idx % 2 == 0
+    kv_weight = jnp.concatenate([k_weight, v_weight], axis=1)
+    own_kv_cols = lax.dynamic_slice_in_dim(
+        kv_weight, (mp_idx % 2) * k_weight.shape[1] + first_kv * head_dim, head_dim, 1
+    )
     q_cols = q_weight.shape[1]
-    joined_cols = jnp.concatenate([q_weight, key_cols, value_cols], axis=1)
+    joined_cols = jnp.concatenate([q_weight, own_kv_cols], axis=1)
     joined_sum = jnp.dot(
         normed,
-        lax.all_gather(
-            lax.all_gather(joined_cols, "gy", axis=0, tiled=True), "gz", axis=0, tiled=True
-        ),
+        lax.all_gather(gather_by_permutes(joined_cols, "gy", 0), "gz", axis=0, tiled=True),
         preferred_element_type=jnp.float32,
     )
     query_sum = joined_sum[:, :q_cols]
-    key_sum = joined_sum[:, q_cols : q_cols + head_dim]
-    value_sum = joined_sum[:, q_cols + head_dim :]
+    kv_sum = joined_sum[:, q_cols:]
     position = token_positions(token_request, lengths, requests_here)
     queries = (
         rotate(query_sum.reshape(rows_here, heads_here, head_dim), position)
         .astype(jnp.bfloat16)
         .transpose(1, 0, 2)
     )
-    new_keys = rotate(key_sum.reshape(rows_here, 1, head_dim), position).astype(jnp.bfloat16)[:, 0]
-    new_values = value_sum.astype(jnp.bfloat16)
+    rotated_kv = rotate(kv_sum.reshape(rows_here, 1, head_dim), position)[:, 0]
+    own_kv = jnp.where(is_even, rotated_kv, kv_sum).astype(jnp.bfloat16)
+    other_kv = from_partner(own_kv, "mp", 0)
+    new_keys = jnp.where(is_even, own_kv, other_kv)
+    new_values = jnp.where(is_even, other_kv, own_kv)
     allowed = build_mask(token_request, lengths, max_len)
     score_scale = head_dim ** (-0.5)
     partner_cache = from_partner(decoded, "mp", 0)
-    is_even = mp_idx % 2 == 0
     layer_zero = jnp.where(is_even, decoded, partner_cache)[:, 0]
     all_keys = jnp.concatenate(
         [layer_zero[:, 0].reshape(requests_here * max_len, head_dim), new_keys], axis=0

time: 165 us -> 219 us (1.33)
  starting transfers between devices: 32.6 us -> 94.3 us
  blocking collectives: 24.5 us -> 0 us
  waiting for transfers between devices: 49.2 us -> 59.7 us
  local copies, waits for them, and re-layouts: 27.2 us -> 31.6 us
    ppermute x0 -> x14, starting transfers between devices: none -> 62.5 us  [gather_by_permutes(): lax.ppermute(x, axis, [(i, (i + shift) % count) for i in range(count)])]
    all_gather x1 -> x0, blocking collectives: 24.5 us -> none  [on_device(): lax.all_gather(joined_cols, 'gy', axis=0, tiled=True)]
    ppermute x0 -> x14, waiting for transfers between devices: none -> 22 us  [gather_by_permutes(): lax.ppermute(x, axis, [(i, (i + shift) % count) for i in range(count)])]
    all_gather x2 -> x1, waiting for transfers between devices: 24.6 us -> 16.9 us  [on_device(): lax.all_gather(gather_by_permutes(joined_cols, 'gy', 0), 'gz', axis=0, ti...]
    ppermute x1 -> x2, starting transfers between devices: 12.6 us -> 7.3 us  [from_partner(): lax.ppermute(x, axis, [(i, i ^ 1 << bit) for i in range(lax.axis_size(axi...]
    all_to_all x1, waiting for transfers between devices: 7.41 us -> 2.59 us  [on_device(): lax.all_to_all(outgoing_slots, GROUP, split_axis=0, concat_axis=0, tiled=...]
    all_to_all x1, starting transfers between devices: 4.74 us -> 9.55 us  [on_device(): lax.all_to_all(outgoing, GROUP, split_axis=0, concat_axis=0, tiled=True)]
    unnamed x16 -> x60, local copies, waits for them, and re-layouts: 1.05 us -> 3.89 us
  transfers between devices with their start and end apart: 5 -> 19, of which waited for: 3 -> 12; matrix products, arithmetic and copies ran while one was open for 20% -> 17% of each run, Pallas kernels for 0% -> 0%
where the time goes in v3:
time: 219 us; the launch traced here: 218 us
  starting transfers between devices  94.3 us (43%)
  waiting for transfers between devices  59.7 us (27%)
  local copies, waits for them, and re-layouts  31.6 us (14%)
  between operations  14.9 us (7%)
  other arithmetic  11.2 us (5%)
  matrix products  6.17 us (3%)
    ppermute x14, starting transfers between devices, gather_by_permutes(): lax.ppermute(x, axis, [(i, (i + shift) % count) for i in range(count)])  62.5 us
    ppermute x14, waiting for transfers between devices, gather_by_permutes(): lax.ppermute(x, axis, [(i, (i + shift) % count) for i in range(count)])  22 us
    all_to_all x1, waiting for transfers between devices, on_device(): lax.all_to_all(outgoing, GROUP, split_axis=0, concat_axis=0, tiled=True)  17.4 us
    all_gather x1, waiting for transfers between devices, on_device(): lax.all_gather(gather_by_permutes(joined_cols, 'gy', 0), 'gz', axis=0, ti...  16.9 us
    scatter x1, local copies, waits for them, and re-layouts, on_device(): jnp.zeros((flat_table.shape[0],), jnp.int32).at[flat_table].set(slot_ids)  15.5 us
    all_to_all x1, starting transfers between devices, on_device(): lax.all_to_all(outgoing_slots, GROUP, split_axis=0, concat_axis=0, tiled=...  15 us
    all_to_all x1, starting transfers between devices, on_device(): lax.all_to_all(outgoing, GROUP, split_axis=0, concat_axis=0, tiled=True)  9.55 us
    ppermute x2, starting transfers between devices, from_partner(): lax.ppermute(x, axis, [(i, i ^ 1 << bit) for i in range(lax.axis_size(axi...  7.3 us
  transfers between devices with their start and end apart: 19, of which 12 were waited for; matrix products, arithmetic and copies ran while one was open for 17% of the time, Pallas kernels for 0%

profile of v3, /device:TPU:1, one launch (start us, length us, event | category | flops | bytes accessed | tf_op | source)
XLA Modules:
  0.0 218.0 jit_solution(7648636929038345513)
XLA Ops:
  8.2 6.8 %collective-permute-start = (bf16[128,512]{0,1:T(8,128)(2,1)S(1)}, bf16[128,512]{0,1:T(8,128)(2,1)S(1)}, u32[]{:S(2)}, u32[]{:S(2)}) collective-permute-start(bf16[128,512]{0,1:T(8,128)(2,1)S(1)} %copy.40), channel_id=1, source_target_pairs={{0,7},{1,0},{2,1},{3,2},{4,3},{5,4},{6,5},{7,6},{8,15},{9,8},{10,9... | collective-permute-start | bytes 393224 | tf_op jit(solution)/shard_map/ppermute | solution.py:23
  15.1 1.9 collective-permute-start.1
  17.0 1.9 collective-permute-start.2
  18.9 5.3 %collective-permute-start.3 = (bf16[128,512]{0,1:T(8,128)(2,1)S(1)}, bf16[128,512]{0,1:T(8,128)(2,1)S(1)}, u32[]{:S(2)}, u32[]{:S(2)}) collective-permute-start(bf16[128,512]{0,1:T(8,128)(2,1)S(1)} %copy.40), channel_id=1, source_target_pairs={{0,4},{1,5},{2,6},{3,7},{4,0},{5,1},{6,2},{7,3},{8,12},{9,13},{10,... | collective-permute-start | bytes 393224 | tf_op jit(solution)/shard_map/ppermute | solution.py:23
  25.9 1.9 collective-permute-start.7
  28.8 15.5 %scatter_custom_fusion = s32[4096]{0:T(1024)S(1)} fusion(s32[4096]{0:T(1024)S(1)} %bitcast.131, s32[4096]{0:T(1024)S(1)} %iota.46, s32[]{:T(128)} %copy.114), kind=kCustom, calls=%fused_computation.114 | custom fusion | bytes 16388 | tf_op jit(solution)/shard_map/scatter | solution.py:98
  44.5 3.8 %collective-permute-start.8 = (bf16[64,640]{1,0:T(8,128)(2,1)S(1)}, bf16[64,640]{1,0:T(8,128)(2,1)S(1)}, u32[]{:S(2)}, u32[]{:S(2)}) collective-permute-start(bf16[64,640]{1,0:T(8,128)(2,1)S(1)} %pad_maximum_fusion.2), channel_id=1, source_target_pairs={{0,48},{8,56},{16,0},{24,8},{32,16},{40,24},{48,32},{56,40},{1,49}... | collective-permute-start | bytes 245768 | tf_op jit(solution)/shard_map/ppermute | solution.py:23
  48.3 2.4 %collective-permute-done.8 = bf16[64,640]{1,0:T(8,128)(2,1)S(1)} collective-permute-done((bf16[64,640]{1,0:T(8,128)(2,1)S(1)}, bf16[64,640]{1,0:T(8,128)(2,1)S(1)}, u32[]{:S(2)}, u32[]{:S(2)}) %collective-permute-start.8) | collective-permute-done | bytes 81952 | tf_op jit(solution)/shard_map/ppermute | solution.py:23
  50.7 4.5 %collective-permute-start.9 = (bf16[64,640]{1,0:T(8,128)(2,1)S(1)}, bf16[64,640]{1,0:T(8,128)(2,1)S(1)}, u32[]{:S(2)}, u32[]{:S(2)}) collective-permute-start(bf16[64,640]{1,0:T(8,128)(2,1)S(1)} %pad_maximum_fusion.2), channel_id=1, source_target_pairs={{0,40},{8,48},{16,56},{24,0},{32,8},{40,16},{48,24},{56,32},{1,41}... | collective-permute-start | bytes 245768 | tf_op jit(solution)/shard_map/ppermute | solution.py:23
  55.2 2.4 %collective-permute-done.9 = bf16[64,640]{1,0:T(8,128)(2,1)S(1)} collective-permute-done((bf16[64,640]{1,0:T(8,128)(2,1)S(1)}, bf16[64,640]{1,0:T(8,128)(2,1)S(1)}, u32[]{:S(2)}, u32[]{:S(2)}) %collective-permute-start.9) | collective-permute-done | bytes 81952 | tf_op jit(solution)/shard_map/ppermute | solution.py:23
  57.7 5.6 %collective-permute-start.10 = (bf16[64,640]{1,0:T(8,128)(2,1)S(1)}, bf16[64,640]{1,0:T(8,128)(2,1)S(1)}, u32[]{:S(2)}, u32[]{:S(2)}) collective-permute-start(bf16[64,640]{1,0:T(8,128)(2,1)S(1)} %pad_maximum_fusion.2), channel_id=1, source_target_pairs={{0,32},{8,40},{16,48},{24,56},{32,0},{40,8},{48,16},{56,24},{1,33}... | collective-permute-start | bytes 245768 | tf_op jit(solution)/shard_map/ppermute | solution.py:23
  63.3 3.5 %collective-permute-done.10 = bf16[64,640]{1,0:T(8,128)(2,1)S(1)} collective-permute-done((bf16[64,640]{1,0:T(8,128)(2,1)S(1)}, bf16[64,640]{1,0:T(8,128)(2,1)S(1)}, u32[]{:S(2)}, u32[]{:S(2)}) %collective-permute-start.10) | collective-permute-done | bytes 81952 | tf_op jit(solution)/shard_map/ppermute | solution.py:23
  66.7 7.1 %collective-permute-start.11 = (bf16[64,640]{1,0:T(8,128)(2,1)S(1)}, bf16[64,640]{1,0:T(8,128)(2,1)S(1)}, u32[]{:S(2)}, u32[]{:S(2)}) collective-permute-start(bf16[64,640]{1,0:T(8,128)(2,1)S(1)} %pad_maximum_fusion.2), channel_id=1, source_target_pairs={{0,24},{8,32},{16,40},{24,48},{32,56},{40,0},{48,8},{56,16},{1,25}... | collective-permute-start | bytes 245768 | tf_op jit(solution)/shard_map/ppermute | solution.py:23
  75.3 7.0 %collective-permute-start.12 = (bf16[64,640]{1,0:T(8,128)(2,1)S(1)}, bf16[64,640]{1,0:T(8,128)(2,1)S(1)}, u32[]{:S(2)}, u32[]{:S(2)}) collective-permute-start(bf16[64,640]{1,0:T(8,128)(2,1)S(1)} %pad_maximum_fusion.2), channel_id=1, source_target_pairs={{0,16},{8,24},{16,32},{24,40},{32,48},{40,56},{48,0},{56,8},{1,17}... | collective-permute-start | bytes 245768 | tf_op jit(solution)/shard_map/ppermute | solution.py:23
  82.3 3.3 %collective-permute-done.12 = bf16[64,640]{1,0:T(8,128)(2,1)S(1)} collective-permute-done((bf16[64,640]{1,0:T(8,128)(2,1)S(1)}, bf16[64,640]{1,0:T(8,128)(2,1)S(1)}, u32[]{:S(2)}, u32[]{:S(2)}) %collective-permute-start.12) | collective-permute-done | bytes 81952 | tf_op jit(solution)/shard_map/ppermute | solution.py:23
  85.7 3.9 %collective-permute-start.13 = (bf16[64,640]{1,0:T(8,128)(2,1)S(1)}, bf16[64,640]{1,0:T(8,128)(2,1)S(1)}, u32[]{:S(2)}, u32[]{:S(2)}) collective-permute-start(bf16[64,640]{1,0:T(8,128)(2,1)S(1)} %pad_maximum_fusion.2), channel_id=1, source_target_pairs={{0,8},{8,16},{16,24},{24,32},{32,40},{40,48},{48,56},{56,0},{1,9},... | collective-permute-start | bytes 245768 | tf_op jit(solution)/shard_map/ppermute | solution.py:23
  89.6 3.9 %collective-permute-done.13 = bf16[64,640]{1,0:T(8,128)(2,1)S(1)} collective-permute-done((bf16[64,640]{1,0:T(8,128)(2,1)S(1)}, bf16[64,640]{1,0:T(8,128)(2,1)S(1)}, u32[]{:S(2)}, u32[]{:S(2)}) %collective-permute-start.13) | collective-permute-done | bytes 81952 | tf_op jit(solution)/shard_map/ppermute | solution.py:23
  93.4 10.0 %collective-permute-start.4 = (bf16[128,512]{0,1:T(8,128)(2,1)S(1)}, bf16[128,512]{0,1:T(8,128)(2,1)S(1)}, u32[]{:S(2)}, u32[]{:S(2)}) collective-permute-start(bf16[128,512]{0,1:T(8,128)(2,1)S(1)} %copy.40), channel_id=1, source_target_pairs={{0,3},{1,4},{2,5},{3,6},{4,7},{5,0},{6,1},{7,2},{8,11},{9,12},{10,... | collective-permute-start | bytes 393224 | tf_op jit(solution)/shard_map/ppermute | solution.py:23
  106.5 15.0 %all-to-all-start = ((s32[64,1,2]{2,1,0:T(1,128)}), s32[64,1,2]{2,1,0:T(1,128)S(1)}, u32[]{:S(2)}, u32[]{:S(2)}) async-start(s32[64,1,2]{2,1,0:T(1,128)} %bitcast.23), calls=%async_computation | async-start | bytes 65536 | tf_op jit(solution)/shard_map/all_to_all | solution.py:123
  122.4 2.5 %compare_select_fusion.2 = s32[1024,1]{0,1:T(1,128)S(1)} fusion(s32[]{:T(128)} %bitcast.31, s32[]{:T(128)} %bitcast.32, s32[]{:T(128)} %bitcast.34, s32[]{:T(128)} %bitcast.33), kind=kLoop, calls=%fused_computation.100 | loop fusion | flops 17408 | bytes 4112 | tf_op jit(solution)/shard_map/gather | solution.py:66
  126.5 1.8 scatter_custom_fusion.2
  129.7 2.6 %all-to-all-done = s32[64,1,2]{2,1,0:T(1,128)S(1)} async-done(((s32[64,1,2]{2,1,0:T(1,128)}), s32[64,1,2]{2,1,0:T(1,128)S(1)}, u32[]{:S(2)}, u32[]{:S(2)}) %all-to-all-start) | async-done | bytes 544 | tf_op jit(solution)/shard_map/all_to_all | solution.py:123
  132.3 9.6 %all-to-all-start.1 = ((bf16[64,2,4096]{2,1,0:T(2,128)(2,1)}), bf16[64,2,4096]{2,1,0:T(2,128)(2,1)S(1)}, u32[]{:S(2)}, u32[]{:S(2)}) async-start(bf16[64,2,4096]{2,1,0:T(2,128)(2,1)} %reshape.336), calls=%async_computation.1 | async-start | bytes 2097152 | tf_op jit(solution)/shard_map/all_to_all | solution.py:122
  143.8 2.6 %collective-permute-start.5 = (bf16[128,512]{0,1:T(8,128)(2,1)S(1)}, bf16[128,512]{0,1:T(8,128)(2,1)S(1)}, u32[]{:S(2)}, u32[]{:S(2)}) collective-permute-start(bf16[128,512]{0,1:T(8,128)(2,1)S(1)} %copy.40), channel_id=1, source_target_pairs={{0,2},{1,3},{2,4},{3,5},{4,6},{5,7},{6,0},{7,1},{8,10},{9,11},{10,... | collective-permute-start | bytes 393224 | tf_op jit(solution)/shard_map/ppermute | solution.py:23
  146.7 5.1 %collective-permute-done.5 = bf16[128,512]{0,1:T(8,128)(2,1)S(1)} collective-permute-done((bf16[128,512]{0,1:T(8,128)(2,1)S(1)}, bf16[128,512]{0,1:T(8,128)(2,1)S(1)}, u32[]{:S(2)}, u32[]{:S(2)}) %collective-permute-start.5) | collective-permute-done | bytes 131104 | tf_op jit(solution)/shard_map/ppermute | solution.py:23
  152.8 17.4 %all-to-all-done.1 = bf16[64,2,4096]{2,1,0:T(2,128)(2,1)S(1)} async-done(((bf16[64,2,4096]{2,1,0:T(2,128)(2,1)}), bf16[64,2,4096]{2,1,0:T(2,128)(2,1)S(1)}, u32[]{:S(2)}, u32[]{:S(2)}) %all-to-all-start.1) | async-done | bytes 1048608 | tf_op jit(solution)/shard_map/all_to_all | solution.py:122
  171.3 2.8 %scatter_custom_fusion.3 = bf16[65,4096]{1,0:T(8,128)(2,1)S(1)} fusion(s32[128]{0:T(128)} %fusion.37, bf16[128,4096]{1,0:T(8,128)(2,1)} %reshape.382, bf16[]{:T(256)} %constant.167.clone.1), kind=kCustom, calls=%fused_computation.31 | custom fusion | bytes 532992 | tf_op jit(solution)/shard_map/scatter | solution.py:129
  174.6 4.4 %collective-permute-start.14 = (bf16[4,1,2,256,128]{4,3,2,0,1:T(8,128)(2,1)S(1)}, bf16[4,1,2,256,128]{4,3,2,0,1:T(8,128)(2,1)S(1)}, u32[]{:S(2)}, u32[]{:S(2)}) collective-permute-start(bf16[4,1,2,256,128]{4,3,2,0,1:T(8,128)(2,1)S(1)} %bitcast_select_fusion), channel_id=1, source_target_pairs={{0,1},{1,0},{2,3},{3,2},{4,5},{5,4},{6,7},{7,6},{8,9},{9,8},{10,11... | collective-permute-start | bytes 1572872 | tf_op jit(solution)/shard_map/ppermute | solution.py:16
  181.2 16.9 %all-gather.2.cloned.1.call-done = bf16[4096,640]{1,0:T(8,128)(2,1)} async-done(((bf16[512,640]{1,0:T(8,128)(2,1)}), bf16[4096,640]{1,0:T(8,128)(2,1)}) %all-gather.2.cloned.1.call-update) | async-done | bytes 5242896 | tf_op jit(solution)/shard_map/all_gather | solution.py:152
  198.2 3.5 %fusion.44 = f32[128,640]{1,0:T(8,128)S(1)} fusion(bf16[128,4096]{0,1:T(8,128)(2,1)S(1)} %fusion.8, bf16[4096,640]{1,0:T(8,128)(2,1)} %all-gather.2.cloned.1.call-done), kind=kOutput, calls=%fused_computation.141 | convolution fusion | flops 671088640 | bytes 6619136 | tf_op jit(solution)/shard_map/dot_general | solution.py:150
  202.2 2.8 %collective-permute-start.15 = (bf16[128,128]{1,0:T(8,128)(2,1)S(1)}, bf16[128,128]{1,0:T(8,128)(2,1)S(1)}, u32[]{:S(2)}, u32[]{:S(2)}) collective-permute-start(bf16[128,128]{1,0:T(8,128)(2,1)S(1)} %fusion.22), channel_id=1, source_target_pairs={{0,1},{1,0},{2,3},{3,2},{4,5},{5,4},{6,7},{7,6},{8,9},{9,8},{10,11... | collective-permute-start | bytes 98312 | tf_op jit(solution)/shard_map/ppermute | solution.py:16
  206.0 3.7 %while.10 = (s32[]{:T(128)}, bf16[4,128,128]{2,1,0:T(8,128)(2,1)S(1)}, bf16[4,128,128]{2,1,0:T(8,128)(2,1)S(1)}, bf16[1152,128]{1,0:T(8,128)(2,1)S(1)}, pred[128...) while((s32[]{:T(128)}, bf16[4,128,128]{2,1,0:T(8,128)(2,1)S(1)}, ...), condition=%wide.region_13.14_spmd, body=%wide.region_10.13_spmd.sunk | while | flops 76693248 | bytes 2574933 | solution.py:189
  (141 shorter events, 25.2 us)
Async XLA Ops:
  7.2 96.3 %copy-start.2 = (bf16[64,512]{1,0:T(8,128)(2,1)S(1)}, bf16[64,512]{1,0:T(8,128)(2,1)}, u32[]{:S(2)}) copy-start(bf16[64,512]{1,0:T(8,128)(2,1)} %param.13) | copy-start | bytes 196612
  7.2 191.0 %all-gather.2.cloned.1.call-start = ((), (), s32[]{:S(2)}) async-start(), calls=%async_computation.2 | async-start | bytes 5898240 | tf_op jit(solution)/shard_map/all_gather | solution.py:152
  8.2 135.5 %collective-permute-start = (bf16[128,512]{0,1:T(8,128)(2,1)S(1)}, bf16[128,512]{0,1:T(8,128)(2,1)S(1)}, u32[]{:S(2)}, u32[]{:S(2)}) collective-permute-start(bf16[128,512]{0,1:T(8,128)(2,1)S(1)} %copy.40), channel_id=1, source_target_pairs={{0,7},{1,0},{2,1},{3,2},{4,3},{5,4},{6,5},{7,6},{8,15},{9,8},{10,9... | collective-permute-start | bytes 393224 | tf_op jit(solution)/shard_map/ppermute | solution.py:23
  15.1 131.3 %collective-permute-start.1 = (bf16[128,512]{0,1:T(8,128)(2,1)S(1)}, bf16[128,512]{0,1:T(8,128)(2,1)S(1)}, u32[]{:S(2)}, u32[]{:S(2)}) collective-permute-start(bf16[128,512]{0,1:T(8,128)(2,1)S(1)} %copy.40), channel_id=1, source_target_pairs={{0,6},{1,7},{2,0},{3,1},{4,2},{5,3},{6,4},{7,5},{8,14},{9,15},{10,... | collective-permute-start | bytes 393224 | tf_op jit(solution)/shard_map/ppermute | solution.py:23
  17.0 129.6 %collective-permute-start.2 = (bf16[128,512]{0,1:T(8,128)(2,1)S(1)}, bf16[128,512]{0,1:T(8,128)(2,1)S(1)}, u32[]{:S(2)}, u32[]{:S(2)}) collective-permute-start(bf16[128,512]{0,1:T(8,128)(2,1)S(1)} %copy.40), channel_id=1, source_target_pairs={{0,5},{1,6},{2,7},{3,0},{4,1},{5,2},{6,3},{7,4},{8,13},{9,14},{10,... | collective-permute-start | bytes 393224 | tf_op jit(solution)/shard_map/ppermute | solution.py:23
  18.9 127.7 %collective-permute-start.3 = (bf16[128,512]{0,1:T(8,128)(2,1)S(1)}, bf16[128,512]{0,1:T(8,128)(2,1)S(1)}, u32[]{:S(2)}, u32[]{:S(2)}) collective-permute-start(bf16[128,512]{0,1:T(8,128)(2,1)S(1)} %copy.40), channel_id=1, source_target_pairs={{0,4},{1,5},{2,6},{3,7},{4,0},{5,1},{6,2},{7,3},{8,12},{9,13},{10,... | collective-permute-start | bytes 393224 | tf_op jit(solution)/shard_map/ppermute | solution.py:23
  25.9 18.6 %collective-permute-start.7 = (bf16[64,640]{1,0:T(8,128)(2,1)S(1)}, bf16[64,640]{1,0:T(8,128)(2,1)S(1)}, u32[]{:S(2)}, u32[]{:S(2)}) collective-permute-start(bf16[64,640]{1,0:T(8,128)(2,1)S(1)} %pad_maximum_fusion.2), channel_id=1, source_target_pairs={{0,56},{8,0},{16,8},{24,16},{32,24},{40,32},{48,40},{56,48},{1,57}... | collective-permute-start | bytes 245768 | tf_op jit(solution)/shard_map/ppermute | solution.py:23
  44.5 6.2 %collective-permute-start.8 = (bf16[64,640]{1,0:T(8,128)(2,1)S(1)}, bf16[64,640]{1,0:T(8,128)(2,1)S(1)}, u32[]{:S(2)}, u32[]{:S(2)}) collective-permute-start(bf16[64,640]{1,0:T(8,128)(2,1)S(1)} %pad_maximum_fusion.2), channel_id=1, source_target_pairs={{0,48},{8,56},{16,0},{24,8},{32,16},{40,24},{48,32},{56,40},{1,49}... | collective-permute-start | bytes 245768 | tf_op jit(solution)/shard_map/ppermute | solution.py:23
  50.7 7.0 %collective-permute-start.9 = (bf16[64,640]{1,0:T(8,128)(2,1)S(1)}, bf16[64,640]{1,0:T(8,128)(2,1)S(1)}, u32[]{:S(2)}, u32[]{:S(2)}) collective-permute-start(bf16[64,640]{1,0:T(8,128)(2,1)S(1)} %pad_maximum_fusion.2), channel_id=1, source_target_pairs={{0,40},{8,48},{16,56},{24,0},{32,8},{40,16},{48,24},{56,32},{1,41}... | collective-permute-start | bytes 245768 | tf_op jit(solution)/shard_map/ppermute | solution.py:23
  57.7 9.1 %collective-permute-start.10 = (bf16[64,640]{1,0:T(8,128)(2,1)S(1)}, bf16[64,640]{1,0:T(8,128)(2,1)S(1)}, u32[]{:S(2)}, u32[]{:S(2)}) collective-permute-start(bf16[64,640]{1,0:T(8,128)(2,1)S(1)} %pad_maximum_fusion.2), channel_id=1, source_target_pairs={{0,32},{8,40},{16,48},{24,56},{32,0},{40,8},{48,16},{56,24},{1,33}... | collective-permute-start | bytes 245768 | tf_op jit(solution)/shard_map/ppermute | solution.py:23
  66.7 8.6 %collective-permute-start.11 = (bf16[64,640]{1,0:T(8,128)(2,1)S(1)}, bf16[64,640]{1,0:T(8,128)(2,1)S(1)}, u32[]{:S(2)}, u32[]{:S(2)}) collective-permute-start(bf16[64,640]{1,0:T(8,128)(2,1)S(1)} %pad_maximum_fusion.2), channel_id=1, source_target_pairs={{0,24},{8,32},{16,40},{24,48},{32,56},{40,0},{48,8},{56,16},{1,25}... | collective-permute-start | bytes 245768 | tf_op jit(solution)/shard_map/ppermute | solution.py:23
  73.9 47.6 %copy-start.6 = (s32[128]{0:T(128)S(1)}, s32[128]{0:T(128)}, u32[]{:S(2)}) copy-start(s32[128]{0:T(128)} %param.19) | copy-start | bytes 1540
  75.3 10.4 %collective-permute-start.12 = (bf16[64,640]{1,0:T(8,128)(2,1)S(1)}, bf16[64,640]{1,0:T(8,128)(2,1)S(1)}, u32[]{:S(2)}, u32[]{:S(2)}) collective-permute-start(bf16[64,640]{1,0:T(8,128)(2,1)S(1)} %pad_maximum_fusion.2), channel_id=1, source_target_pairs={{0,16},{8,24},{16,32},{24,40},{32,48},{40,56},{48,0},{56,8},{1,17}... | collective-permute-start | bytes 245768 | tf_op jit(solution)/shard_map/ppermute | solution.py:23
  82.3 39.5 %copy-start.7 = (s32[4]{0:T(128)S(1)}, s32[4]{0:T(128)}, u32[]{:S(2)}) copy-start(s32[4]{0:T(128)} %param.18) | copy-start | bytes 52
  85.7 7.8 %collective-permute-start.13 = (bf16[64,640]{1,0:T(8,128)(2,1)S(1)}, bf16[64,640]{1,0:T(8,128)(2,1)S(1)}, u32[]{:S(2)}, u32[]{:S(2)}) collective-permute-start(bf16[64,640]{1,0:T(8,128)(2,1)S(1)} %pad_maximum_fusion.2), channel_id=1, source_target_pairs={{0,8},{8,16},{16,24},{24,32},{32,40},{40,48},{48,56},{56,0},{1,9},... | collective-permute-start | bytes 245768 | tf_op jit(solution)/shard_map/ppermute | solution.py:23
  93.4 53.2 %collective-permute-start.4 = (bf16[128,512]{0,1:T(8,128)(2,1)S(1)}, bf16[128,512]{0,1:T(8,128)(2,1)S(1)}, u32[]{:S(2)}, u32[]{:S(2)}) collective-permute-start(bf16[128,512]{0,1:T(8,128)(2,1)S(1)} %copy.40), channel_id=1, source_target_pairs={{0,3},{1,4},{2,5},{3,6},{4,7},{5,0},{6,1},{7,2},{8,11},{9,12},{10,... | collective-permute-start | bytes 393224 | tf_op jit(solution)/shard_map/ppermute | solution.py:23
  103.6 22.9 %copy-start.3 = (bf16[64,1,2,16,128]{4,3,2,1,0:T(8,128)(2,1)S(1)}, bf16[64,1,2,16,128]{4,3,2,1,0:T(8,128)(2,1)}, u32[]{:S(2)}) copy-start(bf16[64,1,2,16,128]{4,3,2,1,0:T(8,128)(2,1)} %param.16) | copy-start | bytes 1572868
  106.5 25.8 %all-to-all-start = ((s32[64,1,2]{2,1,0:T(1,128)}), s32[64,1,2]{2,1,0:T(1,128)S(1)}, u32[]{:S(2)}, u32[]{:S(2)}) async-start(s32[64,1,2]{2,1,0:T(1,128)} %bitcast.23), calls=%async_computation | async-start | bytes 65536 | tf_op jit(solution)/shard_map/all_to_all | solution.py:123
  121.8 4.4 %copy-start.9 = (f32[64]{0:T(128)}, f32[64]{0:T(128)S(1)}, u32[]{:S(2)}) copy-start(f32[64]{0:T(128)S(1)} %negate_power_fusion) | copy-start | bytes 772
  125.8 0.6 copy-start.11
  132.3 37.8 %all-to-all-start.1 = ((bf16[64,2,4096]{2,1,0:T(2,128)(2,1)}), bf16[64,2,4096]{2,1,0:T(2,128)(2,1)S(1)}, u32[]{:S(2)}, u32[]{:S(2)}) async-start(bf16[64,2,4096]{2,1,0:T(2,128)(2,1)} %reshape.336), calls=%async_computation.1 | async-start | bytes 2097152 | tf_op jit(solution)/shard_map/all_to_all | solution.py:122
  143.8 8.0 %collective-permute-start.5 = (bf16[128,512]{0,1:T(8,128)(2,1)S(1)}, bf16[128,512]{0,1:T(8,128)(2,1)S(1)}, u32[]{:S(2)}, u32[]{:S(2)}) collective-permute-start(bf16[128,512]{0,1:T(8,128)(2,1)S(1)} %copy.40), channel_id=1, source_target_pairs={{0,2},{1,3},{2,4},{3,5},{4,6},{5,7},{6,0},{7,1},{8,10},{9,11},{10,... | collective-permute-start | bytes 393224 | tf_op jit(solution)/shard_map/ppermute | solution.py:23
  146.4 5.4 %collective-permute-start.6 = (bf16[128,512]{0,1:T(8,128)(2,1)S(1)}, bf16[128,512]{0,1:T(8,128)(2,1)S(1)}, u32[]{:S(2)}, u32[]{:S(2)}) collective-permute-start(bf16[128,512]{0,1:T(8,128)(2,1)S(1)} %copy.40), channel_id=1, source_target_pairs={{0,1},{1,2},{2,3},{3,4},{4,5},{5,6},{6,7},{7,0},{8,9},{9,10},{10,1... | collective-permute-start | bytes 393224 | tf_op jit(solution)/shard_map/ppermute | solution.py:23
  171.3 3.0 %copy-start.8 = (pred[4,256]{1,0:T(4,128)(4,1)S(1)}, pred[4,256]{1,0:T(4,128)(4,1)}, u32[]{:S(2)}) copy-start(pred[4,256]{1,0:T(4,128)(4,1)} %iota_compare_fusion.3) | copy-start | bytes 3076
  174.2 4.9 %copy-start.5 = (f32[4096]{0:T(1024)S(1)}, f32[4096]{0:T(1024)}, u32[]{:S(2)}) copy-start(f32[4096]{0:T(1024)} %param.12) | copy-start | bytes 49156
  174.6 5.8 %collective-permute-start.14 = (bf16[4,1,2,256,128]{4,3,2,0,1:T(8,128)(2,1)S(1)}, bf16[4,1,2,256,128]{4,3,2,0,1:T(8,128)(2,1)S(1)}, u32[]{:S(2)}, u32[]{:S(2)}) collective-permute-start(bf16[4,1,2,256,128]{4,3,2,0,1:T(8,128)(2,1)S(1)} %bitcast_select_fusion), channel_id=1, source_target_pairs={{0,1},{1,0},{2,3},{3,2},{4,5},{5,4},{6,7},{7,6},{8,9},{9,8},{10,11... | collective-permute-start | bytes 1572872 | tf_op jit(solution)/shard_map/ppermute | solution.py:16
  180.4 0.8 copy-start
  181.2 20.5 %copy-start.10 = (f32[64]{0:T(128)S(1)}, f32[64]{0:T(128)}, u32[]{:S(2)}) copy-start(f32[64]{0:T(128)} %copy-done.9) | copy-start | bytes 772
  181.2 20.5 %copy-start.12 = (f32[128]{0:T(128)S(1)}, f32[128]{0:T(128)}, u32[]{:S(2)}) copy-start(f32[128]{0:T(128)} %copy-done.11) | copy-start | bytes 1540
  202.2 3.8 %copy-start.4 = (bf16[4,128,128]{2,1,0:T(8,128)(2,1)S(1)}, bf16[4,128,128]{2,1,0:T(8,128)(2,1)}, u32[]{:S(2)}) copy-start(bf16[4,128,128]{2,1,0:T(8,128)(2,1)} %custom-call.2) | copy-start | bytes 393220
  202.2 3.7 %collective-permute-start.15 = (bf16[128,128]{1,0:T(8,128)(2,1)S(1)}, bf16[128,128]{1,0:T(8,128)(2,1)S(1)}, u32[]{:S(2)}, u32[]{:S(2)}) collective-permute-start(bf16[128,128]{1,0:T(8,128)(2,1)S(1)} %fusion.22), channel_id=1, source_target_pairs={{0,1},{1,0},{2,3},{3,2},{4,5},{5,4},{6,7},{7,6},{8,9},{9,8},{10,11... | collective-permute-start | bytes 98312 | tf_op jit(solution)/shard_map/ppermute | solution.py:16
  205.9 4.4 %copy-start.1 = (bf16[4,1,2,256,128]{4,3,2,0,1:T(8,128)(2,1)S(1)}, bf16[4,1,2,256,128]{4,3,2,0,1:T(8,128)(2,1)}, u32[]{:S(2)}) copy-start(bf16[4,1,2,256,128]{4,3,2,0,1:T(8,128)(2,1)} %copy-done) | copy-start | bytes 1572868
Sparse Core Ops, SparseCore 0:
  104.8 93.3 all-gather.1

commit v4 on v3

--- a/solution.py
+++ b/solution.py
@@ -16,15 +16,10 @@
     return lax.ppermute(x, axis, [(i, i ^ 1 << bit) for i in range(lax.axis_size(axis))])
 
 
-def gather_by_permutes(x, axis, dim):
+def gather_by_all_to_all(x, axis, dim):
     count = lax.axis_size(axis)
-    me = lax.axis_index(axis)
-    pieces = [x] + [
-        lax.ppermute(x, axis, [(i, (i + shift) % count) for i in range(count)])
-        for shift in range(1, count)
-    ]
-    stacked = jnp.stack(pieces[::-1], axis=0)
-    ordered = jnp.roll(stacked, me + 1, axis=0)
+    spread = jnp.broadcast_to(x[None], (count,) + x.shape)
+    ordered = lax.all_to_all(spread, axis, 0, 0, tiled=True)
     ordered = jnp.moveaxis(ordered, 0, dim)
     shape = list(x.shape)
     shape[dim] *= count
@@ -95,10 +90,11 @@
     capacity = 2 * pool_pages // groups
     flat_table = page_table.reshape(-1)
     slot_ids = jnp.arange(flat_table.shape[0], dtype=jnp.int32)
-    owner_slot = jnp.zeros((flat_table.shape[0],), jnp.int32).at[flat_table].set(slot_ids)
-    held_slots = lax.dynamic_slice_in_dim(owner_slot, group_idx * pool_pages, pool_pages)
+    held_pages = group_idx * pool_pages + jnp.arange(pool_pages, dtype=jnp.int32)
+    held_slots = jnp.sum(
+        jnp.where(flat_table[None, :] == held_pages[:, None], slot_ids[None, :], 0), axis=1
+    )
     target_owner = held_slots // pool_pages
-    slot_local = held_slots % pool_pages
     owner_hits = (target_owner[:, None] == jnp.arange(groups, dtype=jnp.int32)[None, :]).astype(
         jnp.int32
     )
@@ -106,35 +102,29 @@
     buffer_row = target_owner * capacity + order_within
     page_rows = kv_pool.reshape(pool_pages, -1)
     row_width = page_rows.shape[1]
+    buffer_ids = jnp.arange(groups * capacity, dtype=jnp.int32)
+    send_pick = (buffer_ids[:, None] == buffer_row[None, :]).astype(jnp.bfloat16)
     outgoing = (
-        jnp.zeros((groups * capacity, row_width), jnp.bfloat16)
-        .at[buffer_row]
-        .set(page_rows)
+        jnp.dot(send_pick, page_rows, preferred_element_type=jnp.float32)
+        .astype(jnp.bfloat16)
         .reshape(groups, capacity, row_width)
     )
-    outgoing_slots = (
-        jnp.full((groups * capacity,), -1, jnp.int32)
-        .at[buffer_row]
-        .set(slot_local)
-        .reshape(groups, capacity)
-    )
-    arrived, arrived_slots = (
-        lax.all_to_all(outgoing, GROUP, split_axis=0, concat_axis=0, tiled=True),
-        lax.all_to_all(outgoing_slots, GROUP, split_axis=0, concat_axis=0, tiled=True),
-    )
-    landing = jnp.where(arrived_slots < 0, pool_pages, arrived_slots).reshape(-1)
-    placed = (
-        jnp.zeros((pool_pages + 1, row_width), jnp.bfloat16)
-        .at[landing]
-        .set(arrived.reshape(-1, row_width))[:pool_pages]
-    )
+    arrived = lax.all_to_all(outgoing, GROUP, split_axis=0, concat_axis=0, tiled=True)
+    my_pages = lax.dynamic_slice_in_dim(flat_table, group_idx * pool_pages, pool_pages)
+    sender = my_pages // pool_pages
+    earlier_same = (sender[None, :] == sender[:, None]) & (my_pages[None, :] < my_pages[:, None])
+    arrival_row = sender * capacity + jnp.sum(earlier_same.astype(jnp.int32), axis=1)
+    take_pick = (arrival_row[:, None] == buffer_ids[None, :]).astype(jnp.bfloat16)
+    placed = jnp.dot(
+        take_pick, arrived.reshape(-1, row_width), preferred_element_type=jnp.float32
+    ).astype(jnp.bfloat16)
     decoded = placed.reshape(requests_here, slot_count, pair_count, 2, page_len, head_dim)
     decoded = decoded.transpose(0, 2, 3, 1, 4, 5).reshape(
         requests_here, pair_count, 2, max_len, head_dim
     )
     alive_mask = jnp.arange(max_len, dtype=jnp.int32)[None, :] < lengths[:, None]
     decoded = jnp.where(alive_mask[:, None, None, :, None], decoded, jnp.zeros((), jnp.bfloat16))
-    whole_rows = gather_by_permutes(tokens, "mp", 1)
+    whole_rows = gather_by_all_to_all(tokens, "mp", 1)
     normed = normalize(whole_rows, attn_gain)
     rows_here = tokens.shape[0]
     heads_here = q_weight.shape[1] // head_dim
@@ -149,7 +139,7 @@
     joined_cols = jnp.concatenate([q_weight, own_kv_cols], axis=1)
     joined_sum = jnp.dot(
         normed,
-        lax.all_gather(gather_by_permutes(joined_cols, "gy", 0), "gz", axis=0, tiled=True),
+        lax.all_gather(joined_cols, GROUP, axis=0, tiled=True),
         preferred_element_type=jnp.float32,
     )
     query_sum = joined_sum[:, :q_cols]

time: 219 us -> 141 us (0.64)
  starting transfers between devices: 94.3 us -> 34.1 us
  local copies, waits for them, and re-layouts: 31.6 us -> 7.34 us
  waiting for transfers between devices: 59.7 us -> 65.2 us
    ppermute x14 -> x0, starting transfers between devices: 62.5 us -> none  [gather_by_permutes(): lax.ppermute(x, axis, [(i, (i + shift) % count) for i in range(count)])]
    ppermute x14 -> x0, waiting for transfers between devices: 22 us -> none  [gather_by_permutes(): lax.ppermute(x, axis, [(i, (i + shift) % count) for i in range(count)])]
    scatter x4 -> x0, local copies, waits for them, and re-layouts: 20.9 us -> none  [the longest x1 15.5 us: on_device(): jnp.zeros((flat_table.shape[0],), jnp.int32).at[flat_table].set(slot_ids)]
    all_gather x1, waiting for transfers between devices: 16.9 us -> 30.8 us  [on_device(): lax.all_gather(joined_cols, GROUP, axis=0, tiled=True)]
    all_to_all x1, waiting for transfers between devices: 17.4 us -> 25.5 us  [on_device(): lax.all_to_all(outgoing, GROUP, split_axis=0, concat_axis=0, tiled=True)]
    all_to_all x1, waiting for transfers between devices: 2.59 us -> 7.53 us  [gather_by_all_to_all(): ordered = lax.all_to_all(spread, axis, 0, 0, tiled=True)]
    ppermute x2, starting transfers between devices: 7.3 us -> 11.9 us  [from_partner(): lax.ppermute(x, axis, [(i, i ^ 1 << bit) for i in range(lax.axis_size(axi...]
    all_to_all x1, starting transfers between devices: 15 us -> 10.4 us  [gather_by_all_to_all(): ordered = lax.all_to_all(spread, axis, 0, 0, tiled=True)]
  transfers between devices with their start and end apart: 19 -> 5, of which waited for: 12 -> 5; matrix products, arithmetic and copies ran while one was open for 17% -> 10% of each run, Pallas kernels for 0% -> 0%
where the time goes in v4:
time: 141 us
  waiting for transfers between devices  65.2 us (46%)
  starting transfers between devices  34.1 us (24%)
  between operations  14.4 us (10%)
  other arithmetic  11.8 us (8%)
  matrix products  7.56 us (5%)
  local copies, waits for them, and re-layouts  7.34 us (5%)
    all_gather x1, waiting for transfers between devices, on_device(): lax.all_gather(joined_cols, GROUP, axis=0, tiled=True)  30.8 us
    all_to_all x1, waiting for transfers between devices, on_device(): lax.all_to_all(outgoing, GROUP, split_axis=0, concat_axis=0, tiled=True)  25.5 us
    ppermute x2, starting transfers between devices, from_partner(): lax.ppermute(x, axis, [(i, i ^ 1 << bit) for i in range(lax.axis_size(axi...  11.9 us
    all_to_all x1, starting transfers between devices, on_device(): lax.all_to_all(outgoing, GROUP, split_axis=0, concat_axis=0, tiled=True)  11.8 us
    all_to_all x1, starting transfers between devices, gather_by_all_to_all(): ordered = lax.all_to_all(spread, axis, 0, 0, tiled=True)  10.4 us
    all_to_all x1, waiting for transfers between devices, gather_by_all_to_all(): ordered = lax.all_to_all(spread, axis, 0, 0, tiled=True)  7.53 us
    dot_general x1, matrix products, on_device(): jnp.dot(normed, lax.all_gather(joined_cols, GROUP, axis=0, tiled=True), p...  3.5 us
  transfers between devices with their start and end apart: 5, of which 5 were waited for; matrix products, arithmetic and copies ran while one was open for 10% of the time, Pallas kernels for 0%

profile of v4, /device:TPU:1, one launch (start us, length us, event | category | flops | bytes accessed | tf_op | source)
XLA Modules:
  0.0 140.6 jit_solution(239663356987556904)
XLA Ops:
  7.2 0.7 fusion.24
  8.0 1.5 %pad_maximum_fusion.2 = bf16[64,640]{1,0:T(8,128)(2,1)} fusion(bf16[64,128]{1,0:T(8,128)(2,1)S(1)} %fusion.24, bf16[64,512]{1,0:T(8,128)(2,1)} %param.13), kind=kLoop, calls=%fused_computation.41 | loop fusion | flops 163840 | bytes 163840 | tf_op jit(solution)/shard_map/concatenate | solution.py:139
  9.6 1.0 copy.21
  10.6 1.1 broadcast_in_dim.35
  11.7 10.4 %all-to-all-start = ((bf16[8,128,512]{1,2,0:T(8,128)(2,1)}), bf16[8,128,512]{1,2,0:T(8,128)(2,1)S(1)}, u32[]{:S(2)}, u32[]{:S(2)}) async-start(bf16[8,128,512]{1,2,0:T(8,128)(2,1)} %broadcast_in_dim.35), calls=%async_computation | async-start | bytes 2097152 | tf_op jit(solution)/shard_map/all_to_all | solution.py:22
  23.2 0.4 convolution_convert_fusion.1
  23.9 1.5 %reshape.318 = bf16[64,2,4096]{2,1,0:T(2,128)(2,1)} reshape(bf16[128,4096]{1,0:T(8,128)(2,1)S(1)} %convolution_convert_fusion.1) | data formatting | bytes 2097152 | tf_op jit(solution)/shard_map/reshape | solution.py:110
  25.4 0.7 fusion.37
  26.0 2.6 %compare_select_fusion.1 = s32[1024,1]{0,1:T(1,128)S(1)} fusion(s32[]{:T(128)} %bitcast.11, s32[]{:T(128)} %bitcast.12, s32[]{:T(128)} %bitcast.14, s32[]{:T(128)} %bitcast.13), kind=kLoop, calls=%fused_computation.66 | loop fusion | flops 17408 | bytes 4112 | tf_op jit(solution)/shard_map/gather | solution.py:61
  29.0 0.6 iota_compare_fusion.7
  29.6 7.5 %all-to-all-done = bf16[8,128,512]{1,2,0:T(8,128)(2,1)S(1)} async-done(((bf16[8,128,512]{1,2,0:T(8,128)(2,1)}), bf16[8,128,512]{1,2,0:T(8,128)(2,1)S(1)}, u32[]{:S(2)}, u32[]{:S(2)}) %all-to-all-start) | async-done | bytes 1048608 | tf_op jit(solution)/shard_map/all_to_all | solution.py:22
  37.2 11.8 %all-to-all-start.1 = ((bf16[64,2,4096]{2,1,0:T(2,128)(2,1)}), bf16[64,2,4096]{2,1,0:T(2,128)(2,1)S(1)}, u32[]{:S(2)}, u32[]{:S(2)}) async-start(bf16[64,2,4096]{2,1,0:T(2,128)(2,1)} %reshape.318), calls=%async_computation.1 | async-start | bytes 2097152 | tf_op jit(solution)/shard_map/all_to_all | solution.py:112
  49.0 0.5 multiply_add_fusion.1
  50.2 0.6 multiply_reduce_fusion
  50.7 0.6 add_sqrt_fusion
  51.4 25.5 %all-to-all-done.1 = bf16[64,2,4096]{2,1,0:T(2,128)(2,1)S(1)} async-done(((bf16[64,2,4096]{2,1,0:T(2,128)(2,1)}), bf16[64,2,4096]{2,1,0:T(2,128)(2,1)S(1)}, u32[]{:S(2)}, u32[]{:S(2)}) %all-to-all-start.1) | async-done | bytes 1048608 | tf_op jit(solution)/shard_map/all_to_all | solution.py:112
  76.8 0.4 reshape.319
  77.3 0.9 fusion.9
  78.6 5.4 %collective-permute-start = (bf16[4,1,2,256,128]{4,3,2,1,0:T(8,128)(2,1)S(1)}, bf16[4,1,2,256,128]{4,3,2,1,0:T(8,128)(2,1)S(1)}, u32[]{:S(2)}, u32[]{:S(2)}) collective-permute-start(bf16[4,1,2,256,128]{4,3,2,1,0:T(8,128)(2,1)S(1)} %broadcast_select_fusion), channel_id=1, source_target_pairs={{0,1},{1,0},{2,3},{3,2},{4,5},{5,4},{6,7},{7,6},{8,9},{9,8},{10,11... | collective-permute-start | bytes 1572872 | tf_op jit(solution)/shard_map/ppermute | solution.py:16
  84.0 0.7 fusion.8
  84.8 0.8 collective-permute-done
  85.8 30.8 %all-gather.2.cloned.1.call-done = bf16[4096,640]{1,0:T(8,128)(2,1)} async-done(((bf16[64,640]{1,0:T(8,128)(2,1)}), bf16[4096,640]{1,0:T(8,128)(2,1)}) %all-gather.2.cloned.1.call-update) | async-done | bytes 5242896 | tf_op jit(solution)/shard_map/all_gather | solution.py:142
  116.6 3.5 %fusion.38 = f32[128,640]{1,0:T(8,128)S(1)} fusion(bf16[128,4096]{0,1:T(8,128)(2,1)S(1)} %fusion.8, bf16[4096,640]{1,0:T(8,128)(2,1)} %all-gather.2.cloned.1.call-done), kind=kOutput, calls=%fused_computation.104 | convolution fusion | flops 671088640 | bytes 6619136 | tf_op jit(solution)/shard_map/dot_general | solution.py:140
  121.2 6.5 %collective-permute-start.1 = (bf16[128,128]{1,0:T(8,128)(2,1)S(1)}, bf16[128,128]{1,0:T(8,128)(2,1)S(1)}, u32[]{:S(2)}, u32[]{:S(2)}) collective-permute-start(bf16[128,128]{1,0:T(8,128)(2,1)S(1)} %fusion.19), channel_id=1, source_target_pairs={{0,1},{1,0},{2,3},{3,2},{4,5},{5,4},{6,7},{7,6},{8,9},{9,8},{10,11... | collective-permute-start | bytes 98312 | tf_op jit(solution)/shard_map/ppermute | solution.py:16
  127.9 0.6 collective-permute-done.1
  128.6 3.8 %while.10 = (s32[]{:T(128)}, bf16[4,128,128]{2,1,0:T(8,128)(2,1)S(1)}, bf16[4,128,128]{2,1,0:T(8,128)(2,1)S(1)}, bf16[1152,128]{1,0:T(8,128)(2,1)S(1)}, pred[128...) while((s32[]{:T(128)}, bf16[4,128,128]{2,1,0:T(8,128)(2,1)S(1)}, ...), condition=%wide.region_11.12_spmd, body=%wide.region_8.11_spmd.sunk | while | flops 76693248 | bytes 2574941 | solution.py:179
  128.6 0.3 fusion.52
  129.5 0.3 fusion.52
  130.5 0.3 fusion.52
  131.4 0.3 fusion.52
  132.3 0.7 copy_bitcast_fusion
  133.0 0.8 copy.57
  (70 shorter events, 6.5 us)
Async XLA Ops:
  7.2 15.0 %copy-start.2 = (s32[256,16]{0,1:T(8,128)S(1)}, s32[256,16]{0,1:T(8,128)}, u32[]{:S(2)}) copy-start(s32[256,16]{0,1:T(8,128)} %param.17) | copy-start | bytes 49156
  7.2 109.4 %all-gather.2.cloned.1.call-start = ((), (), s32[]{:S(2)}) async-start(), calls=%async_computation.2 | async-start | bytes 5324800 | tf_op jit(solution)/shard_map/all_gather | solution.py:142
  8.0 15.2 %copy-start = (bf16[64,1,2,16,128]{4,3,2,1,0:T(8,128)(2,1)S(1)}, bf16[64,1,2,16,128]{4,3,2,1,0:T(8,128)(2,1)}, u32[]{:S(2)}) copy-start(bf16[64,1,2,16,128]{4,3,2,1,0:T(8,128)(2,1)} %param.16) | copy-start | bytes 1572868
  11.7 11.9 %copy-start.3 = (s32[128]{0:T(128)S(1)}, s32[128]{0:T(128)}, u32[]{:S(2)}) copy-start(s32[128]{0:T(128)} %param.19) | copy-start | bytes 1540
  11.7 25.4 %all-to-all-start = ((bf16[8,128,512]{1,2,0:T(8,128)(2,1)}), bf16[8,128,512]{1,2,0:T(8,128)(2,1)S(1)}, u32[]{:S(2)}, u32[]{:S(2)}) async-start(bf16[8,128,512]{1,2,0:T(8,128)(2,1)} %broadcast_in_dim.35), calls=%async_computation | async-start | bytes 2097152 | tf_op jit(solution)/shard_map/all_to_all | solution.py:22
  22.3 3.1 %copy-start.4 = (s32[4]{0:T(128)S(1)}, s32[4]{0:T(128)}, u32[]{:S(2)}) copy-start(s32[4]{0:T(128)} %param.18) | copy-start | bytes 52
  37.2 39.7 %all-to-all-start.1 = ((bf16[64,2,4096]{2,1,0:T(2,128)(2,1)}), bf16[64,2,4096]{2,1,0:T(2,128)(2,1)S(1)}, u32[]{:S(2)}, u32[]{:S(2)}) async-start(bf16[64,2,4096]{2,1,0:T(2,128)(2,1)} %reshape.318), calls=%async_computation.1 | async-start | bytes 2097152 | tf_op jit(solution)/shard_map/all_to_all | solution.py:112
  49.0 2.4 %copy-start.6 = (f32[64]{0:T(128)}, f32[64]{0:T(128)S(1)}, u32[]{:S(2)}) copy-start(f32[64]{0:T(128)S(1)} %negate_power_fusion) | copy-start | bytes 772
  49.5 0.5 copy-start.8
  77.3 1.1 copy-start.5
  77.3 6.7 %copy-start.1 = (f32[4096]{0:T(1024)S(1)}, f32[4096]{0:T(1024)}, u32[]{:S(2)}) copy-start(f32[4096]{0:T(1024)} %param.12) | copy-start | bytes 49156
  77.3 6.7 %copy-start.10 = (f32[128]{0:T(128)S(1)}, f32[128]{0:T(128)}, u32[]{:S(2)}) copy-start(f32[128]{0:T(128)} %add_sqrt_fusion) | copy-start | bytes 1540
  78.6 6.9 %collective-permute-start = (bf16[4,1,2,256,128]{4,3,2,1,0:T(8,128)(2,1)S(1)}, bf16[4,1,2,256,128]{4,3,2,1,0:T(8,128)(2,1)S(1)}, u32[]{:S(2)}, u32[]{:S(2)}) collective-permute-start(bf16[4,1,2,256,128]{4,3,2,1,0:T(8,128)(2,1)S(1)} %broadcast_select_fusion), channel_id=1, source_target_pairs={{0,1},{1,0},{2,3},{3,2},{4,5},{5,4},{6,7},{7,6},{8,9},{9,8},{10,11... | collective-permute-start | bytes 1572872 | tf_op jit(solution)/shard_map/ppermute | solution.py:16
  120.1 0.7 copy-start.7
  120.1 0.7 copy-start.9
  121.2 7.3 %collective-permute-start.1 = (bf16[128,128]{1,0:T(8,128)(2,1)S(1)}, bf16[128,128]{1,0:T(8,128)(2,1)S(1)}, u32[]{:S(2)}, u32[]{:S(2)}) collective-permute-start(bf16[128,128]{1,0:T(8,128)(2,1)S(1)} %fusion.19), channel_id=1, source_target_pairs={{0,1},{1,0},{2,3},{3,2},{4,5},{5,4},{6,7},{7,6},{8,9},{9,8},{10,11... | collective-permute-start | bytes 98312 | tf_op jit(solution)/shard_map/ppermute | solution.py:16
Sparse Core Ops, SparseCore 0:
  11.6 104.9 all-gather.1

commit v5 on v4

--- a/solution.py
+++ b/solution.py
@@ -145,10 +145,8 @@
     query_sum = joined_sum[:, :q_cols]
     kv_sum = joined_sum[:, q_cols:]
     position = token_positions(token_request, lengths, requests_here)
-    queries = (
-        rotate(query_sum.reshape(rows_here, heads_here, head_dim), position)
-        .astype(jnp.bfloat16)
-        .transpose(1, 0, 2)
+    queries = rotate(query_sum.reshape(rows_here, heads_here, head_dim), position).astype(
+        jnp.bfloat16
     )
     rotated_kv = rotate(kv_sum.reshape(rows_here, 1, head_dim), position)[:, 0]
     own_kv = jnp.where(is_even, rotated_kv, kv_sum).astype(jnp.bfloat16)
@@ -166,18 +164,15 @@
         [layer_zero[:, 1].reshape(requests_here * max_len, head_dim), new_values], axis=0
     )
 
-    def attend(query_one):
-        scores = (
-            jnp.einsum("td,nd->tn", query_one, all_keys, preferred_element_type=jnp.float32)
-            * score_scale
-        )
-        attn_probs = weigh(scores, allowed)
-        return jnp.dot(attn_probs, all_values, preferred_element_type=jnp.float32).astype(
-            jnp.bfloat16
-        )
-
-    heads_out = lax.map(attend, queries)
-    attention = heads_out.transpose(1, 0, 2).reshape(rows_here, heads_here * head_dim)
+    scores = (
+        jnp.einsum("thd,nd->thn", queries, all_keys, preferred_element_type=jnp.float32)
+        * score_scale
+    )
+    attn_probs = weigh(scores, allowed[:, None, :])
+    heads_out = jnp.einsum(
+        "thn,nd->thd", attn_probs, all_values, preferred_element_type=jnp.float32
+    ).astype(jnp.bfloat16)
+    attention = heads_out.reshape(rows_here, heads_here * head_dim)
     return (attention, partner_cache)
 
 

time: 141 us -> 140 us (level)
  other arithmetic: 11.8 us -> 9.02 us
  waiting for transfers between devices: 65.2 us -> 67.4 us
  transfers between devices with their start and end apart: 5 -> 5, of which waited for: 5 -> 5; matrix products, arithmetic and copies ran while one was open for 10% -> 9% of each run, Pallas kernels for 0% -> 0%
where the time goes in v5:
time: 140 us; the launch traced here: 139 us
  waiting for transfers between devices  67.4 us (48%)
  starting transfers between devices  34.1 us (24%)
  between operations  14.4 us (10%)
  other arithmetic  9.02 us (6%)
  local copies, waits for them, and re-layouts  7.25 us (5%)
  matrix products  6.98 us (5%)
    all_gather x1, waiting for transfers between devices, on_device(): lax.all_gather(joined_cols, GROUP, axis=0, tiled=True)  31.2 us
    all_to_all x1, waiting for transfers between devices, on_device(): lax.all_to_all(outgoing, GROUP, split_axis=0, concat_axis=0, tiled=True)  26.7 us
    ppermute x2, starting transfers between devices, from_partner(): lax.ppermute(x, axis, [(i, i ^ 1 << bit) for i in range(lax.axis_size(axi...  11.9 us
    all_to_all x1, starting transfers between devices, on_device(): lax.all_to_all(outgoing, GROUP, split_axis=0, concat_axis=0, tiled=True)  11.8 us
    all_to_all x1, starting transfers between devices, gather_by_all_to_all(): ordered = lax.all_to_all(spread, axis, 0, 0, tiled=True)  10.4 us
    all_to_all x1, waiting for transfers between devices, gather_by_all_to_all(): ordered = lax.all_to_all(spread, axis, 0, 0, tiled=True)  8.17 us
    dot_general x1, matrix products, on_device(): jnp.dot(normed, lax.all_gather(joined_cols, GROUP, axis=0, tiled=True), p...  3.51 us
  transfers between devices with their start and end apart: 5, of which 5 were waited for; matrix products, arithmetic and copies ran while one was open for 9% of the time, Pallas kernels for 0%

profile of v5, /device:TPU:1, one launch (start us, length us, event | category | flops | bytes accessed | tf_op | source)
XLA Modules:
  0.0 139.1 jit_solution(6100696128546786113)
XLA Ops:
  7.3 0.8 fusion.27
  8.1 1.5 %pad_maximum_fusion.1 = bf16[64,640]{1,0:T(8,128)(2,1)} fusion(bf16[64,128]{1,0:T(8,128)(2,1)S(1)} %fusion.27, bf16[64,512]{1,0:T(8,128)(2,1)} %param.11), kind=kLoop, calls=%fused_computation.41 | loop fusion | flops 163840 | bytes 163840 | tf_op jit(solution)/shard_map/concatenate | solution.py:139
  9.6 1.0 copy.25
  10.6 1.2 broadcast_in_dim.35
  11.8 10.4 %all-to-all-start = ((bf16[8,128,512]{1,2,0:T(8,128)(2,1)}), bf16[8,128,512]{1,2,0:T(8,128)(2,1)S(1)}, u32[]{:S(2)}, u32[]{:S(2)}) async-start(bf16[8,128,512]{1,2,0:T(8,128)(2,1)} %broadcast_in_dim.35), calls=%async_computation | async-start | bytes 2097152 | tf_op jit(solution)/shard_map/all_to_all | solution.py:22
  22.4 0.3 select_reduce_fusion
  23.2 0.4 convolution_convert_fusion
  23.9 1.5 %reshape.319 = bf16[64,2,4096]{2,1,0:T(2,128)(2,1)} reshape(bf16[128,4096]{1,0:T(8,128)(2,1)S(1)} %convolution_convert_fusion) | data formatting | bytes 2097152 | tf_op jit(solution)/shard_map/reshape | solution.py:110
  25.4 0.6 fusion.53
  26.0 2.5 %compare_select_fusion.1 = s32[1024,1]{0,1:T(1,128)S(1)} fusion(s32[]{:T(128)} %bitcast, s32[]{:T(128)} %bitcast.1, s32[]{:T(128)} %bitcast.3, s32[]{:T(128)} %bitcast.2), kind=kLoop, calls=%fused_computation.66 | loop fusion | flops 17408 | bytes 4112 | tf_op jit(solution)/shard_map/gather | solution.py:61
  29.0 8.2 %all-to-all-done = bf16[8,128,512]{1,2,0:T(8,128)(2,1)S(1)} async-done(((bf16[8,128,512]{1,2,0:T(8,128)(2,1)}), bf16[8,128,512]{1,2,0:T(8,128)(2,1)S(1)}, u32[]{:S(2)}, u32[]{:S(2)}) %all-to-all-start) | async-done | bytes 1048608 | tf_op jit(solution)/shard_map/all_to_all | solution.py:22
  37.2 11.8 %all-to-all-start.1 = ((bf16[64,2,4096]{2,1,0:T(2,128)(2,1)}), bf16[64,2,4096]{2,1,0:T(2,128)(2,1)S(1)}, u32[]{:S(2)}, u32[]{:S(2)}) async-start(bf16[64,2,4096]{2,1,0:T(2,128)(2,1)} %reshape.319), calls=%async_computation.1 | async-start | bytes 2097152 | tf_op jit(solution)/shard_map/all_to_all | solution.py:112
  49.1 0.3 multiply_cosine_fusion.1
  49.6 0.6 multiply_reduce_fusion
  50.2 26.7 %all-to-all-done.1 = bf16[64,2,4096]{2,1,0:T(2,128)(2,1)S(1)} async-done(((bf16[64,2,4096]{2,1,0:T(2,128)(2,1)}), bf16[64,2,4096]{2,1,0:T(2,128)(2,1)S(1)}, u32[]{:S(2)}, u32[]{:S(2)}) %all-to-all-start.1) | async-done | bytes 1048608 | tf_op jit(solution)/shard_map/all_to_all | solution.py:112
  76.8 0.4 reshape.320
  77.3 0.4 fusion.6
  77.8 0.2 broadcast_select_fusion
  78.0 5.4 %collective-permute-start = (bf16[4,1,2,256,128]{4,3,2,1,0:T(8,128)(2,1)S(1)}, bf16[4,1,2,256,128]{4,3,2,1,0:T(8,128)(2,1)S(1)}, u32[]{:S(2)}, u32[]{:S(2)}) collective-permute-start(bf16[4,1,2,256,128]{4,3,2,1,0:T(8,128)(2,1)S(1)} %broadcast_select_fusion), channel_id=1, source_target_pairs={{0,1},{1,0},{2,3},{3,2},{4,5},{5,4},{6,7},{7,6},{8,9},{9,8},{10,11... | collective-permute-start | bytes 1572872 | tf_op jit(solution)/shard_map/ppermute | solution.py:16
  83.4 0.7 fusion.5
  84.1 0.8 collective-permute-done
  84.9 0.2 select_bitcast_fusion
  85.3 31.2 %all-gather.2.cloned.1.call-done = bf16[4096,640]{1,0:T(8,128)(2,1)} async-done(((bf16[64,640]{1,0:T(8,128)(2,1)}), bf16[4096,640]{1,0:T(8,128)(2,1)}) %all-gather.2.cloned.1.call-update) | async-done | bytes 5242896 | tf_op jit(solution)/shard_map/all_gather | solution.py:142
  116.6 3.5 %fusion.55 = f32[128,640]{1,0:T(8,128)S(1)} fusion(bf16[128,4096]{0,1:T(8,128)(2,1)S(1)} %fusion.5, bf16[4096,640]{1,0:T(8,128)(2,1)} %all-gather.2.cloned.1.call-done), kind=kOutput, calls=%fused_computation.113 | convolution fusion | flops 671088640 | bytes 6619136 | tf_op jit(solution)/shard_map/dot_general | solution.py:140
  120.1 0.3 fusion.19
  120.5 6.5 %collective-permute-start.1 = (bf16[128,128]{1,0:T(8,128)(2,1)S(1)}, bf16[128,128]{1,0:T(8,128)(2,1)S(1)}, u32[]{:S(2)}, u32[]{:S(2)}) collective-permute-start(bf16[128,128]{1,0:T(8,128)(2,1)S(1)} %fusion.22), channel_id=1, source_target_pairs={{0,1},{1,0},{2,3},{3,2},{4,5},{5,4},{6,7},{7,6},{8,9},{9,8},{10,11... | collective-permute-start | bytes 98312 | tf_op jit(solution)/shard_map/ppermute | solution.py:16
  127.1 0.2 fusion.52
  127.4 0.5 collective-permute-done.1
  128.0 1.1 fusion.54
  129.1 1.6 %fusion.8 = bf16[128,4,128]{0,2,1:T(8,128)(2,1)S(1)} fusion(f32[128,4]{0,1:T(4,128)S(1)} %fusion.54, bf16[128,128]{0,1:T(8,128)(2,1)S(1)} %copy.31, bf16[1024,128]{0,1:T(8,128)(2,1)S(1)} %copy.33, pred[128,1152]{1,0:T(8,128)(4,1)S(1)} %pad_add_fusion, bf16[128,128]{1,0:T(8,128)(2,1)S(1)} %get-tuple-element.21, bf16[1024,128]{1,0:T(8,128)(2,1)S(1)} %bitcast.64, ...), kind=kOutput, calls=%fused_computation.14 | convolution fusion | flops 306448000 | bytes 1001472 | tf_op jit(solution)/shard_map/thn,nd->thd/dot_general | solution.py:172
  130.7 0.8 copy.32
  131.5 0.8 copy.47
  (45 shorter events, 2.4 us)
Async XLA Ops:
  7.2 15.0 %copy-start.2 = (s32[256,16]{0,1:T(8,128)S(1)}, s32[256,16]{0,1:T(8,128)}, u32[]{:S(2)}) copy-start(s32[256,16]{0,1:T(8,128)} %param.15) | copy-start | bytes 49156
  7.2 16.0 %copy-start = (bf16[64,1,2,16,128]{4,3,2,1,0:T(8,128)(2,1)S(1)}, bf16[64,1,2,16,128]{4,3,2,1,0:T(8,128)(2,1)}, u32[]{:S(2)}) copy-start(bf16[64,1,2,16,128]{4,3,2,1,0:T(8,128)(2,1)} %param.14) | copy-start | bytes 1572868
  7.2 109.4 %all-gather.2.cloned.1.call-start = ((), (), s32[]{:S(2)}) async-start(), calls=%async_computation.2 | async-start | bytes 5324800 | tf_op jit(solution)/shard_map/all_gather | solution.py:142
  11.8 11.9 %copy-start.3 = (s32[128]{0:T(128)S(1)}, s32[128]{0:T(128)}, u32[]{:S(2)}) copy-start(s32[128]{0:T(128)} %param.17) | copy-start | bytes 1540
  11.8 25.4 %all-to-all-start = ((bf16[8,128,512]{1,2,0:T(8,128)(2,1)}), bf16[8,128,512]{1,2,0:T(8,128)(2,1)S(1)}, u32[]{:S(2)}, u32[]{:S(2)}) async-start(bf16[8,128,512]{1,2,0:T(8,128)(2,1)} %broadcast_in_dim.35), calls=%async_computation | async-start | bytes 2097152 | tf_op jit(solution)/shard_map/all_to_all | solution.py:22
  22.2 3.2 %copy-start.4 = (s32[4]{0:T(128)S(1)}, s32[4]{0:T(128)}, u32[]{:S(2)}) copy-start(s32[4]{0:T(128)} %param.16) | copy-start | bytes 52
  37.2 39.7 %all-to-all-start.1 = ((bf16[64,2,4096]{2,1,0:T(2,128)(2,1)}), bf16[64,2,4096]{2,1,0:T(2,128)(2,1)S(1)}, u32[]{:S(2)}, u32[]{:S(2)}) async-start(bf16[64,2,4096]{2,1,0:T(2,128)(2,1)} %reshape.319), calls=%async_computation.1 | async-start | bytes 2097152 | tf_op jit(solution)/shard_map/all_to_all | solution.py:112
  77.3 6.1 %copy-start.1 = (f32[4096]{0:T(1024)S(1)}, f32[4096]{0:T(1024)}, u32[]{:S(2)}) copy-start(f32[4096]{0:T(1024)} %param.10) | copy-start | bytes 49156
  78.0 6.9 %collective-permute-start = (bf16[4,1,2,256,128]{4,3,2,1,0:T(8,128)(2,1)S(1)}, bf16[4,1,2,256,128]{4,3,2,1,0:T(8,128)(2,1)S(1)}, u32[]{:S(2)}, u32[]{:S(2)}) collective-permute-start(bf16[4,1,2,256,128]{4,3,2,1,0:T(8,128)(2,1)S(1)} %broadcast_select_fusion), channel_id=1, source_target_pairs={{0,1},{1,0},{2,3},{3,2},{4,5},{5,4},{6,7},{7,6},{8,9},{9,8},{10,11... | collective-permute-start | bytes 1572872 | tf_op jit(solution)/shard_map/ppermute | solution.py:16
  120.5 7.3 %collective-permute-start.1 = (bf16[128,128]{1,0:T(8,128)(2,1)S(1)}, bf16[128,128]{1,0:T(8,128)(2,1)S(1)}, u32[]{:S(2)}, u32[]{:S(2)}) collective-permute-start(bf16[128,128]{1,0:T(8,128)(2,1)S(1)} %fusion.22), channel_id=1, source_target_pairs={{0,1},{1,0},{2,3},{3,2},{4,5},{5,4},{6,7},{7,6},{8,9},{9,8},{10,11... | collective-permute-start | bytes 98312 | tf_op jit(solution)/shard_map/ppermute | solution.py:16
Sparse Core Ops, SparseCore 0:
  11.6 104.9 all-gather.1

commit v6 on v5

--- a/solution.py
+++ b/solution.py
@@ -137,11 +137,14 @@
     )
     q_cols = q_weight.shape[1]
     joined_cols = jnp.concatenate([q_weight, own_kv_cols], axis=1)
-    joined_sum = jnp.dot(
-        normed,
-        lax.all_gather(joined_cols, GROUP, axis=0, tiled=True),
-        preferred_element_type=jnp.float32,
-    )
+    near_rows = lax.all_gather(joined_cols, "gy", axis=0, tiled=True)
+    far = lax.axis_size("gz")
+    feature_blocks = normed.reshape(rows_here, far, near_rows.shape[0]).transpose(1, 0, 2)
+    arrived_rows = lax.all_to_all(feature_blocks, "gz", 0, 0, tiled=True)
+    partial_sums = jnp.einsum(
+        "ztf,fc->ztc", arrived_rows, near_rows, preferred_element_type=jnp.float32
+    )
+    joined_sum = lax.psum_scatter(partial_sums, "gz", scatter_dimension=0, tiled=True)[0]
     query_sum = joined_sum[:, :q_cols]
     kv_sum = joined_sum[:, q_cols:]
     position = token_positions(token_request, lengths, requests_here)

time: 140 us -> 158 us (1.13)
  blocking collectives: 0 us -> 22.4 us
  waiting for transfers between devices: 67.4 us -> 60.1 us
  starting transfers between devices: 34.1 us -> 37.1 us
  local copies, waits for them, and re-layouts: 7.25 us -> 9.55 us
    all_gather x1 -> x0, waiting for transfers between devices: 31.2 us -> none  [on_device(): lax.all_gather(joined_cols, GROUP, axis=0, tiled=True)]
    all_gather x0 -> x1, blocking collectives: none -> 22.4 us  [on_device(): near_rows = lax.all_gather(joined_cols, 'gy', axis=0, tiled=True)]
    reduce_scatter x0 -> x1, waiting for transfers between devices: none -> 15.5 us  [on_device(): lax.psum_scatter(partial_sums, 'gz', scatter_dimension=0, tiled=True)[0]]
    all_to_all x1, waiting for transfers between devices: 8.17 us -> 15 us  [gather_by_all_to_all(): ordered = lax.all_to_all(spread, axis, 0, 0, tiled=True)]
    all_to_all x0 -> x1, waiting for transfers between devices: none -> 6.62 us  [on_device(): arrived_rows = lax.all_to_all(feature_blocks, 'gz', 0, 0, tiled=True)]
    all_to_all x1, waiting for transfers between devices: 26.7 us -> 20.9 us  [on_device(): lax.all_to_all(outgoing, GROUP, split_axis=0, concat_axis=0, tiled=True)]
    all_to_all x0 -> x1, starting transfers between devices: none -> 5.5 us  [on_device(): arrived_rows = lax.all_to_all(feature_blocks, 'gz', 0, 0, tiled=True)]
    all_to_all x1, starting transfers between devices: 11.8 us -> 7.82 us  [on_device(): lax.all_to_all(outgoing, GROUP, split_axis=0, concat_axis=0, tiled=True)]
  transfers between devices with their start and end apart: 5 -> 6, of which waited for: 5 -> 6; matrix products, arithmetic and copies ran while one was open for 9% -> 6% of each run, Pallas kernels for 0% -> 0%
where the time goes in v6:
time: 158 us; the launch traced here: 157 us
  waiting for transfers between devices  60.1 us (38%)
  starting transfers between devices  37.1 us (23%)
  blocking collectives  22.4 us (14%)
  between operations  14.4 us (9%)
  local copies, waits for them, and re-layouts  9.55 us (6%)
  other arithmetic  7.89 us (5%)
  matrix products  5.96 us (4%)
    all_gather x1, blocking collectives, on_device(): near_rows = lax.all_gather(joined_cols, 'gy', axis=0, tiled=True)  22.4 us
    all_to_all x1, waiting for transfers between devices, on_device(): lax.all_to_all(outgoing, GROUP, split_axis=0, concat_axis=0, tiled=True)  20.9 us
    reduce_scatter x1, waiting for transfers between devices, on_device(): lax.psum_scatter(partial_sums, 'gz', scatter_dimension=0, tiled=True)[0]  15.5 us
    all_to_all x1, waiting for transfers between devices, gather_by_all_to_all(): ordered = lax.all_to_all(spread, axis, 0, 0, tiled=True)  15 us
    ppermute x2, starting transfers between devices, from_partner(): lax.ppermute(x, axis, [(i, i ^ 1 << bit) for i in range(lax.axis_size(axi...  13.4 us
    all_to_all x1, starting transfers between devices, gather_by_all_to_all(): ordered = lax.all_to_all(spread, axis, 0, 0, tiled=True)  10.3 us
    all_to_all x1, starting transfers between devices, on_device(): lax.all_to_all(outgoing, GROUP, split_axis=0, concat_axis=0, tiled=True)  7.82 us
    all_to_all x1, waiting for transfers between devices, on_device(): arrived_rows = lax.all_to_all(feature_blocks, 'gz', 0, 0, tiled=True)  6.62 us
  transfers between devices with their start and end apart: 6, of which 6 were waited for; matrix products, arithmetic and copies ran while one was open for 6% of the time, Pallas kernels for 0%

profile of v6, /device:TPU:1, one launch (start us, length us, event | category | flops | bytes accessed | tf_op | source)
XLA Modules:
  0.0 157.4 jit_solution(13533860644982790277)
XLA Ops:
  7.2 2.0 %broadcast_in_dim.35 = bf16[8,128,512]{2,1,0:T(8,128)(2,1)} broadcast(bf16[128,512]{1,0:T(8,128)(2,1)} %param.9), dimensions={1,2} | broadcast | bytes 1179648 | tf_op jit(solution)/shard_map/broadcast_in_dim | solution.py:21
  9.2 10.3 %all-to-all-start = ((bf16[8,128,512]{2,1,0:T(8,128)(2,1)}), bf16[8,128,512]{2,1,0:T(8,128)(2,1)S(1)}, u32[]{:S(2)}, u32[]{:S(2)}) async-start(bf16[8,128,512]{2,1,0:T(8,128)(2,1)} %broadcast_in_dim.35), calls=%async_computation | async-start | bytes 2097152 | tf_op jit(solution)/shard_map/all_to_all | solution.py:22
  19.5 15.0 %all-to-all-done = bf16[8,128,512]{2,1,0:T(8,128)(2,1)S(1)} async-done(((bf16[8,128,512]{2,1,0:T(8,128)(2,1)}), bf16[8,128,512]{2,1,0:T(8,128)(2,1)S(1)}, u32[]{:S(2)}, u32[]{:S(2)}) %all-to-all-start) | async-done | bytes 1048608 | tf_op jit(solution)/shard_map/all_to_all | solution.py:22
  34.8 1.3 fusion.6
  36.1 5.5 %all-to-all-start.1 = ((bf16[8,128,512]{2,1,0:T(8,128)(2,1)}), bf16[8,128,512]{2,1,0:T(8,128)(2,1)S(1)}, u32[]{:S(2)}, u32[]{:S(2)}) async-start(bf16[8,128,512]{2,1,0:T(8,128)(2,1)} %fusion.6), calls=%async_computation.1 | async-start | bytes 2097152 | tf_op jit(solution)/shard_map/all_to_all | solution.py:143
  41.7 22.4 %all_gather.3 = bf16[512,640]{1,0:T(8,128)(2,1)S(1)} all-gather(bf16[64,640]{1,0:T(8,128)(2,1)S(1)} %pad_maximum_fusion.1), channel_id=1, replica_groups=mesh['gz'=8,'gy'=8,'mp'=8] {'gy'}, dimensions={0}, use_global_device_ids=true | all-gather | bytes 737280 | tf_op jit(solution)/shard_map/all_gather | solution.py:140
  64.2 6.6 %all-to-all-done.1 = bf16[8,128,512]{2,1,0:T(8,128)(2,1)S(1)} async-done(((bf16[8,128,512]{2,1,0:T(8,128)(2,1)}), bf16[8,128,512]{2,1,0:T(8,128)(2,1)S(1)}, u32[]{:S(2)}, u32[]{:S(2)}) %all-to-all-start.1) | async-done | bytes 1048608 | tf_op jit(solution)/shard_map/all_to_all | solution.py:143
  70.8 2.5 %fusion.10 = f32[8,128,640]{2,1,0:T(8,128)} fusion(bf16[8,128,512]{2,1,0:T(8,128)(2,1)S(1)} %all-to-all-done.1, bf16[512,640]{1,0:T(8,128)(2,1)S(1)} %all_gather.3), kind=kOutput, calls=%fused_computation.17 | convolution fusion | flops 671088640 | bytes 4325376 | tf_op jit(solution)/shard_map/ztf,fc->ztc/dot_general | solution.py:144
  73.3 0.7 copy-done.4
  74.2 0.3 select_reduce_fusion
  75.0 0.4 convolution_convert_fusion
  75.4 1.5 reshape.328
  76.9 7.8 %all-to-all-start.2 = ((bf16[64,2,4096]{2,1,0:T(2,128)(2,1)}), bf16[64,2,4096]{2,1,0:T(2,128)(2,1)S(1)}, u32[]{:S(2)}, u32[]{:S(2)}) async-start(bf16[64,2,4096]{2,1,0:T(2,128)(2,1)} %reshape.328), calls=%async_computation.3 | async-start | bytes 2097152 | tf_op jit(solution)/shard_map/all_to_all | solution.py:112
  85.1 0.6 fusion.56
  85.7 2.5 %compare_select_fusion.1 = s32[1024,1]{0,1:T(1,128)S(1)} fusion(s32[]{:T(128)} %bitcast, s32[]{:T(128)} %bitcast.1, s32[]{:T(128)} %bitcast.3, s32[]{:T(128)} %bitcast.2), kind=kLoop, calls=%fused_computation.69 | loop fusion | flops 17408 | bytes 4112 | tf_op jit(solution)/shard_map/gather | solution.py:61
  88.7 0.3 multiply_cosine_fusion.1
  89.1 20.9 %all-to-all-done.2 = bf16[64,2,4096]{2,1,0:T(2,128)(2,1)S(1)} async-done(((bf16[64,2,4096]{2,1,0:T(2,128)(2,1)}), bf16[64,2,4096]{2,1,0:T(2,128)(2,1)S(1)}, u32[]{:S(2)}, u32[]{:S(2)}) %all-to-all-start.2) | async-done | bytes 1048608 | tf_op jit(solution)/shard_map/all_to_all | solution.py:112
  109.9 0.4 reshape.329
  110.3 0.4 fusion.7
  111.1 7.6 %collective-permute-start = (bf16[4,1,2,256,128]{4,3,2,1,0:T(8,128)(2,1)S(1)}, bf16[4,1,2,256,128]{4,3,2,1,0:T(8,128)(2,1)S(1)}, u32[]{:S(2)}, u32[]{:S(2)}) collective-permute-start(bf16[4,1,2,256,128]{4,3,2,1,0:T(8,128)(2,1)S(1)} %broadcast_select_fusion), channel_id=1, source_target_pairs={{0,1},{1,0},{2,3},{3,2},{4,5},{5,4},{6,7},{7,6},{8,9},{9,8},{10,11... | collective-permute-start | bytes 1572872 | tf_op jit(solution)/shard_map/ppermute | solution.py:16
  118.9 1.3 collective-permute-done
  120.6 15.5 %reduce-scatter.2.cloned.1.call-done = f32[1,128,640]{2,1,0:T(8,128)} async-done(((f32[8,128,640]{2,1,0:T(8,128)}), f32[1,128,640]{2,1,0:T(8,128)}) %reduce-scatter.2.cloned.1.call-update) | async-done | bytes 327696 | tf_op jit(solution)/shard_map/reduce_scatter | solution.py:147
  136.1 1.0 slice.37
  137.1 0.8 slice_bitcast_fusion
  138.2 0.3 fusion.22
  138.6 0.9 fusion.25
  139.5 5.8 %collective-permute-start.1 = (bf16[128,128]{1,0:T(8,128)(2,1)S(1)}, bf16[128,128]{1,0:T(8,128)(2,1)S(1)}, u32[]{:S(2)}, u32[]{:S(2)}) collective-permute-start(bf16[128,128]{1,0:T(8,128)(2,1)S(1)} %fusion.25), channel_id=1, source_target_pairs={{0,1},{1,0},{2,3},{3,2},{4,5},{5,4},{6,7},{7,6},{8,9},{9,8},{10,11... | collective-permute-start | bytes 98312 | tf_op jit(solution)/shard_map/ppermute | solution.py:16
  145.4 0.8 collective-permute-done.1
  146.3 1.1 fusion.57
  147.4 1.6 fusion.9
  149.0 0.8 copy.30
  149.7 0.8 copy.45
  (54 shorter events, 3.2 us)
Async XLA Ops:
  7.2 12.3 %copy-start.5 = (f32[4096]{0:T(1024)S(1)}, f32[4096]{0:T(1024)}, u32[]{:S(2)}) copy-start(f32[4096]{0:T(1024)} %param.10) | copy-start | bytes 49156
  9.2 25.3 %all-to-all-start = ((bf16[8,128,512]{2,1,0:T(8,128)(2,1)}), bf16[8,128,512]{2,1,0:T(8,128)(2,1)S(1)}, u32[]{:S(2)}, u32[]{:S(2)}) async-start(bf16[8,128,512]{2,1,0:T(8,128)(2,1)} %broadcast_in_dim.35), calls=%async_computation | async-start | bytes 2097152 | tf_op jit(solution)/shard_map/all_to_all | solution.py:22
  34.7 6.9 %copy-start.1 = (bf16[64,512]{1,0:T(8,128)(2,1)S(1)}, bf16[64,512]{1,0:T(8,128)(2,1)}, u32[]{:S(2)}) copy-start(bf16[64,512]{1,0:T(8,128)(2,1)} %param.12) | copy-start | bytes 196612
  34.7 6.9 %copy-start.2 = (bf16[64,512]{1,0:T(8,128)(2,1)S(1)}, bf16[64,512]{1,0:T(8,128)(2,1)}, u32[]{:S(2)}) copy-start(bf16[64,512]{1,0:T(8,128)(2,1)} %param.13) | copy-start | bytes 196612
  34.8 7.0 %copy-start.3 = (bf16[64,512]{1,0:T(8,128)(2,1)S(1)}, bf16[64,512]{1,0:T(8,128)(2,1)}, u32[]{:S(2)}) copy-start(bf16[64,512]{1,0:T(8,128)(2,1)} %param.11) | copy-start | bytes 196612
  36.1 34.7 %all-to-all-start.1 = ((bf16[8,128,512]{2,1,0:T(8,128)(2,1)}), bf16[8,128,512]{2,1,0:T(8,128)(2,1)S(1)}, u32[]{:S(2)}, u32[]{:S(2)}) async-start(bf16[8,128,512]{2,1,0:T(8,128)(2,1)} %fusion.6), calls=%async_computation.1 | async-start | bytes 2097152 | tf_op jit(solution)/shard_map/all_to_all | solution.py:143
  41.6 94.5 %reduce-scatter.2.cloned.1.call-start = ((), (), s32[]{:S(2)}) async-start(), calls=%async_computation.4 | async-start | bytes 2949120 | tf_op jit(solution)/shard_map/reduce_scatter | solution.py:147
  73.3 0.7 copy-start.4
  73.3 1.7 %copy-start = (bf16[64,1,2,16,128]{4,3,2,1,0:T(8,128)(2,1)S(1)}, bf16[64,1,2,16,128]{4,3,2,1,0:T(8,128)(2,1)}, u32[]{:S(2)}) copy-start(bf16[64,1,2,16,128]{4,3,2,1,0:T(8,128)(2,1)} %param.14) | copy-start | bytes 1572868
  75.4 9.4 %copy-start.6 = (s32[128]{0:T(128)S(1)}, s32[128]{0:T(128)}, u32[]{:S(2)}) copy-start(s32[128]{0:T(128)} %param.17) | copy-start | bytes 1540
  75.4 9.6 %copy-start.7 = (s32[4]{0:T(128)S(1)}, s32[4]{0:T(128)}, u32[]{:S(2)}) copy-start(s32[4]{0:T(128)} %param.16) | copy-start | bytes 52
  76.9 33.0 %all-to-all-start.2 = ((bf16[64,2,4096]{2,1,0:T(2,128)(2,1)}), bf16[64,2,4096]{2,1,0:T(2,128)(2,1)S(1)}, u32[]{:S(2)}, u32[]{:S(2)}) async-start(bf16[64,2,4096]{2,1,0:T(2,128)(2,1)} %reshape.328), calls=%async_computation.3 | async-start | bytes 2097152 | tf_op jit(solution)/shard_map/all_to_all | solution.py:112
  111.1 9.1 %collective-permute-start = (bf16[4,1,2,256,128]{4,3,2,1,0:T(8,128)(2,1)S(1)}, bf16[4,1,2,256,128]{4,3,2,1,0:T(8,128)(2,1)S(1)}, u32[]{:S(2)}, u32[]{:S(2)}) collective-permute-start(bf16[4,1,2,256,128]{4,3,2,1,0:T(8,128)(2,1)S(1)} %broadcast_select_fusion), channel_id=1, source_target_pairs={{0,1},{1,0},{2,3},{3,2},{4,5},{5,4},{6,7},{7,6},{8,9},{9,8},{10,11... | collective-permute-start | bytes 1572872 | tf_op jit(solution)/shard_map/ppermute | solution.py:16
  139.5 6.7 %collective-permute-start.1 = (bf16[128,128]{1,0:T(8,128)(2,1)S(1)}, bf16[128,128]{1,0:T(8,128)(2,1)S(1)}, u32[]{:S(2)}, u32[]{:S(2)}) collective-permute-start(bf16[128,128]{1,0:T(8,128)(2,1)S(1)} %fusion.25), channel_id=1, source_target_pairs={{0,1},{1,0},{2,3},{3,2},{4,5},{5,4},{6,7},{7,6},{8,9},{9,8},{10,11... | collective-permute-start | bytes 98312 | tf_op jit(solution)/shard_map/ppermute | solution.py:16
Sparse Core Ops, SparseCore 0:
  73.4 62.6 reduce-scatter.1

commit v7 on v5

--- a/solution.py
+++ b/solution.py
@@ -164,14 +164,18 @@
         [layer_zero[:, 1].reshape(requests_here * max_len, head_dim), new_values], axis=0
     )
 
+    flat_queries = queries.reshape(rows_here * heads_here, head_dim)
     scores = (
-        jnp.einsum("thd,nd->thn", queries, all_keys, preferred_element_type=jnp.float32)
+        jnp.einsum("td,nd->tn", flat_queries, all_keys, preferred_element_type=jnp.float32)
         * score_scale
     )
-    attn_probs = weigh(scores, allowed[:, None, :])
-    heads_out = jnp.einsum(
-        "thn,nd->thd", attn_probs, all_values, preferred_element_type=jnp.float32
-    ).astype(jnp.bfloat16)
+    flat_allowed = jnp.broadcast_to(
+        allowed[:, None, :], (rows_here, heads_here, allowed.shape[1])
+    ).reshape(rows_here * heads_here, allowed.shape[1])
+    attn_probs = weigh(scores, flat_allowed)
+    heads_out = jnp.dot(attn_probs, all_values, preferred_element_type=jnp.float32).astype(
+        jnp.bfloat16
+    )
     attention = heads_out.reshape(rows_here, heads_here * head_dim)
     return (attention, partner_cache)
 

time: 140 us -> 139 us (level)
  waiting for transfers between devices: 67.4 us -> 66 us
    all_to_all x1, waiting for transfers between devices: 26.7 us -> 24.6 us  [on_device(): lax.all_to_all(outgoing, GROUP, split_axis=0, concat_axis=0, tiled=True)]
    reshape x0 -> x2, local copies, waits for them, and re-layouts: none -> 2.02 us  [the longest x1 1.27 us: on_device(): flat_allowed = jnp.broadcast_to(allowed[:, None, :], (rows_here, heads_he...]
  transfers between devices with their start and end apart: 5 -> 5, of which waited for: 5 -> 5; matrix products, arithmetic and copies ran while one was open for 9% -> 10% of each run, Pallas kernels for 0% -> 0%
where the time goes in v7:
time: 139 us; the launch traced here: 138 us
  waiting for transfers between devices  66 us (47%)
  starting transfers between devices  33.7 us (24%)
  between operations  14.4 us (10%)
  other arithmetic  9.75 us (7%)
  local copies, waits for them, and re-layouts  8.57 us (6%)
  matrix products  5.65 us (4%)
    all_gather x1, waiting for transfers between devices, on_device(): lax.all_gather(joined_cols, GROUP, axis=0, tiled=True)  31.6 us
    all_to_all x1, waiting for transfers between devices, on_device(): lax.all_to_all(outgoing, GROUP, split_axis=0, concat_axis=0, tiled=True)  24.6 us
    all_to_all x1, starting transfers between devices, on_device(): lax.all_to_all(outgoing, GROUP, split_axis=0, concat_axis=0, tiled=True)  11.8 us
    ppermute x2, starting transfers between devices, from_partner(): lax.ppermute(x, axis, [(i, i ^ 1 << bit) for i in range(lax.axis_size(axi...  11.6 us
    all_to_all x1, starting transfers between devices, gather_by_all_to_all(): ordered = lax.all_to_all(spread, axis, 0, 0, tiled=True)  10.3 us
    all_to_all x1, waiting for transfers between devices, gather_by_all_to_all(): ordered = lax.all_to_all(spread, axis, 0, 0, tiled=True)  8.6 us
    dot_general x1, matrix products, on_device(): jnp.dot(normed, lax.all_gather(joined_cols, GROUP, axis=0, tiled=True), p...  3.51 us
  transfers between devices with their start and end apart: 5, of which 5 were waited for; matrix products, arithmetic and copies ran while one was open for 10% of the time, Pallas kernels for 0%

profile of v7, /device:TPU:1, one launch (start us, length us, event | category | flops | bytes accessed | tf_op | source)
XLA Modules:
  0.0 138.1 jit_solution(15109051871361708176)
XLA Ops:
  7.3 0.8 fusion.30
  8.1 1.5 %pad_maximum_fusion = bf16[64,640]{1,0:T(8,128)(2,1)} fusion(bf16[64,128]{1,0:T(8,128)(2,1)S(1)} %fusion.30, bf16[64,512]{1,0:T(8,128)(2,1)} %param.11), kind=kLoop, calls=%fused_computation.42 | loop fusion | flops 163840 | bytes 163840 | tf_op jit(solution)/shard_map/concatenate | solution.py:139
  9.6 1.0 copy.15
  10.6 1.1 broadcast_in_dim.32
  11.7 10.3 %all-to-all-start = ((bf16[8,128,512]{1,2,0:T(8,128)(2,1)}), bf16[8,128,512]{1,2,0:T(8,128)(2,1)S(1)}, u32[]{:S(2)}, u32[]{:S(2)}) async-start(bf16[8,128,512]{1,2,0:T(8,128)(2,1)} %broadcast_in_dim.32), calls=%async_computation | async-start | bytes 2097152 | tf_op jit(solution)/shard_map/all_to_all | solution.py:22
  22.3 0.3 select_reduce_fusion
  23.0 0.4 convolution_convert_fusion
  23.5 1.5 %reshape.328 = bf16[64,2,4096]{2,1,0:T(2,128)(2,1)} reshape(bf16[128,4096]{1,0:T(8,128)(2,1)S(1)} %convolution_convert_fusion) | data formatting | bytes 2097152 | tf_op jit(solution)/shard_map/reshape | solution.py:110
  25.0 0.6 fusion.43
  25.6 2.5 %compare_select_fusion.1 = s32[1024,1]{0,1:T(1,128)S(1)} fusion(s32[]{:T(128)} %bitcast, s32[]{:T(128)} %bitcast.1, s32[]{:T(128)} %bitcast.3, s32[]{:T(128)} %bitcast.2), kind=kLoop, calls=%fused_computation.67 | loop fusion | flops 17408 | bytes 4112 | tf_op jit(solution)/shard_map/gather | solution.py:61
  28.4 8.6 %all-to-all-done = bf16[8,128,512]{1,2,0:T(8,128)(2,1)S(1)} async-done(((bf16[8,128,512]{1,2,0:T(8,128)(2,1)}), bf16[8,128,512]{1,2,0:T(8,128)(2,1)S(1)}, u32[]{:S(2)}, u32[]{:S(2)}) %all-to-all-start) | async-done | bytes 1048608 | tf_op jit(solution)/shard_map/all_to_all | solution.py:22
  37.0 11.8 %all-to-all-start.1 = ((bf16[64,2,4096]{2,1,0:T(2,128)(2,1)}), bf16[64,2,4096]{2,1,0:T(2,128)(2,1)S(1)}, u32[]{:S(2)}, u32[]{:S(2)}) async-start(bf16[64,2,4096]{2,1,0:T(2,128)(2,1)} %reshape.328), calls=%async_computation.1 | async-start | bytes 2097152 | tf_op jit(solution)/shard_map/all_to_all | solution.py:112
  48.8 0.5 broadcast_in_dim.31
  49.4 1.3 reshape.324
  51.4 0.3 multiply_cosine_fusion.1
  51.7 0.6 multiply_reduce_fusion
  52.3 24.6 %all-to-all-done.1 = bf16[64,2,4096]{2,1,0:T(2,128)(2,1)S(1)} async-done(((bf16[64,2,4096]{2,1,0:T(2,128)(2,1)}), bf16[64,2,4096]{2,1,0:T(2,128)(2,1)S(1)}, u32[]{:S(2)}, u32[]{:S(2)}) %all-to-all-start.1) | async-done | bytes 1048608 | tf_op jit(solution)/shard_map/all_to_all | solution.py:112
  76.8 0.4 reshape.329
  77.3 0.4 fusion.4
  78.0 5.1 %collective-permute-start = (bf16[4,1,2,256,128]{4,3,2,1,0:T(8,128)(2,1)S(1)}, bf16[4,1,2,256,128]{4,3,2,1,0:T(8,128)(2,1)S(1)}, u32[]{:S(2)}, u32[]{:S(2)}) collective-permute-start(bf16[4,1,2,256,128]{4,3,2,1,0:T(8,128)(2,1)S(1)} %broadcast_select_fusion), channel_id=1, source_target_pairs={{0,1},{1,0},{2,3},{3,2},{4,5},{5,4},{6,7},{7,6},{8,9},{9,8},{10,11... | collective-permute-start | bytes 1572872 | tf_op jit(solution)/shard_map/ppermute | solution.py:16
  83.1 0.7 fusion.2
  83.8 0.8 collective-permute-done
  84.9 31.6 %all-gather.2.cloned.1.call-done = bf16[4096,640]{1,0:T(8,128)(2,1)} async-done(((bf16[64,640]{1,0:T(8,128)(2,1)}), bf16[4096,640]{1,0:T(8,128)(2,1)}) %all-gather.2.cloned.1.call-update) | async-done | bytes 5242896 | tf_op jit(solution)/shard_map/all_gather | solution.py:142
  116.5 3.5 %fusion.45 = f32[128,640]{1,0:T(8,128)S(1)} fusion(bf16[128,4096]{0,1:T(8,128)(2,1)S(1)} %fusion.2, bf16[4096,640]{1,0:T(8,128)(2,1)} %all-gather.2.cloned.1.call-done), kind=kOutput, calls=%fused_computation.106 | convolution fusion | flops 671088640 | bytes 6619136 | tf_op jit(solution)/shard_map/dot_general | solution.py:140
  120.1 0.3 fusion.22
  120.5 6.5 %collective-permute-start.1 = (bf16[128,128]{1,0:T(8,128)(2,1)S(1)}, bf16[128,128]{1,0:T(8,128)(2,1)S(1)}, u32[]{:S(2)}, u32[]{:S(2)}) collective-permute-start(bf16[128,128]{1,0:T(8,128)(2,1)S(1)} %fusion.25), channel_id=1, source_target_pairs={{0,1},{1,0},{2,3},{3,2},{4,5},{5,4},{6,7},{7,6},{8,9},{9,8},{10,11... | collective-permute-start | bytes 98312 | tf_op jit(solution)/shard_map/ppermute | solution.py:16
  127.3 0.4 collective-permute-done.1
  127.8 0.8 fusion.44
  128.6 0.5 fusion.3
  129.1 0.6 fusion.6
  129.7 0.7 reshape.333
  130.5 0.8 copy.26
  (47 shorter events, 2.8 us)
Async XLA Ops:
  7.2 14.9 %copy-start.3 = (s32[256,16]{0,1:T(8,128)S(1)}, s32[256,16]{0,1:T(8,128)}, u32[]{:S(2)}) copy-start(s32[256,16]{0,1:T(8,128)} %param.15) | copy-start | bytes 49156
  7.2 15.9 %copy-start.1 = (bf16[64,1,2,16,128]{4,3,2,1,0:T(8,128)(2,1)S(1)}, bf16[64,1,2,16,128]{4,3,2,1,0:T(8,128)(2,1)}, u32[]{:S(2)}) copy-start(bf16[64,1,2,16,128]{4,3,2,1,0:T(8,128)(2,1)} %param.14) | copy-start | bytes 1572868
  7.2 109.3 %all-gather.2.cloned.1.call-start = ((), (), s32[]{:S(2)}) async-start(), calls=%async_computation.2 | async-start | bytes 5324800 | tf_op jit(solution)/shard_map/all_gather | solution.py:142
  11.7 25.3 %all-to-all-start = ((bf16[8,128,512]{1,2,0:T(8,128)(2,1)}), bf16[8,128,512]{1,2,0:T(8,128)(2,1)S(1)}, u32[]{:S(2)}, u32[]{:S(2)}) async-start(bf16[8,128,512]{1,2,0:T(8,128)(2,1)} %broadcast_in_dim.32), calls=%async_computation | async-start | bytes 2097152 | tf_op jit(solution)/shard_map/all_to_all | solution.py:22
  22.0 3.0 %copy-start.5 = (s32[4]{0:T(128)S(1)}, s32[4]{0:T(128)}, u32[]{:S(2)}) copy-start(s32[4]{0:T(128)} %param.16) | copy-start | bytes 52
  22.0 6.1 %copy-start.4 = (s32[128]{0:T(128)S(1)}, s32[128]{0:T(128)}, u32[]{:S(2)}) copy-start(s32[128]{0:T(128)} %param.17) | copy-start | bytes 1540
  37.0 39.8 %all-to-all-start.1 = ((bf16[64,2,4096]{2,1,0:T(2,128)(2,1)}), bf16[64,2,4096]{2,1,0:T(2,128)(2,1)S(1)}, u32[]{:S(2)}, u32[]{:S(2)}) async-start(bf16[64,2,4096]{2,1,0:T(2,128)(2,1)} %reshape.328), calls=%async_computation.1 | async-start | bytes 2097152 | tf_op jit(solution)/shard_map/all_to_all | solution.py:112
  77.3 5.9 %copy-start.2 = (f32[4096]{0:T(1024)S(1)}, f32[4096]{0:T(1024)}, u32[]{:S(2)}) copy-start(f32[4096]{0:T(1024)} %param.10) | copy-start | bytes 49156
  78.0 6.6 %collective-permute-start = (bf16[4,1,2,256,128]{4,3,2,1,0:T(8,128)(2,1)S(1)}, bf16[4,1,2,256,128]{4,3,2,1,0:T(8,128)(2,1)S(1)}, u32[]{:S(2)}, u32[]{:S(2)}) collective-permute-start(bf16[4,1,2,256,128]{4,3,2,1,0:T(8,128)(2,1)S(1)} %broadcast_select_fusion), channel_id=1, source_target_pairs={{0,1},{1,0},{2,3},{3,2},{4,5},{5,4},{6,7},{7,6},{8,9},{9,8},{10,11... | collective-permute-start | bytes 1572872 | tf_op jit(solution)/shard_map/ppermute | solution.py:16
  120.0 7.8 %copy-start = (pred[512,1152]{1,0:T(32,128)(4,1)S(1)}, pred[512,1152]{1,0:T(32,128)(4,1)}, u32[]{:S(2)}) copy-start(pred[512,1152]{1,0:T(32,128)(4,1)} %reshape.324) | copy-start | bytes 1769476
  120.5 7.3 %collective-permute-start.1 = (bf16[128,128]{1,0:T(8,128)(2,1)S(1)}, bf16[128,128]{1,0:T(8,128)(2,1)S(1)}, u32[]{:S(2)}, u32[]{:S(2)}) collective-permute-start(bf16[128,128]{1,0:T(8,128)(2,1)S(1)} %fusion.25), channel_id=1, source_target_pairs={{0,1},{1,0},{2,3},{3,2},{4,5},{5,4},{6,7},{7,6},{8,9},{9,8},{10,11... | collective-permute-start | bytes 98312 | tf_op jit(solution)/shard_map/ppermute | solution.py:16
Sparse Core Ops, SparseCore 0:
  11.6 104.8 all-gather.1

commit v8 on v7

--- a/solution.py
+++ b/solution.py
@@ -102,6 +102,14 @@
     buffer_row = target_owner * capacity + order_within
     page_rows = kv_pool.reshape(pool_pages, -1)
     row_width = page_rows.shape[1]
+    heads_here = q_weight.shape[1] // head_dim
+    per_kv = HEADS // KVH
+    first_kv = mp_idx * heads_here // per_kv
+    kv_weight = jnp.concatenate([k_weight, v_weight], axis=1)
+    own_kv_cols = lax.dynamic_slice_in_dim(
+        kv_weight, (mp_idx % 2) * k_weight.shape[1] + first_kv * head_dim, head_dim, 1
+    )
+    kv_rows = own_kv_cols.reshape(-1, row_width)
     buffer_ids = jnp.arange(groups * capacity, dtype=jnp.int32)
     send_pick = (buffer_ids[:, None] == buffer_row[None, :]).astype(jnp.bfloat16)
     outgoing = (
@@ -109,7 +117,12 @@
         .astype(jnp.bfloat16)
         .reshape(groups, capacity, row_width)
     )
-    arrived = lax.all_to_all(outgoing, GROUP, split_axis=0, concat_axis=0, tiled=True)
+    with_kv = jnp.concatenate(
+        [outgoing, jnp.broadcast_to(kv_rows[None], (groups,) + kv_rows.shape)], axis=1
+    )
+    arrived_all = lax.all_to_all(with_kv, GROUP, split_axis=0, concat_axis=0, tiled=True)
+    arrived = arrived_all[:, :capacity]
+    kv_full = arrived_all[:, capacity:].reshape(-1, head_dim)
     my_pages = lax.dynamic_slice_in_dim(flat_table, group_idx * pool_pages, pool_pages)
     sender = my_pages // pool_pages
     earlier_same = (sender[None, :] == sender[:, None]) & (my_pages[None, :] < my_pages[:, None])
@@ -127,23 +140,13 @@
     whole_rows = gather_by_all_to_all(tokens, "mp", 1)
     normed = normalize(whole_rows, attn_gain)
     rows_here = tokens.shape[0]
-    heads_here = q_weight.shape[1] // head_dim
-    per_kv = HEADS // KVH
-    first_kv = mp_idx * heads_here // per_kv
     is_even = mp_idx % 2 == 0
-    kv_weight = jnp.concatenate([k_weight, v_weight], axis=1)
-    own_kv_cols = lax.dynamic_slice_in_dim(
-        kv_weight, (mp_idx % 2) * k_weight.shape[1] + first_kv * head_dim, head_dim, 1
-    )
-    q_cols = q_weight.shape[1]
-    joined_cols = jnp.concatenate([q_weight, own_kv_cols], axis=1)
-    joined_sum = jnp.dot(
+    kv_sum = jnp.dot(normed, kv_full, preferred_element_type=jnp.float32)
+    query_sum = jnp.dot(
         normed,
-        lax.all_gather(joined_cols, GROUP, axis=0, tiled=True),
+        lax.all_gather(q_weight, GROUP, axis=0, tiled=True),
         preferred_element_type=jnp.float32,
     )
-    query_sum = joined_sum[:, :q_cols]
-    kv_sum = joined_sum[:, q_cols:]
     position = token_positions(token_request, lengths, requests_here)
     queries = rotate(query_sum.reshape(rows_here, heads_here, head_dim), position).astype(
         jnp.bfloat16

time: 139 us -> 163 us (1.17)
  the two profiles are of different devices: /device:TPU:1 before, /device:TPU:2 now
where the time goes in v8:
time: 163 us
  waiting for transfers between devices  81.5 us (50%)
  starting transfers between devices  26.2 us (16%)
  local copies, waits for them, and re-layouts  23.1 us (14%)
  between operations  14.5 us (9%)
  other arithmetic  11.5 us (7%)
  matrix products  6.06 us (4%)
    all_to_all x1, waiting for transfers between devices, on_device(): lax.all_to_all(with_kv, GROUP, split_axis=0, concat_axis=0, tiled=True)  47 us
    all_gather x1, waiting for transfers between devices, on_device(): lax.all_gather(q_weight, GROUP, axis=0, tiled=True)  25.7 us
    all_to_all x1, starting transfers between devices, on_device(): lax.all_to_all(with_kv, GROUP, split_axis=0, concat_axis=0, tiled=True)  12.3 us
    all_to_all x1, starting transfers between devices, gather_by_all_to_all(): ordered = lax.all_to_all(spread, axis, 0, 0, tiled=True)  9.34 us
    all_to_all x1, waiting for transfers between devices, gather_by_all_to_all(): ordered = lax.all_to_all(spread, axis, 0, 0, tiled=True)  8.09 us
    dot_general x1, local copies, waits for them, and re-layouts, on_device(): jnp.dot(normed, lax.all_gather(q_weight, GROUP, axis=0, tiled=True), pref...  6.45 us
    slice x1, local copies, waits for them, and re-layouts, on_device(): arrived = arrived_all[:, :capacity]  5.23 us
    ppermute x2, starting transfers between devices, from_partner(): lax.ppermute(x, axis, [(i, i ^ 1 << bit) for i in range(lax.axis_size(axi...  4.5 us
  transfers between devices with their start and end apart: 5, of which 3 were waited for; matrix products, arithmetic and copies ran while one was open for 17% of the time, Pallas kernels for 0%

profile of v8, /device:TPU:2, one launch (start us, length us, event | category | flops | bytes accessed | tf_op | source)
XLA Modules:
  0.0 162.8 jit_solution(14130984120105004460)
XLA Ops:
  7.2 0.7 all-gather.2.cloned.1.call-update
  7.9 2.0 %broadcast_in_dim.36 = bf16[8,128,512]{2,1,0:T(8,128)(2,1)} broadcast(bf16[128,512]{1,0:T(8,128)(2,1)} %param.9), dimensions={1,2} | broadcast | bytes 1179648 | tf_op jit(solution)/shard_map/broadcast_in_dim | solution.py:21
  9.9 9.3 %all-to-all-start = ((bf16[8,128,512]{2,1,0:T(8,128)(2,1)}), bf16[8,128,512]{2,1,0:T(8,128)(2,1)S(1)}, u32[]{:S(2)}, u32[]{:S(2)}) async-start(bf16[8,128,512]{2,1,0:T(8,128)(2,1)} %broadcast_in_dim.36), calls=%async_computation | async-start | bytes 2097152 | tf_op jit(solution)/shard_map/all_to_all | solution.py:22
  20.7 0.7 reshape.349
  21.5 1.0 broadcast_in_dim.41
  22.5 3.2 %pad_maximum_fusion = bf16[64,4,4096]{2,1,0:T(4,128)(2,1)} fusion(bf16[64,2,4096]{2,1,0:T(2,128)(2,1)S(1)} %broadcast_in_dim.41, bf16[64,2,4096]{2,1,0:T(2,128)(2,1)S(1)} %reshape.349), kind=kLoop, calls=%fused_computation.11 | loop fusion | flops 4194304 | bytes 4194304 | tf_op jit(solution)/shard_map/concatenate | solution.py:120
  25.7 8.1 %all-to-all-done = bf16[8,128,512]{2,1,0:T(8,128)(2,1)S(1)} async-done(((bf16[8,128,512]{2,1,0:T(8,128)(2,1)}), bf16[8,128,512]{2,1,0:T(8,128)(2,1)S(1)}, u32[]{:S(2)}, u32[]{:S(2)}) %all-to-all-start) | async-done | bytes 1048608 | tf_op jit(solution)/shard_map/all_to_all | solution.py:22
  33.8 12.3 %all-to-all-start.1 = ((bf16[64,4,4096]{2,1,0:T(4,128)(2,1)}), bf16[64,4,4096]{2,1,0:T(4,128)(2,1)}, u32[]{:S(2)}, u32[]{:S(2)}) async-start(bf16[64,4,4096]{2,1,0:T(4,128)(2,1)} %pad_maximum_fusion), calls=%async_computation.1 | async-start | bytes 4194304 | tf_op jit(solution)/shard_map/all_to_all | solution.py:123
  46.4 0.6 fusion.45
  47.0 2.5 %compare_select_fusion.1 = s32[1024,1]{0,1:T(1,128)S(1)} fusion(s32[]{:T(128)} %bitcast, s32[]{:T(128)} %bitcast.1, s32[]{:T(128)} %bitcast.3, s32[]{:T(128)} %bitcast.2), kind=kLoop, calls=%fused_computation.67 | loop fusion | flops 17408 | bytes 4112 | tf_op jit(solution)/shard_map/gather | solution.py:61
  50.2 0.7 copy.38
  50.9 0.6 fusion.1
  51.5 0.7 fusion.3
  52.2 47.0 %all-to-all-done.1 = bf16[64,4,4096]{2,1,0:T(4,128)(2,1)} async-done(((bf16[64,4,4096]{2,1,0:T(4,128)(2,1)}), bf16[64,4,4096]{2,1,0:T(4,128)(2,1)}, u32[]{:S(2)}, u32[]{:S(2)}) %all-to-all-start.1) | async-done | bytes 2097184 | tf_op jit(solution)/shard_map/all_to_all | solution.py:123
  99.2 5.2 %fusion.43 = (bf16[64,2,4096]{2,1,0:T(2,128)(2,1)S(1)}, bf16[64,2,4096]{2,1,0:T(2,128)(2,1)}) fusion(bf16[64,4,4096]{2,1,0:T(4,128)(2,1)} %all-to-all-done.1), kind=kLoop, calls=%fused_computation.103 | loop fusion | bytes 4194304 | tf_op jit(solution)/shard_map/slice | solution.py:124
  105.4 1.0 broadcast_select_fusion
  106.4 1.9 %collective-permute-start = (bf16[4,1,2,256,128]{4,3,2,1,0:T(8,128)(2,1)}, bf16[4,1,2,256,128]{4,3,2,1,0:T(8,128)(2,1)S(1)}, u32[]{:S(2)}, u32[]{:S(2)}) collective-permute-start(bf16[4,1,2,256,128]{4,3,2,1,0:T(8,128)(2,1)} %broadcast_select_fusion), channel_id=1, source_target_pairs={{0,1},{1,0},{2,3},{3,2},{4,5},{5,4},{6,7},{7,6},{8,9},{9,8},{10,11... | collective-permute-start | bytes 1572872 | tf_op jit(solution)/shard_map/ppermute | solution.py:16
  108.3 1.9 %reshape.353 = bf16[4096,128]{1,0:T(8,128)(2,1)S(1)} reshape(bf16[64,2,4096]{2,1,0:T(2,128)(2,1)} %get-tuple-element.7) | data formatting | bytes 2097152 | tf_op jit(solution)/shard_map/reshape | solution.py:125
  110.2 0.5 fusion.48
  110.9 2.6 %collective-permute-start.1 = (bf16[128,128]{0,1:T(8,128)(2,1)S(1)}, bf16[128,128]{0,1:T(8,128)(2,1)S(1)}, u32[]{:S(2)}, u32[]{:S(2)}) collective-permute-start(bf16[128,128]{0,1:T(8,128)(2,1)S(1)} %fusion.20), channel_id=1, source_target_pairs={{0,1},{1,0},{2,3},{3,2},{4,5},{5,4},{6,7},{7,6},{8,9},{9,8},{10,11... | collective-permute-start | bytes 98312 | tf_op jit(solution)/shard_map/ppermute | solution.py:16
  113.5 0.8 multiply_cosine_fusion.1
  114.3 0.5 broadcast_in_dim.35
  114.8 0.6 reshape.346
  115.4 0.7 copy.46
  116.5 25.7 %all-gather.2.cloned.1.call-done = bf16[4096,512]{1,0:T(8,128)(2,1)} async-done(((bf16[64,512]{1,0:T(8,128)(2,1)}), bf16[4096,512]{1,0:T(8,128)(2,1)}) %all-gather.2.cloned.1.call-update) | async-done | bytes 4194320 | tf_op jit(solution)/shard_map/all_gather | solution.py:147
  142.2 6.5 %copy.39 = bf16[512,4096]{1,0:T(8,128)(2,1)} copy(bf16[512,4096]{0,1:T(8,128)(2,1)} %bitcast.48) | data formatting | bytes 8388608 | tf_op jit(solution)/shard_map/dot_general | solution.py:145
  148.7 3.4 %fusion.47 = f32[128,4,128]{0,2,1:T(8,128)S(1)} fusion(bf16[128,4096,1]{0,1,2:T(8,128)(2,1)S(1)} %bitcast.45, bf16[4,128,4096]{2,1,0:T(8,128)(2,1)} %bitcast.43), kind=kOutput, calls=%fused_computation.107 | convolution fusion | flops 536870912 | bytes 5505024 | tf_op jit(solution)/shard_map/dot_general | solution.py:145
  152.5 0.8 fusion.46
  153.3 0.5 fusion.4
  153.8 0.6 fusion.7
  154.4 0.7 reshape.355
  155.2 0.8 copy.57
  (63 shorter events, 4.3 us)
Async XLA Ops:
  7.2 12.1 %copy-start.6 = (s32[256,16]{0,1:T(8,128)S(1)}, s32[256,16]{0,1:T(8,128)}, u32[]{:S(2)}) copy-start(s32[256,16]{0,1:T(8,128)} %param.15) | copy-start | bytes 49156
  7.2 13.0 %copy-start.4 = (bf16[64,512]{1,0:T(8,128)(2,1)S(1)}, bf16[64,512]{1,0:T(8,128)(2,1)}, u32[]{:S(2)}) copy-start(bf16[64,512]{1,0:T(8,128)(2,1)} %param.13) | copy-start | bytes 196612
  7.2 13.0 %copy-start.3 = (bf16[64,512]{1,0:T(8,128)(2,1)S(1)}, bf16[64,512]{1,0:T(8,128)(2,1)}, u32[]{:S(2)}) copy-start(bf16[64,512]{1,0:T(8,128)(2,1)} %param.12) | copy-start | bytes 196612
  7.2 13.1 %copy-start = (bf16[64,1,2,16,128]{4,3,2,1,0:T(8,128)(2,1)S(1)}, bf16[64,1,2,16,128]{4,3,2,1,0:T(8,128)(2,1)}, u32[]{:S(2)}) copy-start(bf16[64,1,2,16,128]{4,3,2,1,0:T(8,128)(2,1)} %param.14) | copy-start | bytes 1572868
  7.2 135.0 %all-gather.2.cloned.1.call-start = ((), (), s32[]{:S(2)}) async-start(), calls=%async_computation.2 | async-start | bytes 4259840 | tf_op jit(solution)/shard_map/all_gather | solution.py:147
  9.9 23.9 %all-to-all-start = ((bf16[8,128,512]{2,1,0:T(8,128)(2,1)}), bf16[8,128,512]{2,1,0:T(8,128)(2,1)S(1)}, u32[]{:S(2)}, u32[]{:S(2)}) async-start(bf16[8,128,512]{2,1,0:T(8,128)(2,1)} %broadcast_in_dim.36), calls=%async_computation | async-start | bytes 2097152 | tf_op jit(solution)/shard_map/all_to_all | solution.py:22
  25.7 20.4 %copy-start.7 = (f32[4096]{0:T(1024)S(1)}, f32[4096]{0:T(1024)}, u32[]{:S(2)}) copy-start(f32[4096]{0:T(1024)} %param.10) | copy-start | bytes 49156
  25.7 20.4 %copy-start.8 = (s32[128]{0:T(128)S(1)}, s32[128]{0:T(128)}, u32[]{:S(2)}) copy-start(s32[128]{0:T(128)} %param.17) | copy-start | bytes 1540
  25.7 20.7 %copy-start.9 = (s32[4]{0:T(128)S(1)}, s32[4]{0:T(128)}, u32[]{:S(2)}) copy-start(s32[4]{0:T(128)} %param.16) | copy-start | bytes 52
  33.8 65.5 %all-to-all-start.1 = ((bf16[64,4,4096]{2,1,0:T(4,128)(2,1)}), bf16[64,4,4096]{2,1,0:T(4,128)(2,1)}, u32[]{:S(2)}, u32[]{:S(2)}) async-start(bf16[64,4,4096]{2,1,0:T(4,128)(2,1)} %pad_maximum_fusion), calls=%async_computation.1 | async-start | bytes 4194304 | tf_op jit(solution)/shard_map/all_to_all | solution.py:123
  106.4 9.9 %collective-permute-start = (bf16[4,1,2,256,128]{4,3,2,1,0:T(8,128)(2,1)}, bf16[4,1,2,256,128]{4,3,2,1,0:T(8,128)(2,1)S(1)}, u32[]{:S(2)}, u32[]{:S(2)}) collective-permute-start(bf16[4,1,2,256,128]{4,3,2,1,0:T(8,128)(2,1)} %broadcast_select_fusion), channel_id=1, source_target_pairs={{0,1},{1,0},{2,3},{3,2},{4,5},{5,4},{6,7},{7,6},{8,9},{9,8},{10,11... | collective-permute-start | bytes 1572872 | tf_op jit(solution)/shard_map/ppermute | solution.py:16
  110.9 4.5 %collective-permute-start.1 = (bf16[128,128]{0,1:T(8,128)(2,1)S(1)}, bf16[128,128]{0,1:T(8,128)(2,1)S(1)}, u32[]{:S(2)}, u32[]{:S(2)}) collective-permute-start(bf16[128,128]{0,1:T(8,128)(2,1)S(1)} %fusion.20), channel_id=1, source_target_pairs={{0,1},{1,0},{2,3},{3,2},{4,5},{5,4},{6,7},{7,6},{8,9},{9,8},{10,11... | collective-permute-start | bytes 98312 | tf_op jit(solution)/shard_map/ppermute | solution.py:16
  148.7 3.5 %copy-start.1 = (f32[128,64]{0,1:T(8,128)S(1)}, f32[128,64]{0,1:T(8,128)}, u32[]{:S(2)}) copy-start(f32[128,64]{0,1:T(8,128)} %get-tuple-element.16) | copy-start | bytes 98308
  148.7 3.5 %copy-start.2 = (f32[128,64]{0,1:T(8,128)S(1)}, f32[128,64]{0,1:T(8,128)}, u32[]{:S(2)}) copy-start(f32[128,64]{0,1:T(8,128)} %get-tuple-element.17) | copy-start | bytes 98308
  152.5 1.3 copy-start.5
Sparse Core Ops, SparseCore 0:
  11.1 131.1 all-gather.1

commit v9 on v7

--- a/solution.py
+++ b/solution.py
@@ -131,9 +131,8 @@
     per_kv = HEADS // KVH
     first_kv = mp_idx * heads_here // per_kv
     is_even = mp_idx % 2 == 0
-    kv_weight = jnp.concatenate([k_weight, v_weight], axis=1)
     own_kv_cols = lax.dynamic_slice_in_dim(
-        kv_weight, (mp_idx % 2) * k_weight.shape[1] + first_kv * head_dim, head_dim, 1
+        jnp.where(is_even, k_weight, v_weight), first_kv * head_dim, head_dim, 1
     )
     q_cols = q_weight.shape[1]
     joined_cols = jnp.concatenate([q_weight, own_kv_cols], axis=1)
@@ -157,18 +156,18 @@
     score_scale = head_dim ** (-0.5)
     partner_cache = from_partner(decoded, "mp", 0)
     layer_zero = jnp.where(is_even, decoded, partner_cache)[:, 0]
-    all_keys = jnp.concatenate(
-        [layer_zero[:, 0].reshape(requests_here * max_len, head_dim), new_keys], axis=0
-    )
+    cache_keys = layer_zero[:, 0].reshape(requests_here * max_len, head_dim)
     all_values = jnp.concatenate(
         [layer_zero[:, 1].reshape(requests_here * max_len, head_dim), new_values], axis=0
     )
-
     flat_queries = queries.reshape(rows_here * heads_here, head_dim)
-    scores = (
-        jnp.einsum("td,nd->tn", flat_queries, all_keys, preferred_element_type=jnp.float32)
-        * score_scale
-    )
+    cache_scores = jnp.einsum(
+        "td,nd->tn", flat_queries, cache_keys, preferred_element_type=jnp.float32
+    )
+    fresh_scores = jnp.einsum(
+        "td,nd->tn", flat_queries, new_keys, preferred_element_type=jnp.float32
+    )
+    scores = jnp.concatenate([cache_scores, fresh_scores], axis=1) * score_scale
     flat_allowed = jnp.broadcast_to(
         allowed[:, None, :], (rows_here, heads_here, allowed.shape[1])
     ).reshape(rows_here * heads_here, allowed.shape[1])

time: 139 us -> 146 us (1.050)
  matrix products: 5.65 us -> 8.95 us
  local copies, waits for them, and re-layouts: 8.57 us -> 11.3 us
  other arithmetic: 9.75 us -> 12.4 us
    dot_general x1, matrix products: 0.61 us -> 2.59 us  [on_device(): jnp.dot(attn_probs, all_values, preferred_element_type=jnp.float32)]
    concatenate x0 -> x1, local copies, waits for them, and re-layouts: none -> 1.86 us  [on_device(): scores = jnp.concatenate([cache_scores, fresh_scores], axis=1) * score_scale]
  transfers between devices with their start and end apart: 5 -> 5, of which waited for: 5 -> 4; matrix products, arithmetic and copies ran while one was open for 10% -> 13% of each run, Pallas kernels for 0% -> 0%
where the time goes in v9:
time: 146 us
  waiting for transfers between devices  64.9 us (44%)
  starting transfers between devices  33.9 us (23%)
  between operations  14.4 us (10%)
  other arithmetic  12.4 us (8%)
  local copies, waits for them, and re-layouts  11.3 us (8%)
  matrix products  8.95 us (6%)
    all_gather x1, waiting for transfers between devices, on_device(): lax.all_gather(joined_cols, GROUP, axis=0, tiled=True)  30.9 us
    all_to_all x1, waiting for transfers between devices, on_device(): lax.all_to_all(outgoing, GROUP, split_axis=0, concat_axis=0, tiled=True)  24.6 us
    ppermute x2, starting transfers between devices, from_partner(): lax.ppermute(x, axis, [(i, i ^ 1 << bit) for i in range(lax.axis_size(axi...  11.8 us
    all_to_all x1, starting transfers between devices, on_device(): lax.all_to_all(outgoing, GROUP, split_axis=0, concat_axis=0, tiled=True)  11.8 us
    all_to_all x1, starting transfers between devices, gather_by_all_to_all(): ordered = lax.all_to_all(spread, axis, 0, 0, tiled=True)  10.3 us
    all_to_all x1, waiting for transfers between devices, gather_by_all_to_all(): ordered = lax.all_to_all(spread, axis, 0, 0, tiled=True)  8.61 us
    dot_general x1, matrix products, on_device(): jnp.dot(normed, lax.all_gather(joined_cols, GROUP, axis=0, tiled=True), p...  3.51 us
  transfers between devices with their start and end apart: 5, of which 4 were waited for; matrix products, arithmetic and copies ran while one was open for 13% of the time, Pallas kernels for 0%

profile of v9, /device:TPU:1, one launch (start us, length us, event | category | flops | bytes accessed | tf_op | source)
XLA Modules:
  0.0 145.8 jit_solution(17581705440357845326)
XLA Ops:
  7.3 0.8 dynamic-slice_select_fusion
  8.1 1.5 %pad_maximum_fusion.1 = bf16[64,640]{1,0:T(8,128)(2,1)} fusion(bf16[64,128]{1,0:T(8,128)(2,1)S(1)} %dynamic-slice_select_fusion, bf16[64,512]{1,0:T(8,128)(2,1)} %param.11), kind=kLoop, calls=%fused_computation.40 | loop fusion | flops 163840 | bytes 163840 | tf_op jit(solution)/shard_map/concatenate | solution.py:138
  9.6 1.0 copy.15
  10.6 1.1 broadcast_in_dim.34
  11.7 10.3 %all-to-all-start = ((bf16[8,128,512]{1,2,0:T(8,128)(2,1)}), bf16[8,128,512]{1,2,0:T(8,128)(2,1)S(1)}, u32[]{:S(2)}, u32[]{:S(2)}) async-start(bf16[8,128,512]{1,2,0:T(8,128)(2,1)} %broadcast_in_dim.34), calls=%async_computation | async-start | bytes 2097152 | tf_op jit(solution)/shard_map/all_to_all | solution.py:22
  23.0 0.4 convolution_convert_fusion
  23.5 1.5 %reshape.341 = bf16[64,2,4096]{2,1,0:T(2,128)(2,1)} reshape(bf16[128,4096]{1,0:T(8,128)(2,1)S(1)} %convolution_convert_fusion) | data formatting | bytes 2097152 | tf_op jit(solution)/shard_map/reshape | solution.py:110
  25.0 0.6 fusion.52
  25.6 2.5 %compare_select_fusion.1 = s32[1024,1]{0,1:T(1,128)S(1)} fusion(s32[]{:T(128)} %bitcast, s32[]{:T(128)} %bitcast.1, s32[]{:T(128)} %bitcast.3, s32[]{:T(128)} %bitcast.2), kind=kLoop, calls=%fused_computation.68 | loop fusion | flops 17408 | bytes 4112 | tf_op jit(solution)/shard_map/gather | solution.py:61
  28.4 8.6 %all-to-all-done = bf16[8,128,512]{1,2,0:T(8,128)(2,1)S(1)} async-done(((bf16[8,128,512]{1,2,0:T(8,128)(2,1)}), bf16[8,128,512]{1,2,0:T(8,128)(2,1)S(1)}, u32[]{:S(2)}, u32[]{:S(2)}) %all-to-all-start) | async-done | bytes 1048608 | tf_op jit(solution)/shard_map/all_to_all | solution.py:22
  37.0 11.8 %all-to-all-start.1 = ((bf16[64,2,4096]{2,1,0:T(2,128)(2,1)}), bf16[64,2,4096]{2,1,0:T(2,128)(2,1)S(1)}, u32[]{:S(2)}, u32[]{:S(2)}) async-start(bf16[64,2,4096]{2,1,0:T(2,128)(2,1)} %reshape.341), calls=%async_computation.1 | async-start | bytes 2097152 | tf_op jit(solution)/shard_map/all_to_all | solution.py:112
  48.8 0.5 broadcast_in_dim.33
  49.4 1.3 reshape.337
  51.7 0.6 multiply_reduce_fusion
  52.3 24.6 %all-to-all-done.1 = bf16[64,2,4096]{2,1,0:T(2,128)(2,1)S(1)} async-done(((bf16[64,2,4096]{2,1,0:T(2,128)(2,1)}), bf16[64,2,4096]{2,1,0:T(2,128)(2,1)S(1)}, u32[]{:S(2)}, u32[]{:S(2)}) %all-to-all-start.1) | async-done | bytes 1048608 | tf_op jit(solution)/shard_map/all_to_all | solution.py:112
  76.8 0.4 reshape.342
  77.3 0.3 fusion.8
  78.0 5.1 %collective-permute-start = (bf16[4,1,2,256,128]{4,3,2,1,0:T(8,128)(2,1)S(1)}, bf16[4,1,2,256,128]{4,3,2,1,0:T(8,128)(2,1)S(1)}, u32[]{:S(2)}, u32[]{:S(2)}) collective-permute-start(bf16[4,1,2,256,128]{4,3,2,1,0:T(8,128)(2,1)S(1)} %broadcast_select_fusion), channel_id=1, source_target_pairs={{0,1},{1,0},{2,3},{3,2},{4,5},{5,4},{6,7},{7,6},{8,9},{9,8},{10,11... | collective-permute-start | bytes 1572872 | tf_op jit(solution)/shard_map/ppermute | solution.py:16
  83.1 0.7 fusion.7
  83.8 0.8 collective-permute-done
  84.8 0.7 fusion.51
  85.6 30.9 %all-gather.2.cloned.1.call-done = bf16[4096,640]{1,0:T(8,128)(2,1)} async-done(((bf16[64,640]{1,0:T(8,128)(2,1)}), bf16[4096,640]{1,0:T(8,128)(2,1)}) %all-gather.2.cloned.1.call-update) | async-done | bytes 5242896 | tf_op jit(solution)/shard_map/all_gather | solution.py:141
  116.5 3.5 %fusion.53 = f32[128,640]{1,0:T(8,128)S(1)} fusion(bf16[128,4096]{0,1:T(8,128)(2,1)S(1)} %fusion.7, bf16[4096,640]{1,0:T(8,128)(2,1)} %all-gather.2.cloned.1.call-done), kind=kOutput, calls=%fused_computation.110 | convolution fusion | flops 671088640 | bytes 6619136 | tf_op jit(solution)/shard_map/dot_general | solution.py:139
  120.0 0.3 fusion.24
  120.5 6.6 %collective-permute-start.1 = (bf16[128,128]{1,0:T(8,128)(2,1)S(1)}, bf16[128,128]{1,0:T(8,128)(2,1)S(1)}, u32[]{:S(2)}, u32[]{:S(2)}) collective-permute-start(bf16[128,128]{1,0:T(8,128)(2,1)S(1)} %fusion.27), channel_id=1, source_target_pairs={{0,1},{1,0},{2,3},{3,2},{4,5},{5,4},{6,7},{7,6},{8,9},{9,8},{10,11... | collective-permute-start | bytes 98312 | tf_op jit(solution)/shard_map/ppermute | solution.py:16
  127.5 1.8 %fusion.35 = f32[512,1024]{1,0:T(8,128)} fusion(bf16[1024,128]{1,0:T(8,128)(2,1)S(1)} %bitcast.54, bf16[512,64]{1,0:T(8,128)(2,1)S(1)} %bitcast.52, bf16[512,64]{1,0:T(8,128)(2,1)S(1)} %bitcast.50), kind=kOutput, calls=%fused_computation.65 | convolution fusion | flops 134479872 | bytes 2490368 | tf_op jit(solution)/shard_map/td,nd->tn/dot_general | solution.py:164
  129.3 1.9 %concatenate.39 = f32[128,4,1024]{2,1,0:T(4,128)S(1)} reshape(f32[512,1024]{1,0:T(8,128)} %fusion.35) | data formatting | bytes 4194304 | tf_op jit(solution)/shard_map/concatenate | solution.py:170
  131.5 1.3 fusion.14
  132.7 1.9 %exponential_reduce_fusion = f32[128,4]{1,0:T(8,128)S(1)} fusion(f32[128,4]{1,0:T(8,128)S(1)} %fusion.14, f32[128,4,128]{2,1,0:T(4,128)S(1)} %bitcast.48, f32[128,4,1024]{2,1,0:T(4,128)S(1)} %concatenate.39, pred[128,1152]{1,0:T(8,128)(4,1)S(1)} %pad_add_fusion), kind=kLoop, calls=%fused_computation.9 | loop fusion | flops 2948608 | bytes 2510848 | tf_op jit(solution)/shard_map/reduce_sum | solution.py:74
  134.8 2.6 %fusion.11 = bf16[512,128]{1,0:T(8,128)(2,1)S(1)} fusion(pred[512,1152]{1,0:T(32,128)(4,1)} %reshape.337, f32[512,128]{1,0:T(8,128)S(1)} %fusion.30, f32[512,1024]{1,0:T(8,128)} %fusion.35, f32[512]{0:T(512)S(1)} %div.89, f32[512]{0:T(512)S(1)} %sub.58, bf16[128,128]{1,0:T(8,128)(2,1)S(1)} %broadcast_select_fusion.1, bf16[1024,128]{1,0:T(8,128)(2,1)} %bitcast.56), kind=kOutput, calls=%fused_computation.17 | convolution fusion | flops 155189248 | bytes 3379200 | tf_op jit(solution)/shard_map/dot_general | solution.py:175
  137.4 0.7 reshape.346
  138.2 0.8 copy.26
  (50 shorter events, 3.8 us)
Async XLA Ops:
  7.2 14.9 %copy-start.2 = (s32[256,16]{0,1:T(8,128)S(1)}, s32[256,16]{0,1:T(8,128)}, u32[]{:S(2)}) copy-start(s32[256,16]{0,1:T(8,128)} %param.15) | copy-start | bytes 49156
  7.2 15.9 %copy-start = (bf16[64,1,2,16,128]{4,3,2,1,0:T(8,128)(2,1)S(1)}, bf16[64,1,2,16,128]{4,3,2,1,0:T(8,128)(2,1)}, u32[]{:S(2)}) copy-start(bf16[64,1,2,16,128]{4,3,2,1,0:T(8,128)(2,1)} %param.14) | copy-start | bytes 1572868
  7.2 109.3 %all-gather.2.cloned.1.call-start = ((), (), s32[]{:S(2)}) async-start(), calls=%async_computation.2 | async-start | bytes 5324800 | tf_op jit(solution)/shard_map/all_gather | solution.py:141
  11.7 25.3 %all-to-all-start = ((bf16[8,128,512]{1,2,0:T(8,128)(2,1)}), bf16[8,128,512]{1,2,0:T(8,128)(2,1)S(1)}, u32[]{:S(2)}, u32[]{:S(2)}) async-start(bf16[8,128,512]{1,2,0:T(8,128)(2,1)} %broadcast_in_dim.34), calls=%async_computation | async-start | bytes 2097152 | tf_op jit(solution)/shard_map/all_to_all | solution.py:22
  22.0 3.0 %copy-start.4 = (s32[4]{0:T(128)S(1)}, s32[4]{0:T(128)}, u32[]{:S(2)}) copy-start(s32[4]{0:T(128)} %param.16) | copy-start | bytes 52
  22.0 6.1 %copy-start.3 = (s32[128]{0:T(128)S(1)}, s32[128]{0:T(128)}, u32[]{:S(2)}) copy-start(s32[128]{0:T(128)} %param.17) | copy-start | bytes 1540
  37.0 39.8 %all-to-all-start.1 = ((bf16[64,2,4096]{2,1,0:T(2,128)(2,1)}), bf16[64,2,4096]{2,1,0:T(2,128)(2,1)S(1)}, u32[]{:S(2)}, u32[]{:S(2)}) async-start(bf16[64,2,4096]{2,1,0:T(2,128)(2,1)} %reshape.341), calls=%async_computation.1 | async-start | bytes 2097152 | tf_op jit(solution)/shard_map/all_to_all | solution.py:112
  77.3 5.9 %copy-start.1 = (f32[4096]{0:T(1024)S(1)}, f32[4096]{0:T(1024)}, u32[]{:S(2)}) copy-start(f32[4096]{0:T(1024)} %param.10) | copy-start | bytes 49156
  78.0 6.7 %collective-permute-start = (bf16[4,1,2,256,128]{4,3,2,1,0:T(8,128)(2,1)S(1)}, bf16[4,1,2,256,128]{4,3,2,1,0:T(8,128)(2,1)S(1)}, u32[]{:S(2)}, u32[]{:S(2)}) collective-permute-start(bf16[4,1,2,256,128]{4,3,2,1,0:T(8,128)(2,1)S(1)} %broadcast_select_fusion), channel_id=1, source_target_pairs={{0,1},{1,0},{2,3},{3,2},{4,5},{5,4},{6,7},{7,6},{8,9},{9,8},{10,11... | collective-permute-start | bytes 1572872 | tf_op jit(solution)/shard_map/ppermute | solution.py:16
  120.5 10.7 %collective-permute-start.1 = (bf16[128,128]{1,0:T(8,128)(2,1)S(1)}, bf16[128,128]{1,0:T(8,128)(2,1)S(1)}, u32[]{:S(2)}, u32[]{:S(2)}) collective-permute-start(bf16[128,128]{1,0:T(8,128)(2,1)S(1)} %fusion.27), channel_id=1, source_target_pairs={{0,1},{1,0},{2,3},{3,2},{4,5},{5,4},{6,7},{7,6},{8,9},{9,8},{10,11... | collective-permute-start | bytes 98312 | tf_op jit(solution)/shard_map/ppermute | solution.py:16
Sparse Core Ops, SparseCore 0:
  11.6 104.8 all-gather.1

commit v10 on v7

--- a/solution.py
+++ b/solution.py
@@ -1,6 +1,7 @@
 import jax
 import jax.numpy as jnp
 from jax import lax
+from jax.experimental import pallas as pl
 from jax.sharding import Mesh, PartitionSpec as P
 
 HEADS = 32
@@ -24,6 +25,28 @@
     shape = list(x.shape)
     shape[dim] *= count
     return ordered.reshape(shape)
+
+
+def project_kernel(rows_ref, weight_ref, out_ref):
+    @pl.when(pl.program_id(0) == 0)
+    def _():
+        out_ref[...] = jnp.zeros_like(out_ref)
+
+    out_ref[...] += jnp.dot(rows_ref[...], weight_ref[...], preferred_element_type=jnp.float32)
+
+
+def project(rows, weight, block=512):
+    steps = weight.shape[0] // block
+    return pl.pallas_call(
+        project_kernel,
+        grid=(steps,),
+        in_specs=[
+            pl.BlockSpec((rows.shape[0], block), lambda k: (0, k)),
+            pl.BlockSpec((block, weight.shape[1]), lambda k: (k, 0)),
+        ],
+        out_specs=pl.BlockSpec((rows.shape[0], weight.shape[1]), lambda k: (0, 0)),
+        out_shape=jax.ShapeDtypeStruct((rows.shape[0], weight.shape[1]), jnp.float32),
+    )(rows, weight)
 
 
 def rotate(vectors, position):
@@ -137,11 +160,7 @@
     )
     q_cols = q_weight.shape[1]
     joined_cols = jnp.concatenate([q_weight, own_kv_cols], axis=1)
-    joined_sum = jnp.dot(
-        normed,
-        lax.all_gather(joined_cols, GROUP, axis=0, tiled=True),
-        preferred_element_type=jnp.float32,
-    )
+    joined_sum = project(normed, lax.all_gather(joined_cols, GROUP, axis=0, tiled=True))
     query_sum = joined_sum[:, :q_cols]
     kv_sum = joined_sum[:, q_cols:]
     position = token_positions(token_request, lengths, requests_here)

time: 139 us -> 145 us (1.043)
  Pallas kernels: 0 us -> 6.87 us
  local copies, waits for them, and re-layouts: 8.57 us -> 12.1 us
  matrix products: 5.65 us -> 2.14 us
  waiting for transfers between devices: 66 us -> 63.1 us
    pallas_call x0 -> x1, Pallas kernels: none -> 6.87 us  [project(): pl.pallas_call(project_kernel, grid=(steps,), in_specs=[pl.BlockSpec((row...]
    dot_general x1 -> x0, matrix products: 3.51 us -> none  [on_device(): jnp.dot(normed, lax.all_gather(joined_cols, GROUP, axis=0, tiled=True), p...]
    all_gather x1, waiting for transfers between devices: 31.6 us -> 29.8 us  [on_device(): lax.all_gather(joined_cols, GROUP, axis=0, tiled=True)]
    all_to_all x1, waiting for transfers between devices: 8.6 us -> 6.78 us  [gather_by_all_to_all(): ordered = lax.all_to_all(spread, axis, 0, 0, tiled=True)]
  transfers between devices with their start and end apart: 5 -> 5, of which waited for: 5 -> 5; matrix products, arithmetic and copies ran while one was open for 10% -> 11% of each run, Pallas kernels for 0% -> 0%
where the time goes in v10:
time: 145 us; the launch traced here: 144 us
  waiting for transfers between devices  63.1 us (44%)
  starting transfers between devices  34.2 us (24%)
  between operations  14.4 us (10%)
  local copies, waits for them, and re-layouts  12.1 us (8%)
  other arithmetic  11.1 us (8%)
  Pallas kernels  6.87 us (5%)
  matrix products  2.14 us (1%)
    all_gather x1, waiting for transfers between devices, on_device(): lax.all_gather(joined_cols, GROUP, axis=0, tiled=True)  29.8 us
    all_to_all x1, waiting for transfers between devices, on_device(): lax.all_to_all(outgoing, GROUP, split_axis=0, concat_axis=0, tiled=True)  25.9 us
    all_to_all x1, starting transfers between devices, on_device(): lax.all_to_all(outgoing, GROUP, split_axis=0, concat_axis=0, tiled=True)  12 us
    ppermute x2, starting transfers between devices, from_partner(): lax.ppermute(x, axis, [(i, i ^ 1 << bit) for i in range(lax.axis_size(axi...  11.7 us
    all_to_all x1, starting transfers between devices, gather_by_all_to_all(): ordered = lax.all_to_all(spread, axis, 0, 0, tiled=True)  10.4 us
    pallas_call x1, Pallas kernels, project(): pl.pallas_call(project_kernel, grid=(steps,), in_specs=[pl.BlockSpec((row...  6.87 us
    all_to_all x1, waiting for transfers between devices, gather_by_all_to_all(): ordered = lax.all_to_all(spread, axis, 0, 0, tiled=True)  6.78 us
  transfers between devices with their start and end apart: 5, of which 5 were waited for; matrix products, arithmetic and copies ran while one was open for 11% of the time, Pallas kernels for 0%

profile of v10, /device:TPU:1, one launch (start us, length us, event | category | flops | bytes accessed | tf_op | source)
XLA Modules:
  0.0 144.0 jit_solution(9433234203117856958)
XLA Ops:
  7.3 0.7 fusion.29
  8.0 1.5 %pad_maximum_fusion = bf16[64,640]{1,0:T(8,128)(2,1)} fusion(bf16[64,128]{1,0:T(8,128)(2,1)S(1)} %fusion.29, bf16[64,512]{1,0:T(8,128)(2,1)} %param.11), kind=kLoop, calls=%fused_computation.42 | loop fusion | flops 163840 | bytes 163840 | tf_op jit(solution)/shard_map/concatenate | solution.py:162
  9.5 2.0 %broadcast_in_dim.32 = bf16[8,128,512]{2,1,0:T(8,128)(2,1)} broadcast(bf16[128,512]{1,0:T(8,128)(2,1)} %param.9), dimensions={1,2} | broadcast | bytes 1179648 | tf_op jit(solution)/shard_map/broadcast_in_dim | solution.py:22
  11.5 10.4 %all-to-all-start = ((bf16[8,128,512]{2,1,0:T(8,128)(2,1)}), bf16[8,128,512]{2,1,0:T(8,128)(2,1)S(1)}, u32[]{:S(2)}, u32[]{:S(2)}) async-start(bf16[8,128,512]{2,1,0:T(8,128)(2,1)} %broadcast_in_dim.32), calls=%async_computation | async-start | bytes 2097152 | tf_op jit(solution)/shard_map/all_to_all | solution.py:23
  22.2 0.7 fusion.42
  22.9 2.5 %compare_select_fusion.1 = s32[1024,1]{0,1:T(1,128)S(1)} fusion(s32[]{:T(128)} %bitcast, s32[]{:T(128)} %bitcast.1, s32[]{:T(128)} %bitcast.3, s32[]{:T(128)} %bitcast.2), kind=kLoop, calls=%fused_computation.67 | loop fusion | flops 17408 | bytes 4112 | tf_op jit(solution)/shard_map/gather | solution.py:84
  26.0 0.5 broadcast_in_dim.31
  26.6 1.3 reshape.324
  28.2 0.4 convolution_convert_fusion
  28.7 1.5 %reshape.328 = bf16[64,2,4096]{2,1,0:T(2,128)(2,1)} reshape(bf16[128,4096]{1,0:T(8,128)(2,1)S(1)} %convolution_convert_fusion) | data formatting | bytes 2097152 | tf_op jit(solution)/shard_map/reshape | solution.py:133
  30.2 6.8 %all-to-all-done = bf16[8,128,512]{2,1,0:T(8,128)(2,1)S(1)} async-done(((bf16[8,128,512]{2,1,0:T(8,128)(2,1)}), bf16[8,128,512]{2,1,0:T(8,128)(2,1)S(1)}, u32[]{:S(2)}, u32[]{:S(2)}) %all-to-all-start) | async-done | bytes 1048608 | tf_op jit(solution)/shard_map/all_to_all | solution.py:23
  37.0 12.0 %all-to-all-start.1 = ((bf16[64,2,4096]{2,1,0:T(2,128)(2,1)}), bf16[64,2,4096]{2,1,0:T(2,128)(2,1)}, u32[]{:S(2)}, u32[]{:S(2)}) async-start(bf16[64,2,4096]{2,1,0:T(2,128)(2,1)} %reshape.328), calls=%async_computation.1 | async-start | bytes 2097152 | tf_op jit(solution)/shard_map/all_to_all | solution.py:135
  49.7 0.3 multiply_cosine_fusion.1
  50.8 25.9 %all-to-all-done.1 = bf16[64,2,4096]{2,1,0:T(2,128)(2,1)} async-done(((bf16[64,2,4096]{2,1,0:T(2,128)(2,1)}), bf16[64,2,4096]{2,1,0:T(2,128)(2,1)}, u32[]{:S(2)}, u32[]{:S(2)}) %all-to-all-start.1) | async-done | bytes 1048608 | tf_op jit(solution)/shard_map/all_to_all | solution.py:135
  76.8 1.5 %reshape.329 = bf16[128,4096]{1,0:T(8,128)(2,1)S(1)} reshape(bf16[64,2,4096]{2,1,0:T(2,128)(2,1)} %all-to-all-done.1) | data formatting | bytes 2097152 | tf_op jit(solution)/shard_map/reshape | solution.py:142
  78.3 0.4 fusion.3
  79.0 5.3 %collective-permute-start = (bf16[4,1,2,256,128]{4,3,2,1,0:T(8,128)(2,1)S(1)}, bf16[4,1,2,256,128]{4,3,2,1,0:T(8,128)(2,1)S(1)}, u32[]{:S(2)}, u32[]{:S(2)}) collective-permute-start(bf16[4,1,2,256,128]{4,3,2,1,0:T(8,128)(2,1)S(1)} %broadcast_select_fusion), channel_id=1, source_target_pairs={{0,1},{1,0},{2,3},{3,2},{4,5},{5,4},{6,7},{7,6},{8,9},{9,8},{10,11... | collective-permute-start | bytes 1572872 | tf_op jit(solution)/shard_map/ppermute | solution.py:17
  84.3 1.3 multiply_convert_fusion.rows_ref
  86.0 0.6 copy-done.1
  86.6 29.8 %all-gather.2.cloned.1.call-done.weight_ref = bf16[4096,640]{1,0:T(8,128)(2,1)} async-done(((bf16[64,640]{1,0:T(8,128)(2,1)}), bf16[4096,640]{1,0:T(8,128)(2,1)}) %all-gather.2.cloned.1.call-update) | async-done | bytes 5242896 | tf_op jit(solution)/shard_map/all_gather | solution.py:163
  116.4 6.9 %shard_map.104 = f32[128,640]{1,0:T(8,128)} custom-call(bf16[128,4096]{1,0:T(8,128)(2,1)} %multiply_convert_fusion.rows_ref, bf16[4096,640]{1,0:T(8,128)(2,1)} %all-gather.2.cloned.1.call-done.weight_ref), custom_call_target="tpu_custom_call" | custom-call | tf_op jit(solution)/shard_map/pallas_call | solution.py:40
  123.2 0.9 slice_bitcast_fusion
  124.1 1.0 slice.37
  125.1 0.3 fusion.21
  125.4 0.9 fusion.24
  126.4 6.5 %collective-permute-start.1 = (bf16[128,128]{1,0:T(8,128)(2,1)S(1)}, bf16[128,128]{1,0:T(8,128)(2,1)S(1)}, u32[]{:S(2)}, u32[]{:S(2)}) collective-permute-start(bf16[128,128]{1,0:T(8,128)(2,1)S(1)} %fusion.24), channel_id=1, source_target_pairs={{0,1},{1,0},{2,3},{3,2},{4,5},{5,4},{6,7},{7,6},{8,9},{9,8},{10,11... | collective-permute-start | bytes 98312 | tf_op jit(solution)/shard_map/ppermute | solution.py:17
  133.2 0.4 collective-permute-done.1
  133.7 0.7 fusion.43
  134.5 0.5 fusion.2
  135.0 0.6 fusion.5
  135.6 0.7 reshape.333
  136.4 0.8 copy.29
  (52 shorter events, 3.9 us)
Async XLA Ops:
  7.2 14.8 %copy-start.5 = (s32[256,16]{0,1:T(8,128)S(1)}, s32[256,16]{0,1:T(8,128)}, u32[]{:S(2)}) copy-start(s32[256,16]{0,1:T(8,128)} %param.15) | copy-start | bytes 49156
  7.2 15.0 %copy-start.7 = (s32[4]{0:T(128)S(1)}, s32[4]{0:T(128)}, u32[]{:S(2)}) copy-start(s32[4]{0:T(128)} %param.16) | copy-start | bytes 52
  7.2 18.5 %copy-start.6 = (s32[128]{0:T(128)S(1)}, s32[128]{0:T(128)}, u32[]{:S(2)}) copy-start(s32[128]{0:T(128)} %param.17) | copy-start | bytes 1540
  7.2 109.2 %all-gather.2.cloned.1.call-start = ((), (), s32[]{:S(2)}) async-start(), calls=%async_computation.2 | async-start | bytes 5324800 | tf_op jit(solution)/shard_map/all_gather | solution.py:163
  11.5 16.7 %copy-start.3 = (bf16[64,1,2,16,128]{4,3,2,1,0:T(8,128)(2,1)S(1)}, bf16[64,1,2,16,128]{4,3,2,1,0:T(8,128)(2,1)}, u32[]{:S(2)}) copy-start(bf16[64,1,2,16,128]{4,3,2,1,0:T(8,128)(2,1)} %param.14) | copy-start | bytes 1572868
  11.5 25.4 %all-to-all-start = ((bf16[8,128,512]{2,1,0:T(8,128)(2,1)}), bf16[8,128,512]{2,1,0:T(8,128)(2,1)S(1)}, u32[]{:S(2)}, u32[]{:S(2)}) async-start(bf16[8,128,512]{2,1,0:T(8,128)(2,1)} %broadcast_in_dim.32), calls=%async_computation | async-start | bytes 2097152 | tf_op jit(solution)/shard_map/all_to_all | solution.py:23
  37.0 39.8 %all-to-all-start.1 = ((bf16[64,2,4096]{2,1,0:T(2,128)(2,1)}), bf16[64,2,4096]{2,1,0:T(2,128)(2,1)}, u32[]{:S(2)}, u32[]{:S(2)}) async-start(bf16[64,2,4096]{2,1,0:T(2,128)(2,1)} %reshape.328), calls=%async_computation.1 | async-start | bytes 2097152 | tf_op jit(solution)/shard_map/all_to_all | solution.py:135
  78.3 6.0 %copy-start.4 = (f32[4096]{0:T(1024)S(1)}, f32[4096]{0:T(1024)}, u32[]{:S(2)}) copy-start(f32[4096]{0:T(1024)} %param.10) | copy-start | bytes 49156
  79.0 6.8 %collective-permute-start = (bf16[4,1,2,256,128]{4,3,2,1,0:T(8,128)(2,1)S(1)}, bf16[4,1,2,256,128]{4,3,2,1,0:T(8,128)(2,1)S(1)}, u32[]{:S(2)}, u32[]{:S(2)}) collective-permute-start(bf16[4,1,2,256,128]{4,3,2,1,0:T(8,128)(2,1)S(1)} %broadcast_select_fusion), channel_id=1, source_target_pairs={{0,1},{1,0},{2,3},{3,2},{4,5},{5,4},{6,7},{7,6},{8,9},{9,8},{10,11... | collective-permute-start | bytes 1572872 | tf_op jit(solution)/shard_map/ppermute | solution.py:17
  85.8 0.8 copy-start.1
  123.2 10.5 %copy-start = (pred[512,1152]{1,0:T(32,128)(4,1)S(1)}, pred[512,1152]{1,0:T(32,128)(4,1)}, u32[]{:S(2)}) copy-start(pred[512,1152]{1,0:T(32,128)(4,1)} %reshape.324) | copy-start | bytes 1769476
  126.4 7.3 %collective-permute-start.1 = (bf16[128,128]{1,0:T(8,128)(2,1)S(1)}, bf16[128,128]{1,0:T(8,128)(2,1)S(1)}, u32[]{:S(2)}, u32[]{:S(2)}) collective-permute-start(bf16[128,128]{1,0:T(8,128)(2,1)S(1)} %fusion.24), channel_id=1, source_target_pairs={{0,1},{1,0},{2,3},{3,2},{4,5},{5,4},{6,7},{7,6},{8,9},{9,8},{10,11... | collective-permute-start | bytes 98312 | tf_op jit(solution)/shard_map/ppermute | solution.py:17
  135.0 1.4 copy-start.2
Sparse Core Ops, SparseCore 0:
  11.6 104.7 all-gather.1

commit v11 on v7

--- a/solution.py
+++ b/solution.py
@@ -123,6 +123,7 @@
         requests_here, pair_count, 2, max_len, head_dim
     )
     alive_mask = jnp.arange(max_len, dtype=jnp.int32)[None, :] < lengths[:, None]
+    raw_decoded = decoded
     decoded = jnp.where(alive_mask[:, None, None, :, None], decoded, jnp.zeros((), jnp.bfloat16))
     whole_rows = gather_by_all_to_all(tokens, "mp", 1)
     normed = normalize(whole_rows, attn_gain)
@@ -155,7 +156,11 @@
     new_values = jnp.where(is_even, other_kv, own_kv)
     allowed = build_mask(token_request, lengths, max_len)
     score_scale = head_dim ** (-0.5)
-    partner_cache = from_partner(decoded, "mp", 0)
+    partner_cache = jnp.where(
+        alive_mask[:, None, None, :, None],
+        from_partner(raw_decoded, "mp", 0),
+        jnp.zeros((), jnp.bfloat16),
+    )
     layer_zero = jnp.where(is_even, decoded, partner_cache)[:, 0]
     all_keys = jnp.concatenate(
         [layer_zero[:, 0].reshape(requests_here * max_len, head_dim), new_keys], axis=0

time: 139 us -> 138 us (level)
  transfers between devices with their start and end apart: 5 -> 5, of which waited for: 5 -> 5; matrix products, arithmetic and copies ran while one was open for 10% -> 11% of each run, Pallas kernels for 0% -> 0%
where the time goes in v11:
time: 138 us; the launch traced here: 137 us
  waiting for transfers between devices  65.5 us (47%)
  starting transfers between devices  33.7 us (24%)
  between operations  14.4 us (10%)
  other arithmetic  10.3 us (7%)
  local copies, waits for them, and re-layouts  7.78 us (6%)
  matrix products  5.65 us (4%)
    all_gather x1, waiting for transfers between devices, on_device(): lax.all_gather(joined_cols, GROUP, axis=0, tiled=True)  31 us
    all_to_all x1, waiting for transfers between devices, on_device(): lax.all_to_all(outgoing, GROUP, split_axis=0, concat_axis=0, tiled=True)  24.6 us
    all_to_all x1, starting transfers between devices, on_device(): lax.all_to_all(outgoing, GROUP, split_axis=0, concat_axis=0, tiled=True)  11.8 us
    ppermute x2, starting transfers between devices, from_partner(): lax.ppermute(x, axis, [(i, i ^ 1 << bit) for i in range(lax.axis_size(axi...  11.6 us
    all_to_all x1, starting transfers between devices, gather_by_all_to_all(): ordered = lax.all_to_all(spread, axis, 0, 0, tiled=True)  10.3 us
    all_to_all x1, waiting for transfers between devices, gather_by_all_to_all(): ordered = lax.all_to_all(spread, axis, 0, 0, tiled=True)  8.6 us
    dot_general x1, matrix products, on_device(): jnp.dot(normed, lax.all_gather(joined_cols, GROUP, axis=0, tiled=True), p...  3.51 us
  transfers between devices with their start and end apart: 5, of which 5 were waited for; matrix products, arithmetic and copies ran while one was open for 11% of the time, Pallas kernels for 0%

profile of v11, /device:TPU:1, one launch (start us, length us, event | category | flops | bytes accessed | tf_op | source)
XLA Modules:
  0.0 137.3 jit_solution(13619119290917167883)
XLA Ops:
  7.3 0.8 fusion.30
  8.1 1.5 %pad_maximum_fusion = bf16[64,640]{1,0:T(8,128)(2,1)} fusion(bf16[64,128]{1,0:T(8,128)(2,1)S(1)} %fusion.30, bf16[64,512]{1,0:T(8,128)(2,1)} %param.11), kind=kLoop, calls=%fused_computation.42 | loop fusion | flops 163840 | bytes 163840 | tf_op jit(solution)/shard_map/concatenate | solution.py:140
  9.6 1.0 copy.15
  10.6 1.1 broadcast_in_dim.36
  11.7 10.3 %all-to-all-start = ((bf16[8,128,512]{1,2,0:T(8,128)(2,1)}), bf16[8,128,512]{1,2,0:T(8,128)(2,1)S(1)}, u32[]{:S(2)}, u32[]{:S(2)}) async-start(bf16[8,128,512]{1,2,0:T(8,128)(2,1)} %broadcast_in_dim.36), calls=%async_computation | async-start | bytes 2097152 | tf_op jit(solution)/shard_map/all_to_all | solution.py:22
  22.3 0.3 select_reduce_fusion
  23.0 0.4 convolution_convert_fusion
  23.5 1.5 %reshape.328 = bf16[64,2,4096]{2,1,0:T(2,128)(2,1)} reshape(bf16[128,4096]{1,0:T(8,128)(2,1)S(1)} %convolution_convert_fusion) | data formatting | bytes 2097152 | tf_op jit(solution)/shard_map/reshape | solution.py:110
  25.0 0.6 fusion.43
  25.6 2.5 %compare_select_fusion.1 = s32[1024,1]{0,1:T(1,128)S(1)} fusion(s32[]{:T(128)} %bitcast, s32[]{:T(128)} %bitcast.1, s32[]{:T(128)} %bitcast.3, s32[]{:T(128)} %bitcast.2), kind=kLoop, calls=%fused_computation.67 | loop fusion | flops 17408 | bytes 4112 | tf_op jit(solution)/shard_map/gather | solution.py:61
  28.4 8.6 %all-to-all-done = bf16[8,128,512]{1,2,0:T(8,128)(2,1)S(1)} async-done(((bf16[8,128,512]{1,2,0:T(8,128)(2,1)}), bf16[8,128,512]{1,2,0:T(8,128)(2,1)S(1)}, u32[]{:S(2)}, u32[]{:S(2)}) %all-to-all-start) | async-done | bytes 1048608 | tf_op jit(solution)/shard_map/all_to_all | solution.py:22
  37.0 11.8 %all-to-all-start.1 = ((bf16[64,2,4096]{2,1,0:T(2,128)(2,1)}), bf16[64,2,4096]{2,1,0:T(2,128)(2,1)S(1)}, u32[]{:S(2)}, u32[]{:S(2)}) async-start(bf16[64,2,4096]{2,1,0:T(2,128)(2,1)} %reshape.328), calls=%async_computation.1 | async-start | bytes 2097152 | tf_op jit(solution)/shard_map/all_to_all | solution.py:112
  48.8 0.5 broadcast_in_dim.35
  49.4 1.3 reshape.324
  51.4 0.3 multiply_cosine_fusion.1
  51.7 0.6 multiply_reduce_fusion
  52.3 24.6 %all-to-all-done.1 = bf16[64,2,4096]{2,1,0:T(2,128)(2,1)S(1)} async-done(((bf16[64,2,4096]{2,1,0:T(2,128)(2,1)}), bf16[64,2,4096]{2,1,0:T(2,128)(2,1)S(1)}, u32[]{:S(2)}, u32[]{:S(2)}) %all-to-all-start.1) | async-done | bytes 1048608 | tf_op jit(solution)/shard_map/all_to_all | solution.py:112
  76.8 0.4 reshape.329
  77.3 0.4 fusion.4
  77.8 5.1 %collective-permute-start = (bf16[4,1,2,256,128]{4,3,2,1,0:T(8,128)(2,1)S(1)}, bf16[4,1,2,256,128]{4,3,2,1,0:T(8,128)(2,1)S(1)}, u32[]{:S(2)}, u32[]{:S(2)}) collective-permute-start(bf16[4,1,2,256,128]{4,3,2,1,0:T(8,128)(2,1)S(1)} %bitcast.44), channel_id=1, source_target_pairs={{0,1},{1,0},{2,3},{3,2},{4,5},{5,4},{6,7},{7,6},{8,9},{9,8},{10,11... | collective-permute-start | bytes 1572872 | tf_op jit(solution)/shard_map/ppermute | solution.py:16
  82.9 0.7 fusion.2
  83.6 0.8 collective-permute-done
  84.4 1.0 select_bitcast_fusion
  85.5 31.0 %all-gather.2.cloned.1.call-done = bf16[4096,640]{1,0:T(8,128)(2,1)} async-done(((bf16[64,640]{1,0:T(8,128)(2,1)}), bf16[4096,640]{1,0:T(8,128)(2,1)}) %all-gather.2.cloned.1.call-update) | async-done | bytes 5242896 | tf_op jit(solution)/shard_map/all_gather | solution.py:143
  116.5 3.5 %fusion.45 = f32[128,640]{1,0:T(8,128)S(1)} fusion(bf16[128,4096]{0,1:T(8,128)(2,1)S(1)} %fusion.2, bf16[4096,640]{1,0:T(8,128)(2,1)} %all-gather.2.cloned.1.call-done), kind=kOutput, calls=%fused_computation.106 | convolution fusion | flops 671088640 | bytes 6619136 | tf_op jit(solution)/shard_map/dot_general | solution.py:141
  120.1 0.3 fusion.22
  120.5 6.5 %collective-permute-start.1 = (bf16[128,128]{1,0:T(8,128)(2,1)S(1)}, bf16[128,128]{1,0:T(8,128)(2,1)S(1)}, u32[]{:S(2)}, u32[]{:S(2)}) collective-permute-start(bf16[128,128]{1,0:T(8,128)(2,1)S(1)} %fusion.25), channel_id=1, source_target_pairs={{0,1},{1,0},{2,3},{3,2},{4,5},{5,4},{6,7},{7,6},{8,9},{9,8},{10,11... | collective-permute-start | bytes 98312 | tf_op jit(solution)/shard_map/ppermute | solution.py:16
  127.3 0.4 collective-permute-done.1
  127.8 0.8 fusion.44
  128.6 0.5 fusion.3
  129.1 0.6 fusion.6
  129.7 0.7 reshape.333
  (45 shorter events, 2.4 us)
Async XLA Ops:
  7.2 14.9 %copy-start.3 = (s32[256,16]{0,1:T(8,128)S(1)}, s32[256,16]{0,1:T(8,128)}, u32[]{:S(2)}) copy-start(s32[256,16]{0,1:T(8,128)} %param.15) | copy-start | bytes 49156
  7.2 15.9 %copy-start.1 = (bf16[64,1,2,16,128]{4,3,2,1,0:T(8,128)(2,1)S(1)}, bf16[64,1,2,16,128]{4,3,2,1,0:T(8,128)(2,1)}, u32[]{:S(2)}) copy-start(bf16[64,1,2,16,128]{4,3,2,1,0:T(8,128)(2,1)} %param.14) | copy-start | bytes 1572868
  7.2 109.3 %all-gather.2.cloned.1.call-start = ((), (), s32[]{:S(2)}) async-start(), calls=%async_computation.2 | async-start | bytes 5324800 | tf_op jit(solution)/shard_map/all_gather | solution.py:143
  11.7 25.3 %all-to-all-start = ((bf16[8,128,512]{1,2,0:T(8,128)(2,1)}), bf16[8,128,512]{1,2,0:T(8,128)(2,1)S(1)}, u32[]{:S(2)}, u32[]{:S(2)}) async-start(bf16[8,128,512]{1,2,0:T(8,128)(2,1)} %broadcast_in_dim.36), calls=%async_computation | async-start | bytes 2097152 | tf_op jit(solution)/shard_map/all_to_all | solution.py:22
  22.0 3.0 %copy-start.5 = (s32[4]{0:T(128)S(1)}, s32[4]{0:T(128)}, u32[]{:S(2)}) copy-start(s32[4]{0:T(128)} %param.16) | copy-start | bytes 52
  22.0 6.1 %copy-start.4 = (s32[128]{0:T(128)S(1)}, s32[128]{0:T(128)}, u32[]{:S(2)}) copy-start(s32[128]{0:T(128)} %param.17) | copy-start | bytes 1540
  37.0 39.8 %all-to-all-start.1 = ((bf16[64,2,4096]{2,1,0:T(2,128)(2,1)}), bf16[64,2,4096]{2,1,0:T(2,128)(2,1)S(1)}, u32[]{:S(2)}, u32[]{:S(2)}) async-start(bf16[64,2,4096]{2,1,0:T(2,128)(2,1)} %reshape.328), calls=%async_computation.1 | async-start | bytes 2097152 | tf_op jit(solution)/shard_map/all_to_all | solution.py:112
  77.3 5.6 %copy-start.2 = (f32[4096]{0:T(1024)S(1)}, f32[4096]{0:T(1024)}, u32[]{:S(2)}) copy-start(f32[4096]{0:T(1024)} %param.10) | copy-start | bytes 49156
  77.8 6.6 %collective-permute-start = (bf16[4,1,2,256,128]{4,3,2,1,0:T(8,128)(2,1)S(1)}, bf16[4,1,2,256,128]{4,3,2,1,0:T(8,128)(2,1)S(1)}, u32[]{:S(2)}, u32[]{:S(2)}) collective-permute-start(bf16[4,1,2,256,128]{4,3,2,1,0:T(8,128)(2,1)S(1)} %bitcast.44), channel_id=1, source_target_pairs={{0,1},{1,0},{2,3},{3,2},{4,5},{5,4},{6,7},{7,6},{8,9},{9,8},{10,11... | collective-permute-start | bytes 1572872 | tf_op jit(solution)/shard_map/ppermute | solution.py:16
  120.0 7.8 %copy-start = (pred[512,1152]{1,0:T(32,128)(4,1)S(1)}, pred[512,1152]{1,0:T(32,128)(4,1)}, u32[]{:S(2)}) copy-start(pred[512,1152]{1,0:T(32,128)(4,1)} %reshape.324) | copy-start | bytes 1769476
  120.5 7.3 %collective-permute-start.1 = (bf16[128,128]{1,0:T(8,128)(2,1)S(1)}, bf16[128,128]{1,0:T(8,128)(2,1)S(1)}, u32[]{:S(2)}, u32[]{:S(2)}) collective-permute-start(bf16[128,128]{1,0:T(8,128)(2,1)S(1)} %fusion.25), channel_id=1, source_target_pairs={{0,1},{1,0},{2,3},{3,2},{4,5},{5,4},{6,7},{7,6},{8,9},{9,8},{10,11... | collective-permute-start | bytes 98312 | tf_op jit(solution)/shard_map/ppermute | solution.py:16
Sparse Core Ops, SparseCore 0:
  11.6 104.8 all-gather.1
